TPU v7x, 256 devices: a whole 4x4x8 slice. The times are simulated.
256 devices in a mesh: row: 16 (over x, z_hi, core), col: 4 (over y), rep: 4 (over z_lo).
Axes of the slice: x: 4, y: 4, z: 8 (z_hi: 2, z_lo: 4; z = z_hi * 4 + z_lo), core: 2. Of those that a mesh axis runs over, the one named last changes fastest.
Arguments:
- integrals: bfloat16 [8, 32, 60, 128, 128], P(None, 'row', 'rep', 'col'), may hold values from -0.0625 to 0.0625
- amplitudes: bfloat16 [8, 16, 60, 128, 128], P(None, 'col', 'rep', 'row'), may hold values from -6 to 6
- virt_count: int32 [8], replicated, may hold values from 76 to 128, as said below
- occ_irrep: int32 [60], replicated, may hold values from 0 to 7
Outputs:
- cycle: bfloat16 [8, 32, 128, 16, 128], P('rep', 'row', None, 'col')
Inputs may be any that keep to these rules, and one draw needn't show every extreme that they name: `virt_count`: one irrep has exactly 128 virtual orbitals.
All inputs are finite; a program needn't handle non-finite values.
Results may differ from a plain program's by a relative error of at most 0.001.
Values may be sent and summed in bfloat16 or wider, within the bound.
No kernel may reach another device: no remote copies, remote signals or barrier semaphores. Data moves between devices by JAX's collectives and lax.ppermute only.
A program may use at most 128 MiB of HBM per device.

v0:
```python
import jax
import jax.numpy as jnp
from jax import lax
from jax.sharding import PartitionSpec as P


def contract(w_part, t_part):
    w_full = lax.all_gather(w_part, "col", axis=3, tiled=True)
    return jnp.einsum(
        "gikca,gjkcb->giajb",
        w_full,
        lax.all_gather(t_part, "row", axis=3, tiled=True),
        preferred_element_type=jnp.float32,
    )


def body(integrals, amplitudes, virt_count, occ_irrep):
    ngroup = integrals.shape[0]
    k_local = integrals.shape[2]
    c_local = integrals.shape[3]
    nvirt = integrals.shape[4]
    rep_index = lax.axis_index("rep")
    col_index = lax.axis_index("col")
    occ_local = lax.dynamic_slice_in_dim(occ_irrep, rep_index * k_local, k_local)
    groups = jnp.arange(ngroup, dtype=jnp.int32)
    blocks = jnp.bitwise_xor(groups[:, None], occ_local[None, :])
    onehot = blocks[:, :, None] == groups[None, None, :]
    limit = jnp.sum(jnp.where(onehot, virt_count[None, None, :], 0), axis=2)
    c_global = col_index * c_local + jnp.arange(c_local, dtype=jnp.int32)
    c_live = c_global[None, None, :] < limit[:, :, None]
    places = jnp.arange(nvirt, dtype=jnp.int32)
    a_live = places[None, :] < virt_count[:, None]
    keep = c_live[:, None, :, :, None] & a_live[:, None, None, None, :]
    masked = jnp.where(keep, integrals, jnp.zeros_like(integrals))
    owned = ngroup // lax.axis_size("rep")
    partial_cycle = contract(masked, amplitudes)
    summed = lax.psum_scatter(partial_cycle, "rep", scatter_dimension=0, tiled=True)
    own_counts = lax.dynamic_slice_in_dim(virt_count, rep_index * owned, owned)
    b_live = places[None, :] < own_counts[:, None]
    result = jnp.where(b_live[:, None, None, None, :], summed, jnp.zeros_like(summed))
    return result.astype(jnp.bfloat16)


def solution(mesh):
    return jax.shard_map(
        body,
        mesh=mesh,
        in_specs=(P(None, "row", "rep", "col", None), P(None, "col", "rep", "row", None), P(), P()),
        out_specs=P("rep", "row", None, "col", None),
        check_vma=False,
    )
```

profile of v0, /device:TPU:1, one launch (start us, length us, event | category | flops | bytes accessed | tf_op | source)
XLA Modules:
  0.0 377.3 jit_solution(17503319874373990578)
XLA Ops:
  6.5 0.0 all-gather.3.cloned.1.call-start
  6.5 0.7 iota_compare_fusion.1
  7.3 0.7 dynamic_slice.7
  8.0 0.7 select_reduce_fusion
  8.7 0.1 broadcast_compare_fusion
  8.8 0.8 broadcast_and_fusion
  9.6 3.1 broadcast_select_fusion
  12.7 0.0 all-gather.3.cloned.1.call-update
  12.8 0.0 all-gather.5.cloned.1.call-start
  12.8 0.7 all-gather.5.cloned.1.call-update
  13.5 0.0 copy-start
  13.5 0.0 reduce-scatter.2.cloned.1.call-start
  13.6 84.3 %all-gather.3.cloned.1.call-done = bf16[8,2,15,128,128]{4,3,2,1,0:T(8,128)(2,1)} async-done(((bf16[8,2,15,32,128]{4,3,2,1,0:T(8,128)(2,1)}), bf16[8,2,15,128,128]{4,3,2,1,0:T(8,128)(2,1)}) %all-gather.3.cloned.1.call-update) | async-done | bytes 7864336 | tf_op jit(solution)/shard_map/all_gather | solution.py:8
  97.8 179.9 %all-gather.5.cloned.1.call-done = bf16[8,4,15,128,128]{4,3,2,1,0:T(8,128)(2,1)} async-done(((bf16[8,4,15,8,128]{4,3,2,1,0:T(8,128)(2,1)}), bf16[8,4,15,128,128]{4,3,2,1,0:T(8,128)(2,1)}) %all-gather.5.cloned.1.call-update) | async-done | bytes 15728656 | tf_op jit(solution)/shard_map/all_gather | solution.py:12
  277.7 14.3 %fusion.3 = f32[8,2,128,4,128]{4,2,3,1,0:T(8,128)} fusion(bf16[8,4,15,128,128]{4,3,2,1,0:T(8,128)(2,1)} %all-gather.5.cloned.1.call-done, bf16[8,2,15,128,128]{4,3,2,1,0:T(8,128)(2,1)} %all-gather.3.cloned.1.call-done), kind=kOutput, calls=%fused_computation.3 | convolution fusion | flops 4026531840 | bytes 27787264 | tf_op jit(solution)/shard_map/gikca,gjkcb->giajb/dot_general | solution.py:9
  292.0 0.0 reduce-scatter.2.cloned.1.call-update
  292.1 0.0 copy-done
  292.1 0.1 dynamic_slice.6
  292.2 0.1 iota_compare_fusion.2
  292.2 76.0 %reduce-scatter.2.cloned.1.call-done = f32[2,2,128,4,128]{4,2,3,1,0:T(8,128)} async-done(((f32[8,2,128,4,128]{4,2,3,1,0:T(8,128)}), f32[2,2,128,4,128]{4,2,3,1,0:T(8,128)}) %reduce-scatter.2.cloned.1.call-update) | async-done | bytes 1048592 | tf_op jit(solution)/shard_map/reduce_scatter | solution.py:37
  368.2 1.3 select_convert_fusion
  369.6 1.2 copy.6
  (2 shorter events, 0.0 us)
Async XLA Ops:
  6.5 91.3 %all-gather.3.cloned.1.call-start = ((), (), s32[]{:S(2)}) async-start(), calls=%async_computation.1 | async-start | bytes 9830400 | tf_op jit(solution)/shard_map/all_gather | solution.py:8
  12.8 265.0 %all-gather.5.cloned.1.call-start = ((), (), s32[]{:S(2)}) async-start(), calls=%async_computation.2 | async-start | bytes 16711680 | tf_op jit(solution)/shard_map/all_gather | solution.py:12
  13.5 278.6 %copy-start = (s32[8]{0:T(128)S(1)}, s32[8]{0:T(128)}, u32[]{:S(2)}) copy-start(s32[8]{0:T(128)} %param.6) | copy-start | bytes 100
  13.5 354.7 %reduce-scatter.2.cloned.1.call-start = ((), (), s32[]{:S(2)}) async-start(), calls=%async_computation.3 | async-start | bytes 5242880 | tf_op jit(solution)/shard_map/reduce_scatter | solution.py:37
Sparse Core Ops, SparseCore 0:
  12.9 84.8 all-gather.2
  100.4 177.3 all-gather.4
  292.2 75.9 reduce-scatter.1
where the time goes:
time: 377 us
  waiting for transfers between devices  341 us (90%)
  matrix products  14.3 us (4%)
  between operations  13.2 us (4%)
  other arithmetic  6.86 us (2%)
    all_gather x1, waiting for transfers between devices, contract(): lax.all_gather(t_part, 'row', axis=3, tiled=True)  180 us
    all_gather x1, waiting for transfers between devices, contract(): w_full = lax.all_gather(w_part, 'col', axis=3, tiled=True)  84.3 us
    reduce_scatter x1, waiting for transfers between devices, body(): lax.psum_scatter(partial_cycle, 'rep', scatter_dimension=0, tiled=True)  76 us
    dot_general x1, matrix products, contract(): jnp.einsum('gikca,gjkcb->giajb', w_full, lax.all_gather(t_part, 'row', ax...  14.3 us
  transfers between devices with their start and end apart: 3, of which 3 were waited for; matrix products, arithmetic and copies ran while one was open for 0% of the time, Pallas kernels for 0%

commit v1 on v0

--- a/solution.py
+++ b/solution.py
@@ -4,14 +4,53 @@
 from jax.sharding import PartitionSpec as P
 
 
-def contract(w_part, t_part):
-    w_full = lax.all_gather(w_part, "col", axis=3, tiled=True)
-    return jnp.einsum(
-        "gikca,gjkcb->giajb",
-        w_full,
-        lax.all_gather(t_part, "row", axis=3, tiled=True),
-        preferred_element_type=jnp.float32,
+def shift_perm(n, step, period=1):
+    pairs = []
+    for i in range(n):
+        ring = n // period if period == 1 else 4
+        pos = (i // period) % ring
+        dest = i + ((pos + step) % ring - pos) * period
+        pairs.append((i, dest))
+    return pairs
+
+
+def ring4_gather(block, axis, n, period, pos, split_axis):
+    fwd = shift_perm(n, 1, period)
+    bwd = shift_perm(n, -1, period)
+    from_left = lax.ppermute(block, axis, fwd)
+    from_right = lax.ppermute(block, axis, bwd)
+    half = block.shape[split_axis] // 2
+    lo = lax.slice_in_dim(from_left, 0, half, axis=split_axis)
+    hi = lax.slice_in_dim(from_right, half, block.shape[split_axis], axis=split_axis)
+    opp = jnp.concatenate(
+        [lax.ppermute(lo, axis, fwd), lax.ppermute(hi, axis, bwd)], axis=split_axis
     )
+    ring = jnp.stack([block, from_left, opp, from_right])
+    return [lax.dynamic_index_in_dim(ring, (pos - q) % 4, 0, keepdims=False) for q in range(4)]
+
+
+def gather_amplitudes(t_part):
+    nrow = lax.axis_size("row")
+    r = lax.axis_index("row")
+    x = r // 4
+    zh = (r // 2) % 2
+    core = r % 2
+    t_zh = lax.ppermute(t_part, "row", [(i, i ^ 2) for i in range(nrow)])
+    pair = jnp.where(zh == 0, jnp.stack([t_part, t_zh]), jnp.stack([t_zh, t_part]))
+    blocks = ring4_gather(pair, "row", nrow, 4, x, 1)
+    mine = jnp.stack(blocks)
+    other = lax.ppermute(mine, "row", [(i, i ^ 1) for i in range(nrow)])
+    both = jnp.where(core == 0, jnp.stack([mine, other]), jnp.stack([other, mine]))
+    ng, nj, nk, ncc, nb = t_part.shape
+    full = jnp.transpose(both, (3, 4, 5, 1, 2, 0, 6, 7))
+    return full.reshape(ng, nj, nk, 16 * ncc, nb)
+
+
+def gather_integrals(w_part):
+    ncol = lax.axis_size("col")
+    cl = lax.axis_index("col")
+    blocks = ring4_gather(w_part, "col", ncol, 1, cl, 0)
+    return jnp.concatenate(blocks, axis=3)
 
 
 def body(integrals, amplitudes, virt_count, occ_irrep):
@@ -33,7 +72,11 @@
     keep = c_live[:, None, :, :, None] & a_live[:, None, None, None, :]
     masked = jnp.where(keep, integrals, jnp.zeros_like(integrals))
     owned = ngroup // lax.axis_size("rep")
-    partial_cycle = contract(masked, amplitudes)
+    w_full = gather_integrals(masked)
+    t_full = gather_amplitudes(amplitudes)
+    partial_cycle = jnp.einsum(
+        "gikca,gjkcb->giajb", w_full, t_full, preferred_element_type=jnp.float32
+    )
     summed = lax.psum_scatter(partial_cycle, "rep", scatter_dimension=0, tiled=True)
     own_counts = lax.dynamic_slice_in_dim(virt_count, rep_index * owned, owned)
     b_live = places[None, :] < own_counts[:, None]

time: 377 us -> 392 us (1.040)
  waiting for transfers between devices: 341 us -> 249 us
  local copies, waits for them, and re-layouts: 2.01 us -> 44.6 us
  other arithmetic: 6.86 us -> 38.3 us
  starting transfers between devices: 0.08 us -> 24.3 us
  matrix products: 14.3 us -> 21.7 us
    all_gather x2 -> x0, waiting for transfers between devices: 264 us -> none  [the longest x1 180 us: contract(): lax.all_gather(t_part, 'row', axis=3, tiled=True)]
    ppermute x0 -> x10, waiting for transfers between devices: none -> 147 us  [the longest x2 83 us: ring4_gather(): from_left = lax.ppermute(block, axis, fwd)]
    dynamic_slice x0 -> x6, local copies, waits for them, and re-layouts: none -> 35 us  [ring4_gather(): lax.dynamic_index_in_dim(ring, (pos - q) % 4, 0, keepdims=False)]
    reduce_scatter x1, waiting for transfers between devices: 76 us -> 102 us  [body(): lax.psum_scatter(partial_cycle, 'rep', scatter_dimension=0, tiled=True)]
    ppermute x0 -> x10, starting transfers between devices: none -> 24.3 us  [the longest x1 7.73 us: gather_amplitudes(): t_zh = lax.ppermute(t_part, 'row', [(i, i ^ 2) for i in range(nrow)])]
    select_n x0 -> x2, other arithmetic: none -> 21.5 us  [the longest x1 19.3 us: gather_amplitudes(): jnp.where(core == 0, jnp.stack([mine, other]), jnp.stack([other, mine]))]
    another operation x0 -> x6, other arithmetic: none -> 14.2 us  [the longest x5 8.37 us: ring4_gather(): ring = jnp.stack([block, from_left, opp, from_right])]
    dot_general x1, matrix products: 14.3 us -> 21.7 us  [body(): jnp.einsum('gikca,gjkcb->giajb', w_full, t_full, preferred_element_type=j...]
  transfers between devices with their start and end apart: 3 -> 11, of which waited for: 3 -> 8; matrix products, arithmetic and copies ran while one was open for 0% -> 10% of each run, Pallas kernels for 0% -> 0%
where the time goes in v1:
time: 392 us; the launch traced here: 391 us
  waiting for transfers between devices  249 us (64%)
  local copies, waits for them, and re-layouts  44.6 us (11%)
  other arithmetic  38.3 us (10%)
  starting transfers between devices  24.3 us (6%)
  matrix products  21.7 us (6%)
  between operations  13.6 us (3%)
    reduce_scatter x1, waiting for transfers between devices, body(): lax.psum_scatter(partial_cycle, 'rep', scatter_dimension=0, tiled=True)  102 us
    ppermute x2, waiting for transfers between devices, ring4_gather(): from_left = lax.ppermute(block, axis, fwd)  83 us
    dynamic_slice x6, local copies, waits for them, and re-layouts, ring4_gather(): lax.dynamic_index_in_dim(ring, (pos - q) % 4, 0, keepdims=False)  35 us
    ppermute x2, waiting for transfers between devices, ring4_gather(): lax.ppermute(lo, axis, fwd)  34.8 us
    ppermute x1, waiting for transfers between devices, gather_amplitudes(): t_zh = lax.ppermute(t_part, 'row', [(i, i ^ 2) for i in range(nrow)])  26 us
    dot_general x1, matrix products, body(): jnp.einsum('gikca,gjkcb->giajb', w_full, t_full, preferred_element_type=j...  21.7 us
    select_n x1, other arithmetic, gather_amplitudes(): jnp.where(core == 0, jnp.stack([mine, other]), jnp.stack([other, mine]))  19.3 us
    another operation x5, other arithmetic, ring4_gather(): ring = jnp.stack([block, from_left, opp, from_right])  8.37 us
  transfers between devices with their start and end apart: 11, of which 8 were waited for; matrix products, arithmetic and copies ran while one was open for 10% of the time, Pallas kernels for 0%

profile of v1, /device:TPU:1, one launch (start us, length us, event | category | flops | bytes accessed | tf_op | source)
XLA Modules:
  0.0 391.1 jit_solution(17933462148280538527)
XLA Ops:
  6.5 7.7 %collective-permute-start.4 = (bf16[8,4,15,8,128]{4,3,2,1,0:T(8,128)(2,1)}, bf16[8,4,15,8,128]{4,3,2,1,0:T(8,128)(2,1)S(1)}, u32[]{:S(2)}, u32[]{:S(2)}) collective-permute-start(bf16[8,4,15,8,128]{4,3,2,1,0:T(8,128)(2,1)} %param.5), channel_id=1, source_target_pairs={{0,32},{16,48},{32,0},{48,16},{64,96},{80,112},{96,64},{112,80},{1... | collective-permute-start | bytes 2949128 | tf_op jit(solution)/shard_map/ppermute | solution.py:38
  14.3 26.0 %collective-permute-done.4 = bf16[8,4,15,8,128]{4,3,2,1,0:T(8,128)(2,1)S(1)} collective-permute-done((bf16[8,4,15,8,128]{4,3,2,1,0:T(8,128)(2,1)}, bf16[8,4,15,8,128]{4,3,2,1,0:T(8,128)(2,1)S(1)}, u32[]{:S(2)}, u32[]{:S(2)}) %collective-permute-start.4) | collective-permute-done | bytes 983072 | tf_op jit(solution)/shard_map/ppermute | solution.py:38
  40.3 1.0 copy-done.7
  41.2 2.2 maximum_select_fusion.2
  43.4 1.7 collective-permute-start.5
  45.1 1.4 collective-permute-start.7
  46.4 39.9 %collective-permute-done.5 = bf16[2,8,4,15,8,128]{5,4,0,3,2,1:T(8,128)(2,1)S(1)} collective-permute-done((bf16[2,8,4,15,8,128]{5,4,0,3,2,1:T(8,128)(2,1)S(1)}, bf16[2,8,4,15,8,128]{5,4,0,3,2,1:T(8,128)(2,1)S(1)}, u32[]{:S(2)}, u32[]{:S(2)}) %collective-permute-start.5) | collective-permute-done | bytes 1966112 | tf_op jit(solution)/shard_map/ppermute | solution.py:20
  86.3 1.1 slice.18
  87.4 0.4 collective-permute-start.6
  87.8 0.0 collective-permute-done.7
  87.8 1.3 copy-done.1
  89.1 1.1 slice.19
  90.3 2.3 collective-permute-start.8
  92.5 15.9 %collective-permute-done.6 = bf16[2,4,4,15,8,128]{5,4,0,3,2,1:T(8,128)(2,1)} collective-permute-done((bf16[2,4,4,15,8,128]{5,4,0,3,2,1:T(8,128)(2,1)}, bf16[2,4,4,15,8,128]{5,4,0,3,2,1:T(8,128)(2,1)}, u32[]{:S(2)}, u32[]{:S(2)}) %collective-permute-start.6) | collective-permute-done | bytes 983072 | tf_op jit(solution)/shard_map/ppermute | solution.py:26
  108.5 1.5 collective-permute-done.8
  110.0 1.7 maximum_bitcast_fusion.5
  111.7 0.0 copy-done.6
  111.7 3.8 pad_maximum_fusion.1
  115.5 2.1 constant_dynamic-slice_fusion.2
  117.6 0.0 copy-start.9
  117.6 0.0 copy-start.8
  117.6 0.0 copy-start
  117.6 5.9 %fusion.9 = (bf16[1,4,2,8,4,15,8,128]{7,6,0,2,1,5,4,3:T(8,128)(2,1)}, bf16[4,2,8,4,15,8,128]{6,5,1,0,4,3,2:T(8,128)(2,1)}) fusion(bf16[1,2,8,4,15,8,128]{6,5,1,0,4,3,2:T(8,128)(2,1)S(1)} %get-tuple-element.12, bf16[1,2,8,4,15,8,128]{6,5,1,0,4,3,2:T(8,128)(2,1)S(1)} %get-tuple-element.13, bf16[1,2,8,4,15,8,128]{6,5,1,0,4,3,2:T(8,128)(2,1)S(1)} %get-tuple-element.14, ...), kind=kLoop, calls=%fused_computation.36 | loop fusion | flops 11796480 | bytes 23592960 | tf_op jit(solution)/shard_map/stack | solution.py:43
  123.4 4.8 %collective-permute-start.9 = (bf16[4,2,8,4,15,8,128]{6,5,1,0,4,3,2:T(8,128)(2,1)}, bf16[4,2,8,4,15,8,128]{6,5,1,0,4,3,2:T(8,128)(2,1)}, u32[]{:S(2)}, u32[]{:S(2)}) collective-permute-start(bf16[4,2,8,4,15,8,128]{6,5,1,0,4,3,2:T(8,128)(2,1)} %get-tuple-element.10), channel_id=1, source_target_pairs={{0,16},{16,0},{32,48},{48,32},{64,80},{80,64},{96,112},{112,96},{1... | collective-permute-start | bytes 23592968 | tf_op jit(solution)/shard_map/ppermute | solution.py:42
  128.3 0.0 copy-done.9
  128.3 0.1 dynamic_slice.33
  128.4 0.0 copy-done.8
  128.4 0.1 select_reduce_fusion
  128.5 0.1 iota_compare_fusion.1
  128.5 0.1 broadcast_compare_fusion
  128.6 0.8 broadcast_and_fusion
  129.4 0.0 copy-done
  129.4 0.2 broadcast_select_fusion
  129.6 1.8 collective-permute-start
  131.4 1.5 collective-permute-start.2
  132.9 43.1 %collective-permute-done = bf16[8,2,15,32,128]{4,3,2,1,0:T(8,128)(2,1)S(1)} collective-permute-done((bf16[8,2,15,32,128]{4,3,2,1,0:T(8,128)(2,1)S(1)}, bf16[8,2,15,32,128]{4,3,2,1,0:T(8,128)(2,1)S(1)}, u32[]{:S(2)}, u32[]{:S(2)}) %collective-permute-start) | collective-permute-done | bytes 1966112 | tf_op jit(solution)/shard_map/ppermute | solution.py:20
  176.0 1.3 copy-done.2
  177.3 0.1 slice.16
  177.4 0.1 collective-permute-start.1
  177.5 0.0 collective-permute-done.2
  177.5 1.3 copy-done.4
  178.8 1.0 slice.17
  179.8 2.7 collective-permute-start.3
  182.5 0.2 fusion.11
  182.7 18.9 %collective-permute-done.1 = bf16[4,2,15,32,128]{4,3,2,1,0:T(8,128)(2,1)} collective-permute-done((bf16[4,2,15,32,128]{4,3,2,1,0:T(8,128)(2,1)S(1)}, bf16[4,2,15,32,128]{4,3,2,1,0:T(8,128)(2,1)}, u32[]{:S(2)}, u32[]{:S(2)}) %collective-permute-start.1) | collective-permute-done | bytes 983072 | tf_op jit(solution)/shard_map/ppermute | solution.py:26
  201.5 1.5 collective-permute-done.3
  203.0 1.7 maximum_bitcast_fusion.4
  204.7 0.0 copy-done.3
  204.7 0.0 copy-done.5
  204.7 1.1 pad_maximum_fusion
  205.8 3.5 constant_dynamic-slice_fusion.6
  209.3 7.9 %copy.18 = bf16[1,8,2,15,32,128]{4,5,3,2,1,0:T(8,128)(2,1)} copy(bf16[1,8,2,15,32,128]{5,4,3,2,1,0:T(8,128)(2,1)} %get-tuple-element.5) | data formatting | bytes 3932160 | tf_op jit(solution)/shard_map/jit(dynamic_index_in_dim)/dynamic_slice | solution.py:29
  217.2 7.9 %copy.19 = bf16[1,8,2,15,32,128]{4,5,3,2,1,0:T(8,128)(2,1)} copy(bf16[1,8,2,15,32,128]{5,4,3,2,1,0:T(8,128)(2,1)} %get-tuple-element.8) | data formatting | bytes 3932160 | tf_op jit(solution)/shard_map/jit(dynamic_index_in_dim)/dynamic_slice | solution.py:29
  225.1 7.9 %copy.20 = bf16[1,8,2,15,32,128]{4,5,3,2,1,0:T(8,128)(2,1)} copy(bf16[1,8,2,15,32,128]{5,4,3,2,1,0:T(8,128)(2,1)} %get-tuple-element.7) | data formatting | bytes 3932160 | tf_op jit(solution)/shard_map/jit(dynamic_index_in_dim)/dynamic_slice | solution.py:29
  233.0 5.7 %copy.21 = bf16[1,8,2,15,32,128]{4,5,3,2,1,0:T(8,128)(2,1)} copy(bf16[1,8,2,15,32,128]{5,4,3,2,1,0:T(8,128)(2,1)S(1)} %get-tuple-element.6) | data formatting | bytes 3932160 | tf_op jit(solution)/shard_map/jit(dynamic_index_in_dim)/dynamic_slice | solution.py:29
  238.7 0.0 collective-permute-done.9
  238.7 19.3 %maximum_select_fusion = bf16[2,4,2,8,4,15,8,128]{7,6,0,2,1,5,4,3:T(8,128)(2,1)} fusion(bf16[1,4,2,8,4,15,8,128]{7,6,0,2,1,5,4,3:T(8,128)(2,1)} %bitcast.20, bf16[1,4,2,8,4,15,8,128]{7,6,0,2,1,5,4,3:T(8,128)(2,1)} %get-tuple-element.9, pred[]{:T(512)S(6)} %eq.33), kind=kLoop, calls=%fused_computation | loop fusion | flops 23592960 | bytes 31457280 | tf_op jit(solution)/shard_map/jit(_where)/select_n | solution.py:43
  258.0 21.7 %fusion.7 = f32[8,2,128,4,128]{4,2,3,1,0:T(8,128)} fusion(bf16[8,4,15,128,128,1]{4,3,2,1,5,0:T(8,128)(2,1)} %bitcast.43, bf16[8,2,15,32,128]{3,4,2,1,0:T(8,128)(2,1)} %bitcast.47, bf16[8,2,15,32,128]{3,4,2,1,0:T(8,128)(2,1)} %bitcast.46, bf16[8,2,15,32,128]{3,4,2,1,0:T(8,128)(2,1)} %bitcast.45, bf16[8,2,15,32,128]{3,4,2,1,0:T(8,128)(2,1)} %bitcast.44), kind=kOutput, calls=%fused_computation.12 | convolution fusion | flops 4057989120 | bytes 27787264 | tf_op jit(solution)/shard_map/gikca,gjkcb->giajb/dot_general | solution.py:77
  279.7 0.0 reduce-scatter.2.cloned.1.call-update
  279.7 0.1 dynamic_slice.32
  279.8 0.1 iota_compare_fusion.2
  279.9 101.8 %reduce-scatter.2.cloned.1.call-done = f32[2,2,128,4,128]{4,2,3,1,0:T(8,128)} async-done(((f32[8,2,128,4,128]{4,2,3,1,0:T(8,128)}), f32[2,2,128,4,128]{4,2,3,1,0:T(8,128)}) %reduce-scatter.2.cloned.1.call-update) | async-done | bytes 1048592 | tf_op jit(solution)/shard_map/reduce_scatter | solution.py:80
  381.7 1.3 select_convert_fusion
  383.0 1.2 copy.25
  (10 shorter events, 0.0 us)
Async XLA Ops:
  6.5 105.1 %copy-start.6 = (bf16[8,4,15,8,128]{4,3,2,1,0:T(8,128)(2,1)S(1)}, bf16[8,4,15,8,128]{4,3,2,1,0:T(8,128)(2,1)}, u32[]{:S(2)}) copy-start(bf16[8,4,15,8,128]{4,3,2,1,0:T(8,128)(2,1)} %param.5) | copy-start | bytes 2949124
  6.5 375.1 %reduce-scatter.2.cloned.1.call-start = ((), (), s32[]{:S(2)}) async-start(), calls=%async_computation.1 | async-start | bytes 5242880 | tf_op jit(solution)/shard_map/reduce_scatter | solution.py:80
  6.5 33.7 %collective-permute-start.4 = (bf16[8,4,15,8,128]{4,3,2,1,0:T(8,128)(2,1)}, bf16[8,4,15,8,128]{4,3,2,1,0:T(8,128)(2,1)S(1)}, u32[]{:S(2)}, u32[]{:S(2)}) collective-permute-start(bf16[8,4,15,8,128]{4,3,2,1,0:T(8,128)(2,1)} %param.5), channel_id=1, source_target_pairs={{0,32},{16,48},{32,0},{48,16},{64,96},{80,112},{96,64},{112,80},{1... | collective-permute-start | bytes 2949128 | tf_op jit(solution)/shard_map/ppermute | solution.py:38
  40.3 1.0 copy-start.7
  43.4 42.9 %collective-permute-start.5 = (bf16[2,8,4,15,8,128]{5,4,0,3,2,1:T(8,128)(2,1)S(1)}, bf16[2,8,4,15,8,128]{5,4,0,3,2,1:T(8,128)(2,1)S(1)}, u32[]{:S(2)}, u32[]{:S(2)}) collective-permute-start(bf16[2,8,4,15,8,128]{5,4,0,3,2,1:T(8,128)(2,1)S(1)} %maximum_select_fusion.2), channel_id=1, source_target_pairs={{0,64},{16,80},{32,96},{48,112},{64,128},{80,144},{96,160},{112,17... | collective-permute-start | bytes 5898248 | tf_op jit(solution)/shard_map/ppermute | solution.py:20
  45.1 42.8 %collective-permute-start.7 = (bf16[2,8,4,15,8,128]{5,4,0,3,2,1:T(8,128)(2,1)S(1)}, bf16[2,8,4,15,8,128]{5,4,0,3,2,1:T(8,128)(2,1)S(1)}, u32[]{:S(2)}, u32[]{:S(2)}) collective-permute-start(bf16[2,8,4,15,8,128]{5,4,0,3,2,1:T(8,128)(2,1)S(1)} %maximum_select_fusion.2), channel_id=1, source_target_pairs={{0,192},{16,208},{32,224},{48,240},{64,0},{80,16},{96,32},{112,48}... | collective-permute-start | bytes 5898248 | tf_op jit(solution)/shard_map/ppermute | solution.py:21
  87.4 21.0 %collective-permute-start.6 = (bf16[2,4,4,15,8,128]{5,4,0,3,2,1:T(8,128)(2,1)}, bf16[2,4,4,15,8,128]{5,4,0,3,2,1:T(8,128)(2,1)}, u32[]{:S(2)}, u32[]{:S(2)}) collective-permute-start(bf16[2,4,4,15,8,128]{5,4,0,3,2,1:T(8,128)(2,1)} %slice.18), channel_id=1, source_target_pairs={{0,64},{16,80},{32,96},{48,112},{64,128},{80,144},{96,160},{112,17... | collective-permute-start | bytes 2949128 | tf_op jit(solution)/shard_map/ppermute | solution.py:26
  87.8 1.3 copy-start.1
  90.3 19.7 %collective-permute-start.8 = (bf16[2,4,4,15,8,128]{5,4,0,3,2,1:T(8,128)(2,1)}, bf16[2,4,4,15,8,128]{5,4,0,3,2,1:T(8,128)(2,1)}, u32[]{:S(2)}, u32[]{:S(2)}) collective-permute-start(bf16[2,4,4,15,8,128]{5,4,0,3,2,1:T(8,128)(2,1)} %slice.19), channel_id=1, source_target_pairs={{0,192},{16,208},{32,224},{48,240},{64,0},{80,16},{96,32},{112,48}... | collective-permute-start | bytes 2949128 | tf_op jit(solution)/shard_map/ppermute | solution.py:26
  117.6 10.7 %copy-start.9 = (s32[60]{0:T(128)S(1)}, s32[60]{0:T(128)}, u32[]{:S(2)}) copy-start(s32[60]{0:T(128)} %param.7) | copy-start | bytes 724
  117.6 10.8 %copy-start.8 = (s32[8]{0:T(128)S(1)}, s32[8]{0:T(128)}, u32[]{:S(2)}) copy-start(s32[8]{0:T(128)} %param.6) | copy-start | bytes 100
  117.6 11.8 %copy-start = (bf16[8,2,15,32,128]{4,3,2,1,0:T(8,128)(2,1)S(1)}, bf16[8,2,15,32,128]{4,3,2,1,0:T(8,128)(2,1)}, u32[]{:S(2)}) copy-start(bf16[8,2,15,32,128]{4,3,2,1,0:T(8,128)(2,1)} %param.4) | copy-start | bytes 5898244
  123.4 115.3 %collective-permute-start.9 = (bf16[4,2,8,4,15,8,128]{6,5,1,0,4,3,2:T(8,128)(2,1)}, bf16[4,2,8,4,15,8,128]{6,5,1,0,4,3,2:T(8,128)(2,1)}, u32[]{:S(2)}, u32[]{:S(2)}) collective-permute-start(bf16[4,2,8,4,15,8,128]{6,5,1,0,4,3,2:T(8,128)(2,1)} %get-tuple-element.10), channel_id=1, source_target_pairs={{0,16},{16,0},{32,48},{48,32},{64,80},{80,64},{96,112},{112,96},{1... | collective-permute-start | bytes 23592968 | tf_op jit(solution)/shard_map/ppermute | solution.py:42
  129.6 46.4 %collective-permute-start = (bf16[8,2,15,32,128]{4,3,2,1,0:T(8,128)(2,1)S(1)}, bf16[8,2,15,32,128]{4,3,2,1,0:T(8,128)(2,1)S(1)}, u32[]{:S(2)}, u32[]{:S(2)}) collective-permute-start(bf16[8,2,15,32,128]{4,3,2,1,0:T(8,128)(2,1)S(1)} %broadcast_select_fusion), channel_id=1, source_target_pairs={{0,4},{4,8},{8,12},{12,0},{1,5},{5,9},{9,13},{13,1},{2,6},{6,10},{... | collective-permute-start | bytes 5898248 | tf_op jit(solution)/shard_map/ppermute | solution.py:20
  131.4 46.1 %collective-permute-start.2 = (bf16[8,2,15,32,128]{4,3,2,1,0:T(8,128)(2,1)S(1)}, bf16[8,2,15,32,128]{4,3,2,1,0:T(8,128)(2,1)S(1)}, u32[]{:S(2)}, u32[]{:S(2)}) collective-permute-start(bf16[8,2,15,32,128]{4,3,2,1,0:T(8,128)(2,1)S(1)} %broadcast_select_fusion), channel_id=1, source_target_pairs={{0,12},{4,0},{8,4},{12,8},{1,13},{5,1},{9,5},{13,9},{2,14},{6,2},{... | collective-permute-start | bytes 5898248 | tf_op jit(solution)/shard_map/ppermute | solution.py:21
  176.0 1.3 copy-start.2
  177.4 24.1 %collective-permute-start.1 = (bf16[4,2,15,32,128]{4,3,2,1,0:T(8,128)(2,1)S(1)}, bf16[4,2,15,32,128]{4,3,2,1,0:T(8,128)(2,1)}, u32[]{:S(2)}, u32[]{:S(2)}) collective-permute-start(bf16[4,2,15,32,128]{4,3,2,1,0:T(8,128)(2,1)S(1)} %slice.16), channel_id=1, source_target_pairs={{0,4},{4,8},{8,12},{12,0},{1,5},{5,9},{9,13},{13,1},{2,6},{6,10},{... | collective-permute-start | bytes 2949128 | tf_op jit(solution)/shard_map/ppermute | solution.py:26
  177.5 1.3 copy-start.4
  179.8 23.2 %collective-permute-start.3 = (bf16[4,2,15,32,128]{4,3,2,1,0:T(8,128)(2,1)}, bf16[4,2,15,32,128]{4,3,2,1,0:T(8,128)(2,1)}, u32[]{:S(2)}, u32[]{:S(2)}) collective-permute-start(bf16[4,2,15,32,128]{4,3,2,1,0:T(8,128)(2,1)} %slice.17), channel_id=1, source_target_pairs={{0,12},{4,0},{8,4},{12,8},{1,13},{5,1},{9,5},{13,9},{2,14},{6,2},{... | collective-permute-start | bytes 2949128 | tf_op jit(solution)/shard_map/ppermute | solution.py:26
  182.5 22.2 %copy-start.3 = (bf16[8,2,15,32,128]{4,3,2,1,0:T(8,128)(2,1)S(1)}, bf16[8,2,15,32,128]{4,3,2,1,0:T(8,128)(2,1)}, u32[]{:S(2)}) copy-start(bf16[8,2,15,32,128]{4,3,2,1,0:T(8,128)(2,1)} %copy-done.2) | copy-start | bytes 5898244
  182.5 22.2 %copy-start.5 = (bf16[8,2,15,32,128]{4,3,2,1,0:T(8,128)(2,1)S(1)}, bf16[8,2,15,32,128]{4,3,2,1,0:T(8,128)(2,1)}, u32[]{:S(2)}) copy-start(bf16[8,2,15,32,128]{4,3,2,1,0:T(8,128)(2,1)} %copy-done.4) | copy-start | bytes 5898244
Sparse Core Ops, SparseCore 0:
  279.8 101.7 reduce-scatter.1

commit v2 on v1

--- a/solution.py
+++ b/solution.py
@@ -4,29 +4,30 @@
 from jax.sharding import PartitionSpec as P
 
 
-def shift_perm(n, step, period=1):
+def shift_perm(n, step, period):
     pairs = []
     for i in range(n):
-        ring = n // period if period == 1 else 4
-        pos = (i // period) % ring
-        dest = i + ((pos + step) % ring - pos) * period
-        pairs.append((i, dest))
+        pos = (i // period) % 4
+        pairs.append((i, i + ((pos + step) % 4 - pos) * period))
     return pairs
 
 
-def ring4_gather(block, axis, n, period, pos, split_axis):
+def ring4_into(block, axis, n, period, pos, out_axis):
     fwd = shift_perm(n, 1, period)
     bwd = shift_perm(n, -1, period)
     from_left = lax.ppermute(block, axis, fwd)
     from_right = lax.ppermute(block, axis, bwd)
-    half = block.shape[split_axis] // 2
-    lo = lax.slice_in_dim(from_left, 0, half, axis=split_axis)
-    hi = lax.slice_in_dim(from_right, half, block.shape[split_axis], axis=split_axis)
-    opp = jnp.concatenate(
-        [lax.ppermute(lo, axis, fwd), lax.ppermute(hi, axis, bwd)], axis=split_axis
-    )
-    ring = jnp.stack([block, from_left, opp, from_right])
-    return [lax.dynamic_index_in_dim(ring, (pos - q) % 4, 0, keepdims=False) for q in range(4)]
+    half = block.shape[0] // 2
+    opp_lo = lax.ppermute(from_left[:half], axis, fwd)
+    opp_hi = lax.ppermute(from_right[half:], axis, bwd)
+    width = block.shape[out_axis]
+    shape = list(block.shape)
+    shape[out_axis] = 4 * width
+    opp = jnp.concatenate([opp_lo, opp_hi], axis=0)
+    out = jnp.zeros(shape, block.dtype)
+    for step, piece in enumerate([block, from_left, opp, from_right]):
+        out = lax.dynamic_update_slice_in_dim(out, piece, ((pos - step) % 4) * width, axis=out_axis)
+    return out
 
 
 def gather_amplitudes(t_part):
@@ -35,22 +36,35 @@
     x = r // 4
     zh = (r // 2) % 2
     core = r % 2
+    ng = t_part.shape[0]
+    hg = ng // 2
     t_zh = lax.ppermute(t_part, "row", [(i, i ^ 2) for i in range(nrow)])
-    pair = jnp.where(zh == 0, jnp.stack([t_part, t_zh]), jnp.stack([t_zh, t_part]))
-    blocks = ring4_gather(pair, "row", nrow, 4, x, 1)
-    mine = jnp.stack(blocks)
+    pair = jnp.where(
+        zh == 0, jnp.concatenate([t_part, t_zh], axis=3), jnp.concatenate([t_zh, t_part], axis=3)
+    )
+    keep = jnp.where(core == 0, pair[:hg], pair[hg:])
+    send = jnp.where(core == 0, pair[hg:], pair[:hg])
+    got = lax.ppermute(send, "row", [(i, i ^ 1) for i in range(nrow)])
+    quad = jnp.where(
+        core == 0, jnp.concatenate([keep, got], axis=3), jnp.concatenate([got, keep], axis=3)
+    )
+    mine = ring4_into(quad, "row", nrow, 4, x, 3)
     other = lax.ppermute(mine, "row", [(i, i ^ 1) for i in range(nrow)])
-    both = jnp.where(core == 0, jnp.stack([mine, other]), jnp.stack([other, mine]))
-    ng, nj, nk, ncc, nb = t_part.shape
-    full = jnp.transpose(both, (3, 4, 5, 1, 2, 0, 6, 7))
-    return full.reshape(ng, nj, nk, 16 * ncc, nb)
+    shape = list(mine.shape)
+    shape[0] = ng
+    full = jnp.zeros(shape, mine.dtype)
+    full = lax.dynamic_update_slice_in_dim(full, mine, core * hg, axis=0)
+    full = lax.dynamic_update_slice_in_dim(full, other, (1 - core) * hg, axis=0)
+    return full
 
 
 def gather_integrals(w_part):
+    ng, ni, nk, nc, na = w_part.shape
+    w = w_part.reshape(ng, ni, nk, 2, 2, nc // 4, na)
+    w = jnp.transpose(w, (0, 1, 2, 4, 3, 5, 6)).reshape(ng, ni, nk, nc, na)
     ncol = lax.axis_size("col")
     cl = lax.axis_index("col")
-    blocks = ring4_gather(w_part, "col", ncol, 1, cl, 0)
-    return jnp.concatenate(blocks, axis=3)
+    return ring4_into(w, "col", ncol, 1, cl, 3)
 
 
 def body(integrals, amplitudes, virt_count, occ_irrep):

time: 392 us -> 742 us (1.89); the launches traced: 391 us -> 732 us
  local copies, waits for them, and re-layouts: 44.6 us -> 446 us
  waiting for transfers between devices: 249 us -> 213 us
  other arithmetic: 38.3 us -> 13.5 us
  starting transfers between devices: 24.3 us -> 36.7 us
  matrix products: 21.7 us -> 9.3 us
    dynamic_update_slice x0 -> x8, local copies, waits for them, and re-layouts: none -> 397 us  [the longest x6 377 us: ring4_into(): lax.dynamic_update_slice_in_dim(out, piece, (pos - step) % 4 * width, axi...]
    dynamic_slice x6 -> x0, local copies, waits for them, and re-layouts: 35 us -> none  [ring4_gather(): lax.dynamic_index_in_dim(ring, (pos - q) % 4, 0, keepdims=False)]
    reduce_scatter x1, waiting for transfers between devices: 102 us -> 81.9 us  [body(): lax.psum_scatter(partial_cycle, 'rep', scatter_dimension=0, tiled=True)]
    broadcast_in_dim x0 -> x3, local copies, waits for them, and re-layouts: none -> 19.8 us  [the longest x2 10.3 us: ring4_into(): out = jnp.zeros(shape, block.dtype)]
    select_n x2, other arithmetic: 21.5 us -> 2.31 us  [the longest x1 2.18 us: gather_amplitudes(): jnp.where(zh == 0, jnp.concatenate([t_part, t_zh], axis=3), jnp.concatena...]
    ppermute x8 -> x9, waiting for transfers between devices: 121 us -> 105 us  [the longest x2 85.4 us: ring4_into(): from_left = lax.ppermute(block, axis, fwd)]
    ppermute x8 -> x9, starting transfers between devices: 11.7 us -> 26.9 us  [the longest x1 17 us: gather_amplitudes(): got = lax.ppermute(send, 'row', [(i, i ^ 1) for i in range(nrow)])]
    another operation x6 -> x0, other arithmetic: 14.2 us -> none  [the longest x5 8.37 us: ring4_gather(): ring = jnp.stack([block, from_left, opp, from_right])]
  transfers between devices with their start and end apart: 11 -> 12, of which waited for: 8 -> 7; matrix products, arithmetic and copies ran while one was open for 10% -> 59% of each run, Pallas kernels for 0% -> 0%
where the time goes in v2:
time: 742 us; the launch traced here: 732 us
  local copies, waits for them, and re-layouts  446 us (60%)
  waiting for transfers between devices  213 us (29%)
  starting transfers between devices  36.7 us (5%)
  other arithmetic  13.5 us (2%)
  between operations  13.5 us (2%)
  matrix products  9.3 us (1%)
    dynamic_update_slice x6, local copies, waits for them, and re-layouts, ring4_into(): lax.dynamic_update_slice_in_dim(out, piece, (pos - step) % 4 * width, axi...  377 us
    ppermute x2, waiting for transfers between devices, ring4_into(): from_left = lax.ppermute(block, axis, fwd)  85.4 us
    reduce_scatter x1, waiting for transfers between devices, body(): lax.psum_scatter(partial_cycle, 'rep', scatter_dimension=0, tiled=True)  81.9 us
    ppermute x1, waiting for transfers between devices, gather_amplitudes(): t_zh = lax.ppermute(t_part, 'row', [(i, i ^ 2) for i in range(nrow)])  25.9 us
    ppermute x1, starting transfers between devices, gather_amplitudes(): got = lax.ppermute(send, 'row', [(i, i ^ 1) for i in range(nrow)])  17 us
    ppermute x2, waiting for transfers between devices, ring4_into(): opp_lo = lax.ppermute(from_left[:half], axis, fwd)  16.3 us
  transfers between devices with their start and end apart: 12, of which 7 were waited for; matrix products, arithmetic and copies ran while one was open for 59% of the time, Pallas kernels for 0%

profile of v2, /device:TPU:1, one launch (start us, length us, event | category | flops | bytes accessed | tf_op | source)
XLA Modules:
  0.0 732.2 jit_solution(7564986943145604840)
XLA Ops:
  6.5 7.7 %collective-permute-start.4 = (bf16[8,4,15,8,128]{4,3,2,1,0:T(8,128)(2,1)}, bf16[8,4,15,8,128]{4,3,2,1,0:T(8,128)(2,1)S(1)}, u32[]{:S(2)}, u32[]{:S(2)}) collective-permute-start(bf16[8,4,15,8,128]{4,3,2,1,0:T(8,128)(2,1)} %param.5), channel_id=1, source_target_pairs={{0,32},{16,48},{32,0},{48,16},{64,96},{80,112},{96,64},{112,80},{1... | collective-permute-start | bytes 2949128 | tf_op jit(solution)/shard_map/ppermute | solution.py:41
  14.3 25.9 %collective-permute-done.4 = bf16[8,4,15,8,128]{4,3,2,1,0:T(8,128)(2,1)S(1)} collective-permute-done((bf16[8,4,15,8,128]{4,3,2,1,0:T(8,128)(2,1)}, bf16[8,4,15,8,128]{4,3,2,1,0:T(8,128)(2,1)S(1)}, u32[]{:S(2)}, u32[]{:S(2)}) %collective-permute-start.4) | collective-permute-done | bytes 983072 | tf_op jit(solution)/shard_map/ppermute | solution.py:41
  40.1 2.2 maximum_select_fusion
  42.3 0.1 broadcast_select_fusion.1
  42.4 17.0 %collective-permute-start.5 = (bf16[4,4,15,16,128]{4,3,2,1,0:T(8,128)(2,1)S(1)}, bf16[4,4,15,16,128]{4,3,2,1,0:T(8,128)(2,1)S(1)}, u32[]{:S(2)}, u32[]{:S(2)}) collective-permute-start(bf16[4,4,15,16,128]{4,3,2,1,0:T(8,128)(2,1)S(1)} %get-tuple-element.7), channel_id=1, source_target_pairs={{0,16},{16,0},{32,48},{48,32},{64,80},{80,64},{96,112},{112,96},{1... | collective-permute-start | bytes 2949128 | tf_op jit(solution)/shard_map/ppermute | solution.py:47
  59.5 2.2 collective-permute-done.5
  61.7 5.1 broadcast_in_dim.64
  66.8 2.0 constant_dynamic-update-slice_fusion.3
  68.8 1.2 collective-permute-start.6
  70.0 1.4 collective-permute-start.8
  71.5 42.5 %collective-permute-done.6 = bf16[4,4,15,32,128]{4,3,2,1,0:T(8,128)(2,1)S(1)} collective-permute-done((bf16[4,4,15,32,128]{4,3,2,1,0:T(8,128)(2,1)S(1)}, bf16[4,4,15,32,128]{4,3,2,1,0:T(8,128)(2,1)S(1)}, u32[]{:S(2)}, u32[]{:S(2)}) %collective-permute-start.6) | collective-permute-done | bytes 1966112 | tf_op jit(solution)/shard_map/ppermute | solution.py:18
  114.0 0.1 slice.30
  114.1 0.1 collective-permute-start.7
  114.2 0.0 collective-permute-done.8
  114.2 1.1 copy-done.4
  115.3 1.0 slice.31
  116.4 1.5 collective-permute-start.9
  117.9 3.4 constant_dynamic-update-slice_fusion.2
  121.3 16.3 %collective-permute-done.7 = bf16[2,4,15,32,128]{4,3,2,1,0:T(8,128)(2,1)} collective-permute-done((bf16[2,4,15,32,128]{4,3,2,1,0:T(8,128)(2,1)S(1)}, bf16[2,4,15,32,128]{4,3,2,1,0:T(8,128)(2,1)}, u32[]{:S(2)}, u32[]{:S(2)}) %collective-permute-start.7) | collective-permute-done | bytes 983072 | tf_op jit(solution)/shard_map/ppermute | solution.py:21
  137.6 1.2 collective-permute-done.9
  138.8 3.3 maximum_dynamic-update-slice_fusion
  142.1 1.8 constant_dynamic-update-slice_fusion.1
  143.9 2.1 collective-permute-start.10
  145.9 0.0 copy-done.6
  145.9 0.1 dynamic_slice.7
  146.0 0.0 copy-done.5
  146.0 0.1 select_reduce_fusion
  146.1 0.1 iota_compare_fusion.1
  146.2 0.1 broadcast_compare_fusion
  146.3 0.8 broadcast_and_fusion
  147.1 1.7 broadcast_select_fusion
  148.8 0.3 copy.18
  149.2 1.4 collective-permute-start
  150.5 1.5 collective-permute-start.2
  152.1 42.9 %collective-permute-done = bf16[8,2,15,32,128]{4,3,2,1,0:T(8,128)(2,1)S(1)} collective-permute-done((bf16[8,2,15,32,128]{4,3,2,1,0:T(8,128)(2,1)S(1)}, bf16[8,2,15,32,128]{4,3,2,1,0:T(8,128)(2,1)S(1)}, u32[]{:S(2)}, u32[]{:S(2)}) %collective-permute-start) | collective-permute-done | bytes 1966112 | tf_op jit(solution)/shard_map/ppermute | solution.py:18
  195.0 0.1 slice.26
  195.0 0.1 collective-permute-start.1
  195.1 0.0 collective-permute-done.2
  195.1 1.5 copy-done
  196.6 1.0 slice.27
  197.7 2.5 collective-permute-start.3
  200.2 5.7 copy.19
  205.9 5.2 broadcast_in_dim.58
  211.0 75.9 %dynamic_update_slice.30 = bf16[8,2,15,128,128]{3,4,2,1,0:T(8,128)(2,1)} dynamic-update-slice(bf16[8,2,15,128,128]{3,4,2,1,0:T(8,128)(2,1)} %broadcast_in_dim.58, bf16[8,2,15,32,128]{3,4,2,1,0:T(8,128)(2,1)} %copy.19, s32[]{:T(128)} %constant.97.clone.1, s32[]{:T(128)} %constant.97.clone.1, s32[]{:T(128)} %constant.97.clone.1, s32[]{:T(128)S(6)} %select_n.131, s32[]{:T(128)} %constant.97.clone.1) | dynamic-update-slice | bytes 3932164 | tf_op jit(solution)/shard_map/dynamic_update_slice | solution.py:29
  286.9 5.7 copy.20
  292.6 98.9 %dynamic_update_slice.31 = bf16[8,2,15,128,128]{3,4,2,1,0:T(8,128)(2,1)} dynamic-update-slice(bf16[8,2,15,128,128]{3,4,2,1,0:T(8,128)(2,1)} %dynamic_update_slice.30, bf16[8,2,15,32,128]{3,4,2,1,0:T(8,128)(2,1)} %copy.20, s32[]{:T(128)} %constant.97.clone.1, s32[]{:T(128)} %constant.97.clone.1, s32[]{:T(128)} %constant.97.clone.1, s32[]{:T(128)S(6)} %select_n.133, s32[]{:T(128)} %constant.97.clone.1) | dynamic-update-slice | bytes 3932164 | tf_op jit(solution)/shard_map/dynamic_update_slice | solution.py:29
  391.5 5.7 copy.22
  397.1 0.0 collective-permute-done.1
  397.2 0.0 collective-permute-done.3
  397.2 1.7 pad_maximum_fusion
  398.8 5.8 copy.21
  404.6 98.7 %dynamic_update_slice.32 = bf16[8,2,15,128,128]{3,4,2,1,0:T(8,128)(2,1)} dynamic-update-slice(bf16[8,2,15,128,128]{3,4,2,1,0:T(8,128)(2,1)} %dynamic_update_slice.31, bf16[8,2,15,32,128]{3,4,2,1,0:T(8,128)(2,1)} %copy.21, s32[]{:T(128)} %constant.97.clone.1, s32[]{:T(128)} %constant.97.clone.1, s32[]{:T(128)} %constant.97.clone.1, s32[]{:T(128)S(6)} %select_n.135, s32[]{:T(128)} %constant.97.clone.1) | dynamic-update-slice | bytes 3932164 | tf_op jit(solution)/shard_map/dynamic_update_slice | solution.py:29
  503.3 98.7 %dynamic_update_slice.33 = bf16[8,2,15,128,128]{3,4,2,1,0:T(8,128)(2,1)} dynamic-update-slice(bf16[8,2,15,128,128]{3,4,2,1,0:T(8,128)(2,1)} %dynamic_update_slice.32, bf16[8,2,15,32,128]{3,4,2,1,0:T(8,128)(2,1)} %copy.22, s32[]{:T(128)} %constant.97.clone.1, s32[]{:T(128)} %constant.97.clone.1, s32[]{:T(128)} %constant.97.clone.1, s32[]{:T(128)S(6)} %select_n.137, s32[]{:T(128)} %constant.97.clone.1) | dynamic-update-slice | bytes 3932164 | tf_op jit(solution)/shard_map/dynamic_update_slice | solution.py:29
  602.0 9.5 %broadcast_in_dim.63 = bf16[8,4,15,128,128]{4,3,2,1,0:T(8,128)(2,1)} broadcast(bf16[]{:T(256)} %constant.99.clone.1), dimensions={} | broadcast | bytes 15728642 | tf_op jit(solution)/shard_map/broadcast_in_dim | solution.py:55
  611.5 10.0 %constant_dynamic-update-slice_fusion = bf16[8,4,15,128,128]{4,3,2,1,0:T(8,128)(2,1)} fusion(bf16[8,4,15,128,128]{4,3,2,1,0:T(8,128)(2,1)} %broadcast_in_dim.63, bf16[4,4,15,128,128]{4,3,2,1,0:T(8,128)(2,1)} %constant_dynamic-update-slice_fusion.1, s32[]{:T(128)S(6)} %select_n.157), kind=kLoop, calls=%fused_computation.18 | loop fusion | bytes 15728644 | tf_op jit(solution)/shard_map/dynamic_update_slice | solution.py:56
  621.5 0.0 collective-permute-done.10
  621.5 9.9 %constant_dynamic-update-slice_fusion.4 = bf16[8,4,15,128,128]{4,3,2,1,0:T(8,128)(2,1)} fusion(bf16[8,4,15,128,128]{4,3,2,1,0:T(8,128)(2,1)} %constant_dynamic-update-slice_fusion, bf16[4,4,15,128,128]{4,3,2,1,0:T(8,128)(2,1)} %collective-permute-done.10, s32[]{:T(128)S(6)} %select_n.158), kind=kLoop, calls=%fused_computation.22 | loop fusion | bytes 15728644 | tf_op jit(solution)/shard_map/dynamic_update_slice | solution.py:57
  631.4 9.3 %fusion.3 = f32[8,2,128,4,128]{4,2,3,1,0:T(8,128)} fusion(bf16[8,4,15,128,128]{4,3,2,1,0:T(8,128)(2,1)} %constant_dynamic-update-slice_fusion.4, bf16[8,2,15,128,128]{3,4,2,1,0:T(8,128)(2,1)S(1)} %bitcast.25), kind=kOutput, calls=%fused_computation.3 | convolution fusion | flops 4026531840 | bytes 27787264 | tf_op jit(solution)/shard_map/gikca,gjkcb->giajb/dot_general | solution.py:91
  640.7 0.0 reduce-scatter.2.cloned.1.call-update
  640.7 0.1 dynamic_slice.6
  640.8 0.1 iota_compare_fusion.2
  640.9 81.9 %reduce-scatter.2.cloned.1.call-done = f32[2,2,128,4,128]{4,2,3,1,0:T(8,128)} async-done(((f32[8,2,128,4,128]{4,2,3,1,0:T(8,128)}), f32[2,2,128,4,128]{4,2,3,1,0:T(8,128)}) %reduce-scatter.2.cloned.1.call-update) | async-done | bytes 1048592 | tf_op jit(solution)/shard_map/reduce_scatter | solution.py:94
  722.8 1.3 select_convert_fusion
  724.1 1.2 copy.23
  (18 shorter events, 0.0 us)
Async XLA Ops:
  6.5 716.3 %reduce-scatter.2.cloned.1.call-start = ((), (), s32[]{:S(2)}) async-start(), calls=%async_computation.1 | async-start | bytes 5242880 | tf_op jit(solution)/shard_map/reduce_scatter | solution.py:94
  6.5 33.6 %collective-permute-start.4 = (bf16[8,4,15,8,128]{4,3,2,1,0:T(8,128)(2,1)}, bf16[8,4,15,8,128]{4,3,2,1,0:T(8,128)(2,1)S(1)}, u32[]{:S(2)}, u32[]{:S(2)}) collective-permute-start(bf16[8,4,15,8,128]{4,3,2,1,0:T(8,128)(2,1)} %param.5), channel_id=1, source_target_pairs={{0,32},{16,48},{32,0},{48,16},{64,96},{80,112},{96,64},{112,80},{1... | collective-permute-start | bytes 2949128 | tf_op jit(solution)/shard_map/ppermute | solution.py:41
  42.4 19.2 %collective-permute-start.5 = (bf16[4,4,15,16,128]{4,3,2,1,0:T(8,128)(2,1)S(1)}, bf16[4,4,15,16,128]{4,3,2,1,0:T(8,128)(2,1)S(1)}, u32[]{:S(2)}, u32[]{:S(2)}) collective-permute-start(bf16[4,4,15,16,128]{4,3,2,1,0:T(8,128)(2,1)S(1)} %get-tuple-element.7), channel_id=1, source_target_pairs={{0,16},{16,0},{32,48},{48,32},{64,80},{80,64},{96,112},{112,96},{1... | collective-permute-start | bytes 2949128 | tf_op jit(solution)/shard_map/ppermute | solution.py:47
  68.8 45.2 %collective-permute-start.6 = (bf16[4,4,15,32,128]{4,3,2,1,0:T(8,128)(2,1)S(1)}, bf16[4,4,15,32,128]{4,3,2,1,0:T(8,128)(2,1)S(1)}, u32[]{:S(2)}, u32[]{:S(2)}) collective-permute-start(bf16[4,4,15,32,128]{4,3,2,1,0:T(8,128)(2,1)S(1)} %get-tuple-element.6), channel_id=1, source_target_pairs={{0,64},{16,80},{32,96},{48,112},{64,128},{80,144},{96,160},{112,17... | collective-permute-start | bytes 5898248 | tf_op jit(solution)/shard_map/ppermute | solution.py:18
  70.0 44.2 %collective-permute-start.8 = (bf16[4,4,15,32,128]{4,3,2,1,0:T(8,128)(2,1)S(1)}, bf16[4,4,15,32,128]{4,3,2,1,0:T(8,128)(2,1)S(1)}, u32[]{:S(2)}, u32[]{:S(2)}) collective-permute-start(bf16[4,4,15,32,128]{4,3,2,1,0:T(8,128)(2,1)S(1)} %get-tuple-element.6), channel_id=1, source_target_pairs={{0,192},{16,208},{32,224},{48,240},{64,0},{80,16},{96,32},{112,48}... | collective-permute-start | bytes 5898248 | tf_op jit(solution)/shard_map/ppermute | solution.py:19
  114.0 1.3 copy-start.4
  114.1 23.5 %collective-permute-start.7 = (bf16[2,4,15,32,128]{4,3,2,1,0:T(8,128)(2,1)S(1)}, bf16[2,4,15,32,128]{4,3,2,1,0:T(8,128)(2,1)}, u32[]{:S(2)}, u32[]{:S(2)}) collective-permute-start(bf16[2,4,15,32,128]{4,3,2,1,0:T(8,128)(2,1)S(1)} %slice.30), channel_id=1, source_target_pairs={{0,64},{16,80},{32,96},{48,112},{64,128},{80,144},{96,160},{112,17... | collective-permute-start | bytes 2949128 | tf_op jit(solution)/shard_map/ppermute | solution.py:21
  116.4 22.4 %collective-permute-start.9 = (bf16[2,4,15,32,128]{4,3,2,1,0:T(8,128)(2,1)}, bf16[2,4,15,32,128]{4,3,2,1,0:T(8,128)(2,1)}, u32[]{:S(2)}, u32[]{:S(2)}) collective-permute-start(bf16[2,4,15,32,128]{4,3,2,1,0:T(8,128)(2,1)} %slice.31), channel_id=1, source_target_pairs={{0,192},{16,208},{32,224},{48,240},{64,0},{80,16},{96,32},{112,48}... | collective-permute-start | bytes 2949128 | tf_op jit(solution)/shard_map/ppermute | solution.py:22
  121.3 24.7 %copy-start.6 = (s32[60]{0:T(128)S(1)}, s32[60]{0:T(128)}, u32[]{:S(2)}) copy-start(s32[60]{0:T(128)} %param.7) | copy-start | bytes 724
  121.3 24.8 %copy-start.5 = (s32[8]{0:T(128)S(1)}, s32[8]{0:T(128)}, u32[]{:S(2)}) copy-start(s32[8]{0:T(128)} %param.6) | copy-start | bytes 100
  143.9 477.7 %collective-permute-start.10 = (bf16[4,4,15,128,128]{4,3,2,1,0:T(8,128)(2,1)}, bf16[4,4,15,128,128]{4,3,2,1,0:T(8,128)(2,1)}, u32[]{:S(2)}, u32[]{:S(2)}) collective-permute-start(bf16[4,4,15,128,128]{4,3,2,1,0:T(8,128)(2,1)} %constant_dynamic-update-slice_fusion.1), channel_id=1, source_target_pairs={{0,16},{16,0},{32,48},{48,32},{64,80},{80,64},{96,112},{112,96},{1... | collective-permute-start | bytes 23592968 | tf_op jit(solution)/shard_map/ppermute | solution.py:52
  149.2 45.8 %collective-permute-start = (bf16[8,2,15,32,128]{4,3,2,1,0:T(8,128)(2,1)S(1)}, bf16[8,2,15,32,128]{4,3,2,1,0:T(8,128)(2,1)S(1)}, u32[]{:S(2)}, u32[]{:S(2)}) collective-permute-start(bf16[8,2,15,32,128]{4,3,2,1,0:T(8,128)(2,1)S(1)} %bitcast.21), channel_id=1, source_target_pairs={{0,4},{4,8},{8,12},{12,0},{1,5},{5,9},{9,13},{13,1},{2,6},{6,10},{... | collective-permute-start | bytes 5898248 | tf_op jit(solution)/shard_map/ppermute | solution.py:18
  150.5 44.6 %collective-permute-start.2 = (bf16[8,2,15,32,128]{4,3,2,1,0:T(8,128)(2,1)S(1)}, bf16[8,2,15,32,128]{4,3,2,1,0:T(8,128)(2,1)S(1)}, u32[]{:S(2)}, u32[]{:S(2)}) collective-permute-start(bf16[8,2,15,32,128]{4,3,2,1,0:T(8,128)(2,1)S(1)} %bitcast.22), channel_id=1, source_target_pairs={{0,12},{4,0},{8,4},{12,8},{1,13},{5,1},{9,5},{13,9},{2,14},{6,2},{... | collective-permute-start | bytes 5898248 | tf_op jit(solution)/shard_map/ppermute | solution.py:19
  195.0 2.7 copy-start.2
  195.0 202.1 %collective-permute-start.1 = (bf16[4,2,15,32,128]{4,3,2,1,0:T(8,128)(2,1)S(1)}, bf16[4,2,15,32,128]{4,3,2,1,0:T(8,128)(2,1)}, u32[]{:S(2)}, u32[]{:S(2)}) collective-permute-start(bf16[4,2,15,32,128]{4,3,2,1,0:T(8,128)(2,1)S(1)} %slice.26), channel_id=1, source_target_pairs={{0,4},{4,8},{8,12},{12,0},{1,5},{5,9},{9,13},{13,1},{2,6},{6,10},{... | collective-permute-start | bytes 2949128 | tf_op jit(solution)/shard_map/ppermute | solution.py:21
  195.1 1.5 copy-start
  197.7 199.5 %collective-permute-start.3 = (bf16[4,2,15,32,128]{4,3,2,1,0:T(8,128)(2,1)}, bf16[4,2,15,32,128]{4,3,2,1,0:T(8,128)(2,1)}, u32[]{:S(2)}, u32[]{:S(2)}) collective-permute-start(bf16[4,2,15,32,128]{4,3,2,1,0:T(8,128)(2,1)} %slice.27), channel_id=1, source_target_pairs={{0,12},{4,0},{8,4},{12,8},{1,13},{5,1},{9,5},{13,9},{2,14},{6,2},{... | collective-permute-start | bytes 2949128 | tf_op jit(solution)/shard_map/ppermute | solution.py:22
  211.0 75.9 %copy-start.3 = (bf16[8,2,15,32,128]{4,3,2,1,0:T(8,128)(2,1)S(1)}, bf16[8,2,15,32,128]{4,3,2,1,0:T(8,128)(2,1)}, u32[]{:S(2)}) copy-start(bf16[8,2,15,32,128]{4,3,2,1,0:T(8,128)(2,1)} %copy-done.2) | copy-start | bytes 5898244
  292.6 98.9 %copy-start.1 = (bf16[8,2,15,32,128]{4,3,2,1,0:T(8,128)(2,1)S(1)}, bf16[8,2,15,32,128]{4,3,2,1,0:T(8,128)(2,1)}, u32[]{:S(2)}) copy-start(bf16[8,2,15,32,128]{4,3,2,1,0:T(8,128)(2,1)} %copy-done) | copy-start | bytes 5898244
  611.5 19.9 %slice-start = ((s8[7864320]{0:T(1024)(128)(4,1)}), s8[4194304]{0:T(1024)(128)(4,1)S(1)}, s32[]{:S(2)}) async-start(s8[7864320]{0:T(1024)(128)(4,1)} %bitcast.24), calls=%async_computation.2 | async-start | bytes 8388608
  621.5 9.9 %slice-start.1 = ((s8[7864320]{0:T(1024)(128)(4,1)}), s8[3670016]{0:T(1024)(128)(4,1)S(1)}, s32[]{:S(2)}) async-start(s8[7864320]{0:T(1024)(128)(4,1)} %bitcast.24), calls=%async_computation.3 | async-start | bytes 7340032
Sparse Core Ops, SparseCore 0:
  640.9 81.9 reduce-scatter.1

commit v3 on v2

--- a/solution.py
+++ b/solution.py
@@ -30,41 +30,41 @@
     return out
 
 
-def gather_amplitudes(t_part):
+def gather_amplitudes(t_part, cl):
     nrow = lax.axis_size("row")
     r = lax.axis_index("row")
     x = r // 4
     zh = (r // 2) % 2
     core = r % 2
-    ng = t_part.shape[0]
-    hg = ng // 2
+    hj = t_part.shape[1] // 2
     t_zh = lax.ppermute(t_part, "row", [(i, i ^ 2) for i in range(nrow)])
     pair = jnp.where(
         zh == 0, jnp.concatenate([t_part, t_zh], axis=3), jnp.concatenate([t_zh, t_part], axis=3)
     )
-    keep = jnp.where(core == 0, pair[:hg], pair[hg:])
-    send = jnp.where(core == 0, pair[hg:], pair[:hg])
+    keep = jnp.where(core == 0, pair[:, :hj], pair[:, hj:])
+    send = jnp.where(core == 0, pair[:, hj:], pair[:, :hj])
     got = lax.ppermute(send, "row", [(i, i ^ 1) for i in range(nrow)])
     quad = jnp.where(
         core == 0, jnp.concatenate([keep, got], axis=3), jnp.concatenate([got, keep], axis=3)
     )
-    mine = ring4_into(quad, "row", nrow, 4, x, 3)
+    mine = ring4_into(quad, "row", nrow, 4, x - cl, 3)
     other = lax.ppermute(mine, "row", [(i, i ^ 1) for i in range(nrow)])
-    shape = list(mine.shape)
-    shape[0] = ng
-    full = jnp.zeros(shape, mine.dtype)
-    full = lax.dynamic_update_slice_in_dim(full, mine, core * hg, axis=0)
-    full = lax.dynamic_update_slice_in_dim(full, other, (1 - core) * hg, axis=0)
-    return full
+    return mine, other
 
 
 def gather_integrals(w_part):
     ng, ni, nk, nc, na = w_part.shape
     w = w_part.reshape(ng, ni, nk, 2, 2, nc // 4, na)
-    w = jnp.transpose(w, (0, 1, 2, 4, 3, 5, 6)).reshape(ng, ni, nk, nc, na)
-    ncol = lax.axis_size("col")
-    cl = lax.axis_index("col")
-    return ring4_into(w, "col", ncol, 1, cl, 3)
+    w = jnp.transpose(w, (0, 1, 2, 6, 4, 3, 5)).reshape(ng, ni, nk, na, nc)
+    fwd = shift_perm(4, 1, 1)
+    bwd = shift_perm(4, -1, 1)
+    from_left = lax.ppermute(w, "col", fwd)
+    from_right = lax.ppermute(w, "col", bwd)
+    half = ng // 2
+    opp_lo = lax.ppermute(from_left[:half], "col", fwd)
+    opp_hi = lax.ppermute(from_right[half:], "col", bwd)
+    opp = jnp.concatenate([opp_lo, opp_hi], axis=0)
+    return jnp.concatenate([w, from_right, opp, from_left], axis=4)
 
 
 def body(integrals, amplitudes, virt_count, occ_irrep):
@@ -74,6 +74,7 @@
     nvirt = integrals.shape[4]
     rep_index = lax.axis_index("rep")
     col_index = lax.axis_index("col")
+    core = lax.axis_index("row") % 2
     occ_local = lax.dynamic_slice_in_dim(occ_irrep, rep_index * k_local, k_local)
     groups = jnp.arange(ngroup, dtype=jnp.int32)
     blocks = jnp.bitwise_xor(groups[:, None], occ_local[None, :])
@@ -87,11 +88,14 @@
     masked = jnp.where(keep, integrals, jnp.zeros_like(integrals))
     owned = ngroup // lax.axis_size("rep")
     w_full = gather_integrals(masked)
-    t_full = gather_amplitudes(amplitudes)
-    partial_cycle = jnp.einsum(
-        "gikca,gjkcb->giajb", w_full, t_full, preferred_element_type=jnp.float32
+    t_mine, t_other = gather_amplitudes(amplitudes, col_index)
+    sums = []
+    for t_half in (t_mine, t_other):
+        part = jnp.einsum("gikac,gjkcb->giajb", w_full, t_half, preferred_element_type=jnp.float32)
+        sums.append(lax.psum_scatter(part, "rep", scatter_dimension=0, tiled=True))
+    summed = jnp.where(
+        core == 0, jnp.concatenate(sums, axis=3), jnp.concatenate(sums[::-1], axis=3)
     )
-    summed = lax.psum_scatter(partial_cycle, "rep", scatter_dimension=0, tiled=True)
     own_counts = lax.dynamic_slice_in_dim(virt_count, rep_index * owned, owned)
     b_live = places[None, :] < own_counts[:, None]
     result = jnp.where(b_live[:, None, None, None, :], summed, jnp.zeros_like(summed))

time: 742 us -> 339 us (0.46); the launches traced: 732 us -> 339 us
  local copies, waits for them, and re-layouts: 446 us -> 48 us
  waiting for transfers between devices: 213 us -> 194 us
  other arithmetic: 13.5 us -> 27.2 us
    dynamic_update_slice x6 -> x2, local copies, waits for them, and re-layouts: 377 us -> 4.99 us  [ring4_into(): lax.dynamic_update_slice_in_dim(out, piece, (pos - step) % 4 * width, axi...]
    ppermute x2 -> x1, waiting for transfers between devices: 85.4 us -> 0.01 us  [ring4_into(): from_left = lax.ppermute(block, axis, fwd)]
    ppermute x2 -> x1, waiting for transfers between devices: 0.01 us -> 41.9 us  [ring4_into(): from_right = lax.ppermute(block, axis, bwd)]
    dynamic_update_slice x2 -> x0, local copies, waits for them, and re-layouts: 19.9 us -> none  [the longest x1 9.98 us: gather_amplitudes(): full = lax.dynamic_update_slice_in_dim(full, mine, core * hg, axis=0)]
    ppermute x0 -> x4, waiting for transfers between devices: none -> 15.1 us  [the longest x1 14.4 us: gather_integrals(): from_right = lax.ppermute(w, 'col', bwd)]
    concatenate x1 -> x2, other arithmetic: 1.67 us -> 15.9 us  [the longest x1 14.3 us: gather_integrals(): return jnp.concatenate([w, from_right, opp, from_left], axis=4)]
    reduce_scatter x1 -> x2, waiting for transfers between devices: 81.9 us -> 93.7 us  [body(): sums.append(lax.psum_scatter(part, 'rep', scatter_dimension=0, tiled=True))]
    ppermute x2 -> x1, waiting for transfers between devices: 16.3 us -> 5.71 us  [ring4_into(): opp_lo = lax.ppermute(from_left[:half], axis, fwd)]
  transfers between devices with their start and end apart: 12 -> 13, of which waited for: 7 -> 9; matrix products, arithmetic and copies ran while one was open for 59% -> 22% of each run, Pallas kernels for 0% -> 0%
where the time goes in v3:
time: 339 us
  waiting for transfers between devices  194 us (57%)
  local copies, waits for them, and re-layouts  48 us (14%)
  starting transfers between devices  39.5 us (12%)
  other arithmetic  27.2 us (8%)
  matrix products  16 us (5%)
  between operations  13.5 us (4%)
    reduce_scatter x2, waiting for transfers between devices, body(): sums.append(lax.psum_scatter(part, 'rep', scatter_dimension=0, tiled=True))  93.7 us
    ppermute x1, waiting for transfers between devices, ring4_into(): from_right = lax.ppermute(block, axis, bwd)  41.9 us
    ppermute x1, waiting for transfers between devices, gather_amplitudes(): t_zh = lax.ppermute(t_part, 'row', [(i, i ^ 2) for i in range(nrow)])  25.9 us
    ppermute x1, starting transfers between devices, gather_amplitudes(): got = lax.ppermute(send, 'row', [(i, i ^ 1) for i in range(nrow)])  17 us
    dot_general x2, matrix products, body(): jnp.einsum('gikac,gjkcb->giajb', w_full, t_half, preferred_element_type=j...  16 us
    ppermute x1, waiting for transfers between devices, gather_integrals(): from_right = lax.ppermute(w, 'col', bwd)  14.4 us
    concatenate x1, other arithmetic, gather_integrals(): return jnp.concatenate([w, from_right, opp, from_left], axis=4)  14.3 us
    ppermute x1, waiting for transfers between devices, ring4_into(): opp_hi = lax.ppermute(from_right[half:], axis, bwd)  10 us
  transfers between devices with their start and end apart: 13, of which 9 were waited for; matrix products, arithmetic and copies ran while one was open for 22% of the time, Pallas kernels for 0%

profile of v3, /device:TPU:1, one launch (start us, length us, event | category | flops | bytes accessed | tf_op | source)
XLA Modules:
  0.0 338.7 jit_solution(5800117929361033153)
XLA Ops:
  6.5 0.0 reduce-scatter.3.cloned.1.call-start
  6.5 7.7 %collective-permute-start.4 = (bf16[8,4,15,8,128]{4,3,2,1,0:T(8,128)(2,1)}, bf16[8,4,15,8,128]{4,3,2,1,0:T(8,128)(2,1)S(1)}, u32[]{:S(2)}, u32[]{:S(2)}) collective-permute-start(bf16[8,4,15,8,128]{4,3,2,1,0:T(8,128)(2,1)} %param.5), channel_id=1, source_target_pairs={{0,32},{16,48},{32,0},{48,16},{64,96},{80,112},{96,64},{112,80},{1... | collective-permute-start | bytes 2949128 | tf_op jit(solution)/shard_map/ppermute | solution.py:40
  14.3 25.9 %collective-permute-done.4 = bf16[8,4,15,8,128]{4,3,2,1,0:T(8,128)(2,1)S(1)} collective-permute-done((bf16[8,4,15,8,128]{4,3,2,1,0:T(8,128)(2,1)}, bf16[8,4,15,8,128]{4,3,2,1,0:T(8,128)(2,1)S(1)}, u32[]{:S(2)}, u32[]{:S(2)}) %collective-permute-start.4) | collective-permute-done | bytes 983072 | tf_op jit(solution)/shard_map/ppermute | solution.py:40
  40.1 2.1 maximum_select_fusion
  42.3 0.1 broadcast_select_fusion.1
  42.4 17.0 %collective-permute-start.5 = (bf16[8,2,15,16,128]{4,3,2,1,0:T(8,128)(2,1)S(1)}, bf16[8,2,15,16,128]{4,3,2,1,0:T(8,128)(2,1)S(1)}, u32[]{:S(2)}, u32[]{:S(2)}) collective-permute-start(bf16[8,2,15,16,128]{4,3,2,1,0:T(8,128)(2,1)S(1)} %get-tuple-element.7), channel_id=1, source_target_pairs={{0,16},{16,0},{32,48},{48,32},{64,80},{80,64},{96,112},{112,96},{1... | collective-permute-start | bytes 2949128 | tf_op jit(solution)/shard_map/ppermute | solution.py:46
  59.5 2.2 collective-permute-done.5
  61.7 5.2 %broadcast_in_dim.56 = bf16[8,2,15,128,128]{4,3,2,1,0:T(8,128)(2,1)} broadcast(bf16[]{:T(256)} %constant.87.clone.1), dimensions={} | broadcast | bytes 7864322 | tf_op jit(solution)/shard_map/broadcast_in_dim | solution.py:27
  66.8 2.9 constant_dynamic-update-slice_fusion.1
  69.7 2.5 collective-permute-start.8
  72.1 0.0 collective-permute-start.6
  72.1 0.0 copy-done.5
  72.2 0.1 dynamic_slice.7
  72.2 0.0 copy-done.4
  72.2 0.1 select_reduce_fusion
  72.3 0.1 iota_compare_fusion.1
  72.4 41.9 %collective-permute-done.8 = bf16[8,2,15,32,128]{4,3,2,1,0:T(8,128)(2,1)S(1)} collective-permute-done((bf16[8,2,15,32,128]{4,3,2,1,0:T(8,128)(2,1)}, bf16[8,2,15,32,128]{4,3,2,1,0:T(8,128)(2,1)S(1)}, u32[]{:S(2)}, u32[]{:S(2)}) %collective-permute-start.8) | collective-permute-done | bytes 1966112 | tf_op jit(solution)/shard_map/ppermute | solution.py:19
  114.3 0.1 slice.31
  114.3 3.4 collective-permute-start.9
  117.7 0.0 collective-permute-done.6
  117.7 2.3 slice.30
  120.0 0.0 collective-permute-start.7
  120.0 0.1 broadcast_compare_fusion
  120.1 0.8 broadcast_and_fusion
  120.9 0.2 broadcast_select_fusion
  121.1 0.0 copy-done.1
  121.1 0.3 copy.22
  121.4 2.8 collective-permute-start
  124.3 0.0 collective-permute-start.1
  124.3 3.3 constant_dynamic-update-slice_fusion
  127.6 10.0 %collective-permute-done.9 = bf16[4,2,15,32,128]{4,3,2,1,0:T(8,128)(2,1)} collective-permute-done((bf16[4,2,15,32,128]{4,3,2,1,0:T(8,128)(2,1)S(1)}, bf16[4,2,15,32,128]{4,3,2,1,0:T(8,128)(2,1)}, u32[]{:S(2)}, u32[]{:S(2)}) %collective-permute-start.9) | collective-permute-done | bytes 983072 | tf_op jit(solution)/shard_map/ppermute | solution.py:22
  137.6 5.7 %collective-permute-done.7 = bf16[4,2,15,32,128]{4,3,2,1,0:T(8,128)(2,1)} collective-permute-done((bf16[4,2,15,32,128]{4,3,2,1,0:T(8,128)(2,1)}, bf16[4,2,15,32,128]{4,3,2,1,0:T(8,128)(2,1)}, u32[]{:S(2)}, u32[]{:S(2)}) %collective-permute-start.7) | collective-permute-done | bytes 983072 | tf_op jit(solution)/shard_map/ppermute | solution.py:21
  143.3 3.2 maximum_dynamic-update-slice_fusion
  146.5 0.0 copy-done.2
  146.5 1.7 constant_dynamic-update-slice_fusion.2
  148.2 2.4 collective-permute-start.10
  150.5 14.4 %collective-permute-done = bf16[8,2,15,128,32]{3,4,2,1,0:T(8,128)(2,1)} collective-permute-done((bf16[8,2,15,128,32]{3,4,2,1,0:T(8,128)(2,1)S(1)}, bf16[8,2,15,128,32]{3,4,2,1,0:T(8,128)(2,1)}, u32[]{:S(2)}, u32[]{:S(2)}) %collective-permute-start) | collective-permute-done | bytes 1966112 | tf_op jit(solution)/shard_map/ppermute | solution.py:62
  164.9 1.3 slice.27
  166.2 3.6 %collective-permute-start.3 = (bf16[4,2,15,128,32]{3,4,2,1,0:T(8,128)(2,1)S(1)}, bf16[4,2,15,128,32]{3,4,2,1,0:T(8,128)(2,1)}, u32[]{:S(2)}, u32[]{:S(2)}) collective-permute-start(bf16[4,2,15,128,32]{3,4,2,1,0:T(8,128)(2,1)S(1)} %slice.27), channel_id=1, source_target_pairs={{0,12},{4,0},{8,4},{12,8},{1,13},{5,1},{9,5},{13,9},{2,14},{6,2},{... | collective-permute-start | bytes 2949128 | tf_op jit(solution)/shard_map/ppermute | solution.py:65
  169.8 0.0 collective-permute-done.1
  169.8 2.2 slice.26
  172.0 0.0 collective-permute-start.2
  172.0 5.7 %copy.23 = bf16[8,2,15,128,32]{4,3,2,1,0:T(8,128)(2,1)} copy(bf16[8,2,15,128,32]{3,4,2,1,0:T(8,128)(2,1)S(1)} %bitcast.32) | data formatting | bytes 3932160 | tf_op jit(solution)/shard_map/reshape | solution.py:58
  177.7 8.0 %copy.26 = bf16[8,2,15,128,32]{4,3,2,1,0:T(8,128)(2,1)} copy(bf16[8,2,15,128,32]{3,4,2,1,0:T(8,128)(2,1)} %collective-permute-done.1) | data formatting | bytes 3932160 | tf_op jit(solution)/shard_map/ppermute | solution.py:61
  185.7 7.8 %copy.24 = bf16[8,2,15,128,32]{4,3,2,1,0:T(8,128)(2,1)} copy(bf16[8,2,15,128,32]{3,4,2,1,0:T(8,128)(2,1)} %collective-permute-done) | data formatting | bytes 3932160 | tf_op jit(solution)/shard_map/ppermute | solution.py:62
  193.5 0.0 collective-permute-done.3
  193.5 0.7 collective-permute-done.2
  194.2 1.7 pad_maximum_fusion
  195.9 5.7 %copy.25 = bf16[8,2,15,128,32]{4,3,2,1,0:T(8,128)(2,1)} copy(bf16[8,2,15,128,32]{3,4,2,1,0:T(8,128)(2,1)S(1)} %pad_maximum_fusion) | data formatting | bytes 3932160 | tf_op jit(solution)/shard_map/concatenate | solution.py:66
  201.6 14.3 %maximum_bitcast_fusion = bf16[8,2,15,128,128,1]{4,3,2,5,1,0:T(8,128)(2,1)S(1)} fusion(bf16[8,2,15,128,32]{4,3,2,1,0:T(8,128)(2,1)} %copy.26, bf16[8,2,15,128,32]{4,3,2,1,0:T(8,128)(2,1)} %copy.25, bf16[8,2,15,128,32]{4,3,2,1,0:T(8,128)(2,1)} %copy.24, bf16[8,2,15,128,32]{4,3,2,1,0:T(8,128)(2,1)} %copy.23), kind=kLoop, calls=%fused_computation | loop fusion | flops 31457280 | bytes 15728640 | tf_op jit(solution)/shard_map/concatenate | solution.py:67
  215.9 0.0 copy-start
  215.9 3.1 copy-done
  219.0 6.9 %fusion.4 = f32[8,2,128,2,128]{4,2,3,1,0:T(8,128)} fusion(bf16[8,2,15,128,128,1]{4,3,2,5,1,0:T(8,128)(2,1)S(1)} %maximum_bitcast_fusion, bf16[8,2,15,128,128]{4,3,2,1,0:T(8,128)(2,1)} %constant_dynamic-update-slice_fusion.2), kind=kOutput, calls=%fused_computation.10 | convolution fusion | flops 2013265920 | bytes 17825792 | tf_op jit(solution)/shard_map/gikac,gjkcb->giajb/dot_general | solution.py:94
  225.9 0.0 reduce-scatter.3.cloned.1.call-update
  225.9 0.0 reduce-scatter.5.cloned.1.call-start
  226.0 0.0 collective-permute-done.10
  226.0 9.1 %fusion.7 = f32[8,2,128,2,128]{4,2,3,1,0:T(8,128)} fusion(bf16[8,2,15,128,128,1]{4,3,2,5,1,0:T(8,128)(2,1)} %copy-done, bf16[8,2,15,128,128]{4,3,2,1,0:T(8,128)(2,1)} %collective-permute-done.10), kind=kOutput, calls=%fused_computation.11 | convolution fusion | flops 2013265920 | bytes 17825792 | tf_op jit(solution)/shard_map/gikac,gjkcb->giajb/dot_general | solution.py:94
  235.1 0.0 reduce-scatter.5.cloned.1.call-update
  235.1 0.1 dynamic_slice.6
  235.2 0.1 iota_compare_fusion.2
  235.3 42.7 %reduce-scatter.3.cloned.1.call-done = f32[2,2,128,2,128]{4,2,3,1,0:T(8,128)} async-done(((f32[8,2,128,2,128]{4,2,3,1,0:T(8,128)}), f32[2,2,128,2,128]{4,2,3,1,0:T(8,128)}) %reduce-scatter.3.cloned.1.call-update) | async-done | bytes 524304 | tf_op jit(solution)/shard_map/reduce_scatter | solution.py:95
  278.0 50.9 %reduce-scatter.5.cloned.1.call-done = f32[2,2,128,2,128]{4,2,3,1,0:T(8,128)} async-done(((f32[8,2,128,2,128]{4,2,3,1,0:T(8,128)}), f32[2,2,128,2,128]{4,2,3,1,0:T(8,128)}) %reduce-scatter.5.cloned.1.call-update) | async-done | bytes 524304 | tf_op jit(solution)/shard_map/reduce_scatter | solution.py:95
  329.0 1.7 fusion.11
  330.6 1.2 copy.27
  (8 shorter events, 0.0 us)
Async XLA Ops:
  6.5 271.5 %reduce-scatter.3.cloned.1.call-start = ((), (), s32[]{:S(2)}) async-start(), calls=%async_computation.2 | async-start | bytes 2621440 | tf_op jit(solution)/shard_map/reduce_scatter | solution.py:95
  6.5 33.6 %collective-permute-start.4 = (bf16[8,4,15,8,128]{4,3,2,1,0:T(8,128)(2,1)}, bf16[8,4,15,8,128]{4,3,2,1,0:T(8,128)(2,1)S(1)}, u32[]{:S(2)}, u32[]{:S(2)}) collective-permute-start(bf16[8,4,15,8,128]{4,3,2,1,0:T(8,128)(2,1)} %param.5), channel_id=1, source_target_pairs={{0,32},{16,48},{32,0},{48,16},{64,96},{80,112},{96,64},{112,80},{1... | collective-permute-start | bytes 2949128 | tf_op jit(solution)/shard_map/ppermute | solution.py:40
  42.4 19.2 %collective-permute-start.5 = (bf16[8,2,15,16,128]{4,3,2,1,0:T(8,128)(2,1)S(1)}, bf16[8,2,15,16,128]{4,3,2,1,0:T(8,128)(2,1)S(1)}, u32[]{:S(2)}, u32[]{:S(2)}) collective-permute-start(bf16[8,2,15,16,128]{4,3,2,1,0:T(8,128)(2,1)S(1)} %get-tuple-element.7), channel_id=1, source_target_pairs={{0,16},{16,0},{32,48},{48,32},{64,80},{80,64},{96,112},{112,96},{1... | collective-permute-start | bytes 2949128 | tf_op jit(solution)/shard_map/ppermute | solution.py:46
  66.8 5.3 %copy-start.5 = (s32[60]{0:T(128)S(1)}, s32[60]{0:T(128)}, u32[]{:S(2)}) copy-start(s32[60]{0:T(128)} %param.7) | copy-start | bytes 724
  66.8 5.4 %copy-start.4 = (s32[8]{0:T(128)S(1)}, s32[8]{0:T(128)}, u32[]{:S(2)}) copy-start(s32[8]{0:T(128)} %param.6) | copy-start | bytes 100
  69.7 44.6 %collective-permute-start.8 = (bf16[8,2,15,32,128]{4,3,2,1,0:T(8,128)(2,1)}, bf16[8,2,15,32,128]{4,3,2,1,0:T(8,128)(2,1)S(1)}, u32[]{:S(2)}, u32[]{:S(2)}) collective-permute-start(bf16[8,2,15,32,128]{4,3,2,1,0:T(8,128)(2,1)} %get-tuple-element.6), channel_id=1, source_target_pairs={{0,192},{16,208},{32,224},{48,240},{64,0},{80,16},{96,32},{112,48}... | collective-permute-start | bytes 5898248 | tf_op jit(solution)/shard_map/ppermute | solution.py:19
  72.1 45.6 %collective-permute-start.6 = (bf16[8,2,15,32,128]{4,3,2,1,0:T(8,128)(2,1)}, bf16[8,2,15,32,128]{4,3,2,1,0:T(8,128)(2,1)}, u32[]{:S(2)}, u32[]{:S(2)}) collective-permute-start(bf16[8,2,15,32,128]{4,3,2,1,0:T(8,128)(2,1)} %get-tuple-element.6), channel_id=1, source_target_pairs={{0,64},{16,80},{32,96},{48,112},{64,128},{80,144},{96,160},{112,17... | collective-permute-start | bytes 5898248 | tf_op jit(solution)/shard_map/ppermute | solution.py:18
  72.2 48.7 %copy-start.3 = (bf16[8,2,15,32,128]{4,3,2,1,0:T(8,128)(2,1)S(1)}, bf16[8,2,15,32,128]{4,3,2,1,0:T(8,128)(2,1)}, u32[]{:S(2)}) copy-start(bf16[8,2,15,32,128]{4,3,2,1,0:T(8,128)(2,1)} %param.4) | copy-start | bytes 5898244
  114.3 6.8 %copy-start.1 = (bf16[8,2,15,32,128]{4,3,2,1,0:T(8,128)(2,1)}, bf16[8,2,15,32,128]{4,3,2,1,0:T(8,128)(2,1)S(1)}, u32[]{:S(2)}) copy-start(bf16[8,2,15,32,128]{4,3,2,1,0:T(8,128)(2,1)S(1)} %collective-permute-done.8) | copy-start | bytes 5898244
  114.3 23.3 %collective-permute-start.9 = (bf16[4,2,15,32,128]{4,3,2,1,0:T(8,128)(2,1)S(1)}, bf16[4,2,15,32,128]{4,3,2,1,0:T(8,128)(2,1)}, u32[]{:S(2)}, u32[]{:S(2)}) collective-permute-start(bf16[4,2,15,32,128]{4,3,2,1,0:T(8,128)(2,1)S(1)} %slice.31), channel_id=1, source_target_pairs={{0,192},{16,208},{32,224},{48,240},{64,0},{80,16},{96,32},{112,48}... | collective-permute-start | bytes 2949128 | tf_op jit(solution)/shard_map/ppermute | solution.py:22
  120.0 23.3 %collective-permute-start.7 = (bf16[4,2,15,32,128]{4,3,2,1,0:T(8,128)(2,1)}, bf16[4,2,15,32,128]{4,3,2,1,0:T(8,128)(2,1)}, u32[]{:S(2)}, u32[]{:S(2)}) collective-permute-start(bf16[4,2,15,32,128]{4,3,2,1,0:T(8,128)(2,1)} %slice.30), channel_id=1, source_target_pairs={{0,64},{16,80},{32,96},{48,112},{64,128},{80,144},{96,160},{112,17... | collective-permute-start | bytes 2949128 | tf_op jit(solution)/shard_map/ppermute | solution.py:21
  121.4 43.5 %collective-permute-start = (bf16[8,2,15,128,32]{3,4,2,1,0:T(8,128)(2,1)S(1)}, bf16[8,2,15,128,32]{3,4,2,1,0:T(8,128)(2,1)}, u32[]{:S(2)}, u32[]{:S(2)}) collective-permute-start(bf16[8,2,15,128,32]{3,4,2,1,0:T(8,128)(2,1)S(1)} %bitcast.30), channel_id=1, source_target_pairs={{0,12},{4,0},{8,4},{12,8},{1,13},{5,1},{9,5},{13,9},{2,14},{6,2},{... | collective-permute-start | bytes 5898248 | tf_op jit(solution)/shard_map/ppermute | solution.py:62
  124.3 45.5 %collective-permute-start.1 = (bf16[8,2,15,128,32]{3,4,2,1,0:T(8,128)(2,1)S(1)}, bf16[8,2,15,128,32]{3,4,2,1,0:T(8,128)(2,1)}, u32[]{:S(2)}, u32[]{:S(2)}) collective-permute-start(bf16[8,2,15,128,32]{3,4,2,1,0:T(8,128)(2,1)S(1)} %bitcast.31), channel_id=1, source_target_pairs={{0,4},{4,8},{8,12},{12,0},{1,5},{5,9},{9,13},{13,1},{2,6},{6,10},{... | collective-permute-start | bytes 5898248 | tf_op jit(solution)/shard_map/ppermute | solution.py:61
  124.3 22.2 %copy-start.2 = (bf16[8,2,15,32,128]{4,3,2,1,0:T(8,128)(2,1)S(1)}, bf16[8,2,15,32,128]{4,3,2,1,0:T(8,128)(2,1)}, u32[]{:S(2)}) copy-start(bf16[8,2,15,32,128]{4,3,2,1,0:T(8,128)(2,1)} %copy-done.1) | copy-start | bytes 5898244
  148.2 77.8 %collective-permute-start.10 = (bf16[8,2,15,128,128]{4,3,2,1,0:T(8,128)(2,1)}, bf16[8,2,15,128,128]{4,3,2,1,0:T(8,128)(2,1)}, u32[]{:S(2)}, u32[]{:S(2)}) collective-permute-start(bf16[8,2,15,128,128]{4,3,2,1,0:T(8,128)(2,1)} %constant_dynamic-update-slice_fusion.2), channel_id=1, source_target_pairs={{0,16},{16,0},{32,48},{48,32},{64,80},{80,64},{96,112},{112,96},{1... | collective-permute-start | bytes 23592968 | tf_op jit(solution)/shard_map/ppermute | solution.py:51
  166.2 27.3 %collective-permute-start.3 = (bf16[4,2,15,128,32]{3,4,2,1,0:T(8,128)(2,1)S(1)}, bf16[4,2,15,128,32]{3,4,2,1,0:T(8,128)(2,1)}, u32[]{:S(2)}, u32[]{:S(2)}) collective-permute-start(bf16[4,2,15,128,32]{3,4,2,1,0:T(8,128)(2,1)S(1)} %slice.27), channel_id=1, source_target_pairs={{0,12},{4,0},{8,4},{12,8},{1,13},{5,1},{9,5},{13,9},{2,14},{6,2},{... | collective-permute-start | bytes 2949128 | tf_op jit(solution)/shard_map/ppermute | solution.py:65
  172.0 22.2 %collective-permute-start.2 = (bf16[4,2,15,128,32]{3,4,2,1,0:T(8,128)(2,1)}, bf16[4,2,15,128,32]{3,4,2,1,0:T(8,128)(2,1)}, u32[]{:S(2)}, u32[]{:S(2)}) collective-permute-start(bf16[4,2,15,128,32]{3,4,2,1,0:T(8,128)(2,1)} %slice.26), channel_id=1, source_target_pairs={{0,4},{4,8},{8,12},{12,0},{1,5},{5,9},{9,13},{13,1},{2,6},{6,10},{... | collective-permute-start | bytes 2949128 | tf_op jit(solution)/shard_map/ppermute | solution.py:64
  215.9 3.2 copy-start
  225.9 103.0 %reduce-scatter.5.cloned.1.call-start = ((), (), s32[]{:S(2)}) async-start(), calls=%async_computation.3 | async-start | bytes 2621440 | tf_op jit(solution)/shard_map/reduce_scatter | solution.py:95
Sparse Core Ops, SparseCore 0:
  226.1 51.9 reduce-scatter.2
  280.6 48.3 reduce-scatter.4

commit v4 on v3

--- a/solution.py
+++ b/solution.py
@@ -44,18 +44,20 @@
     keep = jnp.where(core == 0, pair[:, :hj], pair[:, hj:])
     send = jnp.where(core == 0, pair[:, hj:], pair[:, :hj])
     got = lax.ppermute(send, "row", [(i, i ^ 1) for i in range(nrow)])
+    ng, nh, nk, nzc, nb = keep.shape
+    keep5 = keep.reshape(ng, nh, nk, 2, nzc // 2, nb)
+    got5 = got.reshape(ng, nh, nk, 2, nzc // 2, nb)
     quad = jnp.where(
-        core == 0, jnp.concatenate([keep, got], axis=3), jnp.concatenate([got, keep], axis=3)
-    )
+        core == 0, jnp.stack([keep5, got5], axis=4), jnp.stack([got5, keep5], axis=4)
+    ).reshape(ng, nh, nk, 2 * nzc, nb)
     mine = ring4_into(quad, "row", nrow, 4, x - cl, 3)
     other = lax.ppermute(mine, "row", [(i, i ^ 1) for i in range(nrow)])
     return mine, other
 
 
 def gather_integrals(w_part):
-    ng, ni, nk, nc, na = w_part.shape
-    w = w_part.reshape(ng, ni, nk, 2, 2, nc // 4, na)
-    w = jnp.transpose(w, (0, 1, 2, 6, 4, 3, 5)).reshape(ng, ni, nk, na, nc)
+    ng = w_part.shape[0]
+    w = w_part
     fwd = shift_perm(4, 1, 1)
     bwd = shift_perm(4, -1, 1)
     from_left = lax.ppermute(w, "col", fwd)
@@ -64,7 +66,7 @@
     opp_lo = lax.ppermute(from_left[:half], "col", fwd)
     opp_hi = lax.ppermute(from_right[half:], "col", bwd)
     opp = jnp.concatenate([opp_lo, opp_hi], axis=0)
-    return jnp.concatenate([w, from_right, opp, from_left], axis=4)
+    return [w, from_right, opp, from_left]
 
 
 def body(integrals, amplitudes, virt_count, occ_irrep):
@@ -87,11 +89,20 @@
     keep = c_live[:, None, :, :, None] & a_live[:, None, None, None, :]
     masked = jnp.where(keep, integrals, jnp.zeros_like(integrals))
     owned = ngroup // lax.axis_size("rep")
-    w_full = gather_integrals(masked)
+    w_blocks = gather_integrals(masked)
     t_mine, t_other = gather_amplitudes(amplitudes, col_index)
     sums = []
     for t_half in (t_mine, t_other):
-        part = jnp.einsum("gikac,gjkcb->giajb", w_full, t_half, preferred_element_type=jnp.float32)
+        width = c_local
+        part = None
+        for s, w_blk in enumerate(w_blocks):
+            term = jnp.einsum(
+                "gikca,gjkcb->giajb",
+                w_blk,
+                t_half[:, :, :, s * width:(s + 1) * width],
+                preferred_element_type=jnp.float32,
+            )
+            part = term if part is None else part + term
         sums.append(lax.psum_scatter(part, "rep", scatter_dimension=0, tiled=True))
     summed = jnp.where(
         core == 0, jnp.concatenate(sums, axis=3), jnp.concatenate(sums[::-1], axis=3)

time: 339 us -> 337 us (level)
  waiting for transfers between devices: 194 us -> 235 us
  local copies, waits for them, and re-layouts: 48 us -> 18.5 us
  other arithmetic: 27.2 us -> 7.46 us
  matrix products: 16 us -> 22.9 us
    ppermute x1, waiting for transfers between devices: 0.01 us -> 42.9 us  [gather_integrals(): from_left = lax.ppermute(w, 'col', fwd)]
    ppermute x1, waiting for transfers between devices: 0.01 us -> 42.6 us  [ring4_into(): from_left = lax.ppermute(block, axis, fwd)]
    ppermute x1, waiting for transfers between devices: 41.9 us -> 0.01 us  [ring4_into(): from_right = lax.ppermute(block, axis, bwd)]
    ppermute x1, waiting for transfers between devices: 0.69 us -> 20.9 us  [gather_integrals(): opp_lo = lax.ppermute(from_left[:half], 'col', fwd)]
    concatenate x2 -> x0, other arithmetic: 15.9 us -> none  [the longest x1 14.3 us: gather_integrals(): return jnp.concatenate([w, from_right, opp, from_left], axis=4)]
    ppermute x2 -> x0, local copies, waits for them, and re-layouts: 15.8 us -> none  [the longest x1 7.95 us: gather_integrals(): from_left = lax.ppermute(w, 'col', fwd)]
    ppermute x1, waiting for transfers between devices: 14.4 us -> 0.01 us  [gather_integrals(): from_right = lax.ppermute(w, 'col', bwd)]
    ppermute x1, waiting for transfers between devices: 10 us -> 0.34 us  [ring4_into(): opp_hi = lax.ppermute(from_right[half:], axis, bwd)]
  transfers between devices with their start and end apart: 13 -> 13, of which waited for: 9 -> 9; matrix products, arithmetic and copies ran while one was open for 22% -> 11% of each run, Pallas kernels for 0% -> 0%
where the time goes in v4:
time: 337 us; the launch traced here: 336 us
  waiting for transfers between devices  235 us (70%)
  starting transfers between devices  38.6 us (11%)
  matrix products  22.9 us (7%)
  local copies, waits for them, and re-layouts  18.5 us (5%)
  between operations  13.6 us (4%)
  other arithmetic  7.46 us (2%)
    reduce_scatter x2, waiting for transfers between devices, body(): sums.append(lax.psum_scatter(part, 'rep', scatter_dimension=0, tiled=True))  91.2 us
    ppermute x1, waiting for transfers between devices, gather_integrals(): from_left = lax.ppermute(w, 'col', fwd)  42.9 us
    ppermute x1, waiting for transfers between devices, ring4_into(): from_left = lax.ppermute(block, axis, fwd)  42.6 us
    ppermute x1, waiting for transfers between devices, gather_amplitudes(): t_zh = lax.ppermute(t_part, 'row', [(i, i ^ 2) for i in range(nrow)])  25.9 us
    dot_general x8, matrix products, body(): jnp.einsum('gikca,gjkcb->giajb', w_blk, t_half[:, :, :, s * width:(s + 1)...  22.9 us
    ppermute x1, waiting for transfers between devices, gather_integrals(): opp_lo = lax.ppermute(from_left[:half], 'col', fwd)  20.9 us
    ppermute x1, starting transfers between devices, gather_amplitudes(): got = lax.ppermute(send, 'row', [(i, i ^ 1) for i in range(nrow)])  17 us
    ppermute x1, waiting for transfers between devices, ring4_into(): opp_lo = lax.ppermute(from_left[:half], axis, fwd)  9.02 us
  transfers between devices with their start and end apart: 13, of which 9 were waited for; matrix products, arithmetic and copies ran while one was open for 11% of the time, Pallas kernels for 0%

profile of v4, /device:TPU:1, one launch (start us, length us, event | category | flops | bytes accessed | tf_op | source)
XLA Modules:
  0.0 336.2 jit_solution(18081619983404953084)
XLA Ops:
  6.5 0.0 reduce-scatter.3.cloned.1.call-start
  6.5 7.7 %collective-permute-start = (bf16[8,4,15,8,128]{4,3,2,1,0:T(8,128)(2,1)}, bf16[8,4,15,8,128]{4,3,2,1,0:T(8,128)(2,1)S(1)}, u32[]{:S(2)}, u32[]{:S(2)}) collective-permute-start(bf16[8,4,15,8,128]{4,3,2,1,0:T(8,128)(2,1)} %param.5), channel_id=1, source_target_pairs={{0,32},{16,48},{32,0},{48,16},{64,96},{80,112},{96,64},{112,80},{1... | collective-permute-start | bytes 2949128 | tf_op jit(solution)/shard_map/ppermute | solution.py:40
  14.3 25.9 %collective-permute-done = bf16[8,4,15,8,128]{4,3,2,1,0:T(8,128)(2,1)S(1)} collective-permute-done((bf16[8,4,15,8,128]{4,3,2,1,0:T(8,128)(2,1)}, bf16[8,4,15,8,128]{4,3,2,1,0:T(8,128)(2,1)S(1)}, u32[]{:S(2)}, u32[]{:S(2)}) %collective-permute-start) | collective-permute-done | bytes 983072 | tf_op jit(solution)/shard_map/ppermute | solution.py:40
  40.1 2.2 maximum_select_fusion
  42.3 0.1 select_bitcast_fusion
  42.4 17.0 %collective-permute-start.1 = (bf16[8,2,15,16,128]{4,3,2,1,0:T(8,128)(2,1)S(1)}, bf16[8,2,15,16,128]{4,3,2,1,0:T(8,128)(2,1)S(1)}, u32[]{:S(2)}, u32[]{:S(2)}) collective-permute-start(bf16[8,2,15,16,128]{4,3,2,1,0:T(8,128)(2,1)S(1)} %get-tuple-element.6), channel_id=1, source_target_pairs={{0,16},{16,0},{32,48},{48,32},{64,80},{80,64},{96,112},{112,96},{1... | collective-permute-start | bytes 2949128 | tf_op jit(solution)/shard_map/ppermute | solution.py:46
  59.5 2.2 collective-permute-done.1
  61.7 0.6 maximum_select_fusion.1
  62.2 1.3 collective-permute-start.2
  63.5 1.5 collective-permute-start.4
  65.0 0.0 copy-done.7
  65.0 0.1 dynamic_slice.7
  65.1 42.6 %collective-permute-done.2 = bf16[8,2,15,32,128]{4,3,2,1,0:T(8,128)(2,1)} collective-permute-done((bf16[8,2,15,32,128]{4,3,2,1,0:T(8,128)(2,1)S(1)}, bf16[8,2,15,32,128]{4,3,2,1,0:T(8,128)(2,1)}, u32[]{:S(2)}, u32[]{:S(2)}) %collective-permute-start.2) | collective-permute-done | bytes 1966112 | tf_op jit(solution)/shard_map/ppermute | solution.py:18
  107.6 1.3 slice.60
  108.9 0.1 collective-permute-start.3
  109.0 0.0 collective-permute-done.4
  109.0 1.3 slice.61
  110.3 2.7 collective-permute-start.5
  113.0 0.0 copy-done.5
  113.0 0.1 select_reduce_fusion
  113.1 0.1 broadcast_compare_fusion
  113.2 5.2 %broadcast_in_dim.56 = bf16[8,2,15,128,128]{4,3,2,1,0:T(8,128)(2,1)} broadcast(bf16[]{:T(256)} %constant.87.clone.1), dimensions={} | broadcast | bytes 7864322 | tf_op jit(solution)/shard_map/broadcast_in_dim | solution.py:27
  118.4 1.6 constant_dynamic-update-slice_fusion.1
  120.0 3.2 constant_dynamic-update-slice_fusion
  123.3 9.0 %collective-permute-done.3 = bf16[4,2,15,32,128]{4,3,2,1,0:T(8,128)(2,1)S(1)} collective-permute-done((bf16[4,2,15,32,128]{4,3,2,1,0:T(8,128)(2,1)S(1)}, bf16[4,2,15,32,128]{4,3,2,1,0:T(8,128)(2,1)S(1)}, u32[]{:S(2)}, u32[]{:S(2)}) %collective-permute-start.3) | collective-permute-done | bytes 983072 | tf_op jit(solution)/shard_map/ppermute | solution.py:21
  132.3 0.3 collective-permute-done.5
  132.6 1.7 maximum_dynamic-update-slice_fusion
  134.3 3.4 %constant_dynamic-update-slice_fusion.2 = bf16[8,2,15,128,128]{4,3,2,1,0:T(8,128)(2,1)} fusion(bf16[8,2,15,128,128]{4,3,2,1,0:T(8,128)(2,1)} %maximum_dynamic-update-slice_fusion, bf16[8,2,15,32,128]{4,3,2,1,0:T(8,128)(2,1)} %collective-permute-done.4, s32[]{:T(128)S(6)} %select_n.130), kind=kLoop, calls=%fused_computation.46 | loop fusion | bytes 3932164 | tf_op jit(solution)/shard_map/dynamic_update_slice | solution.py:29
  137.7 2.4 collective-permute-start.10
  140.1 0.1 iota_compare_fusion.1
  140.1 0.8 broadcast_and_fusion
  140.9 0.0 copy-done.4
  140.9 0.2 broadcast_select_fusion
  141.1 1.3 collective-permute-start.7
  142.5 1.6 collective-permute-start.6
  144.0 42.9 %collective-permute-done.7 = bf16[8,2,15,32,128]{4,3,2,1,0:T(8,128)(2,1)S(1)} collective-permute-done((bf16[8,2,15,32,128]{4,3,2,1,0:T(8,128)(2,1)S(1)}, bf16[8,2,15,32,128]{4,3,2,1,0:T(8,128)(2,1)S(1)}, u32[]{:S(2)}, u32[]{:S(2)}) %collective-permute-start.7) | collective-permute-done | bytes 1966112 | tf_op jit(solution)/shard_map/ppermute | solution.py:63
  186.9 0.1 slice.64
  187.0 0.3 collective-permute-start.8
  187.3 0.0 collective-permute-done.6
  187.3 0.0 copy-start.2
  187.3 0.1 slice.65
  187.4 2.7 collective-permute-start.9
  190.1 20.9 %collective-permute-done.8 = bf16[4,2,15,32,128]{4,3,2,1,0:T(8,128)(2,1)S(1)} collective-permute-done((bf16[4,2,15,32,128]{4,3,2,1,0:T(8,128)(2,1)S(1)}, bf16[4,2,15,32,128]{4,3,2,1,0:T(8,128)(2,1)S(1)}, u32[]{:S(2)}, u32[]{:S(2)}) %collective-permute-start.8) | collective-permute-done | bytes 983072 | tf_op jit(solution)/shard_map/ppermute | solution.py:66
  211.0 0.0 collective-permute-done.9
  211.0 1.0 copy-done.6
  212.0 2.4 fusion.5
  214.4 2.4 fusion.7
  216.8 0.0 copy-done.2
  216.8 2.4 fusion.6
  219.2 3.9 %bitcast_add_fusion.3 = f32[8,2,128,2,128]{4,2,3,1,0:T(8,128)} fusion(f32[8,2,128,2,128,1]{4,2,5,3,1,0:T(8,128)S(1)} %fusion.5, f32[8,2,128,2,128,1]{4,2,5,3,1,0:T(8,128)S(1)} %fusion.6, f32[8,2,128,2,128,1]{4,2,5,3,1,0:T(8,128)S(1)} %fusion.7, bf16[8,2,15,128,128]{4,3,2,1,0:T(8,128)(2,1)} %constant_dynamic-update-slice_fusion.2, ...), kind=kOutput, calls=%fused_computation.3 | convolution fusion | flops 504889344 | bytes 12320768 | tf_op jit(solution)/shard_map/gikca,gjkcb->giajb/dot_general | solution.py:99
  223.1 0.0 reduce-scatter.3.cloned.1.call-update
  223.2 0.0 reduce-scatter.5.cloned.1.call-start
  223.2 0.0 collective-permute-done.10
  223.2 2.8 fusion.1
  226.1 2.4 fusion.2
  228.5 2.5 fusion.3
  231.1 4.0 %bitcast_add_fusion = f32[8,2,128,2,128]{4,2,3,1,0:T(8,128)} fusion(f32[8,2,128,2,128,1]{4,2,5,3,1,0:T(8,128)S(1)} %fusion.1, f32[8,2,128,2,128,1]{4,2,5,3,1,0:T(8,128)S(1)} %fusion.2, f32[8,2,128,2,128,1]{4,2,5,3,1,0:T(8,128)S(1)} %fusion.3, bf16[8,2,15,128,128]{4,3,2,1,0:T(8,128)(2,1)} %collective-permute-done.10, bf16[8,2,15,32,128]{4,3,2,1,0:T(8,128)(2,1)S(1)} %copy-done.1), kind=kOutput, calls=%fused_computation | convolution fusion | flops 504889344 | bytes 12320768 | tf_op jit(solution)/shard_map/gikca,gjkcb->giajb/dot_general | solution.py:99
  235.1 0.0 reduce-scatter.5.cloned.1.call-update
  235.1 0.1 dynamic_slice.6
  235.2 0.1 iota_compare_fusion.2
  235.2 40.3 %reduce-scatter.3.cloned.1.call-done = f32[2,2,128,2,128]{4,2,3,1,0:T(8,128)} async-done(((f32[8,2,128,2,128]{4,2,3,1,0:T(8,128)}), f32[2,2,128,2,128]{4,2,3,1,0:T(8,128)}) %reduce-scatter.3.cloned.1.call-update) | async-done | bytes 524304 | tf_op jit(solution)/shard_map/reduce_scatter | solution.py:106
  275.6 50.9 %reduce-scatter.5.cloned.1.call-done = f32[2,2,128,2,128]{4,2,3,1,0:T(8,128)} async-done(((f32[8,2,128,2,128]{4,2,3,1,0:T(8,128)}), f32[2,2,128,2,128]{4,2,3,1,0:T(8,128)}) %reduce-scatter.5.cloned.1.call-update) | async-done | bytes 524304 | tf_op jit(solution)/shard_map/reduce_scatter | solution.py:106
  326.5 1.7 fusion.19
  328.2 1.2 copy.14
  (12 shorter events, 0.0 us)
Async XLA Ops:
  6.5 269.0 %reduce-scatter.3.cloned.1.call-start = ((), (), s32[]{:S(2)}) async-start(), calls=%async_computation.2 | async-start | bytes 2621440 | tf_op jit(solution)/shard_map/reduce_scatter | solution.py:106
  6.5 33.6 %collective-permute-start = (bf16[8,4,15,8,128]{4,3,2,1,0:T(8,128)(2,1)}, bf16[8,4,15,8,128]{4,3,2,1,0:T(8,128)(2,1)S(1)}, u32[]{:S(2)}, u32[]{:S(2)}) collective-permute-start(bf16[8,4,15,8,128]{4,3,2,1,0:T(8,128)(2,1)} %param.5), channel_id=1, source_target_pairs={{0,32},{16,48},{32,0},{48,16},{64,96},{80,112},{96,64},{112,80},{1... | collective-permute-start | bytes 2949128 | tf_op jit(solution)/shard_map/ppermute | solution.py:40
  42.4 19.2 %collective-permute-start.1 = (bf16[8,2,15,16,128]{4,3,2,1,0:T(8,128)(2,1)S(1)}, bf16[8,2,15,16,128]{4,3,2,1,0:T(8,128)(2,1)S(1)}, u32[]{:S(2)}, u32[]{:S(2)}) collective-permute-start(bf16[8,2,15,16,128]{4,3,2,1,0:T(8,128)(2,1)S(1)} %get-tuple-element.6), channel_id=1, source_target_pairs={{0,16},{16,0},{32,48},{48,32},{64,80},{80,64},{96,112},{112,96},{1... | collective-permute-start | bytes 2949128 | tf_op jit(solution)/shard_map/ppermute | solution.py:46
  61.7 3.3 copy-start.7
  62.2 45.4 %collective-permute-start.2 = (bf16[8,2,15,32,128]{4,3,2,1,0:T(8,128)(2,1)S(1)}, bf16[8,2,15,32,128]{4,3,2,1,0:T(8,128)(2,1)}, u32[]{:S(2)}, u32[]{:S(2)}) collective-permute-start(bf16[8,2,15,32,128]{4,3,2,1,0:T(8,128)(2,1)S(1)} %bitcast.117), channel_id=1, source_target_pairs={{0,64},{16,80},{32,96},{48,112},{64,128},{80,144},{96,160},{112,17... | collective-permute-start | bytes 5898248 | tf_op jit(solution)/shard_map/ppermute | solution.py:18
  63.5 45.5 %collective-permute-start.4 = (bf16[8,2,15,32,128]{4,3,2,1,0:T(8,128)(2,1)S(1)}, bf16[8,2,15,32,128]{4,3,2,1,0:T(8,128)(2,1)}, u32[]{:S(2)}, u32[]{:S(2)}) collective-permute-start(bf16[8,2,15,32,128]{4,3,2,1,0:T(8,128)(2,1)S(1)} %bitcast.118), channel_id=1, source_target_pairs={{0,192},{16,208},{32,224},{48,240},{64,0},{80,16},{96,32},{112,48}... | collective-permute-start | bytes 5898248 | tf_op jit(solution)/shard_map/ppermute | solution.py:19
  65.1 48.0 %copy-start.5 = (s32[8]{0:T(128)S(1)}, s32[8]{0:T(128)}, u32[]{:S(2)}) copy-start(s32[8]{0:T(128)} %param.6) | copy-start | bytes 100
  108.9 23.4 %collective-permute-start.3 = (bf16[4,2,15,32,128]{4,3,2,1,0:T(8,128)(2,1)S(1)}, bf16[4,2,15,32,128]{4,3,2,1,0:T(8,128)(2,1)S(1)}, u32[]{:S(2)}, u32[]{:S(2)}) collective-permute-start(bf16[4,2,15,32,128]{4,3,2,1,0:T(8,128)(2,1)S(1)} %slice.60), channel_id=1, source_target_pairs={{0,64},{16,80},{32,96},{48,112},{64,128},{80,144},{96,160},{112,17... | collective-permute-start | bytes 2949128 | tf_op jit(solution)/shard_map/ppermute | solution.py:21
  110.3 22.3 %collective-permute-start.5 = (bf16[4,2,15,32,128]{4,3,2,1,0:T(8,128)(2,1)S(1)}, bf16[4,2,15,32,128]{4,3,2,1,0:T(8,128)(2,1)S(1)}, u32[]{:S(2)}, u32[]{:S(2)}) collective-permute-start(bf16[4,2,15,32,128]{4,3,2,1,0:T(8,128)(2,1)S(1)} %slice.61), channel_id=1, source_target_pairs={{0,192},{16,208},{32,224},{48,240},{64,0},{80,16},{96,32},{112,48}... | collective-permute-start | bytes 2949128 | tf_op jit(solution)/shard_map/ppermute | solution.py:22
  134.3 6.6 %copy-start.4 = (bf16[8,2,15,32,128]{4,3,2,1,0:T(8,128)(2,1)S(1)}, bf16[8,2,15,32,128]{4,3,2,1,0:T(8,128)(2,1)}, u32[]{:S(2)}) copy-start(bf16[8,2,15,32,128]{4,3,2,1,0:T(8,128)(2,1)} %param.4) | copy-start | bytes 5898244
  137.7 85.5 %collective-permute-start.10 = (bf16[8,2,15,128,128]{4,3,2,1,0:T(8,128)(2,1)}, bf16[8,2,15,128,128]{4,3,2,1,0:T(8,128)(2,1)}, u32[]{:S(2)}, u32[]{:S(2)}) collective-permute-start(bf16[8,2,15,128,128]{4,3,2,1,0:T(8,128)(2,1)} %constant_dynamic-update-slice_fusion.2), channel_id=1, source_target_pairs={{0,16},{16,0},{32,48},{48,32},{64,80},{80,64},{96,112},{112,96},{1... | collective-permute-start | bytes 23592968 | tf_op jit(solution)/shard_map/ppermute | solution.py:54
  141.1 45.8 %collective-permute-start.7 = (bf16[8,2,15,32,128]{4,3,2,1,0:T(8,128)(2,1)S(1)}, bf16[8,2,15,32,128]{4,3,2,1,0:T(8,128)(2,1)S(1)}, u32[]{:S(2)}, u32[]{:S(2)}) collective-permute-start(bf16[8,2,15,32,128]{4,3,2,1,0:T(8,128)(2,1)S(1)} %broadcast_select_fusion), channel_id=1, source_target_pairs={{0,4},{4,8},{8,12},{12,0},{1,5},{5,9},{9,13},{13,1},{2,6},{6,10},{... | collective-permute-start | bytes 5898248 | tf_op jit(solution)/shard_map/ppermute | solution.py:63
  142.5 44.8 %collective-permute-start.6 = (bf16[8,2,15,32,128]{4,3,2,1,0:T(8,128)(2,1)S(1)}, bf16[8,2,15,32,128]{4,3,2,1,0:T(8,128)(2,1)S(1)}, u32[]{:S(2)}, u32[]{:S(2)}) collective-permute-start(bf16[8,2,15,32,128]{4,3,2,1,0:T(8,128)(2,1)S(1)} %broadcast_select_fusion), channel_id=1, source_target_pairs={{0,12},{4,0},{8,4},{12,8},{1,13},{5,1},{9,5},{13,9},{2,14},{6,2},{... | collective-permute-start | bytes 5898248 | tf_op jit(solution)/shard_map/ppermute | solution.py:64
  186.9 32.3 %copy-start = (bf16[8,2,15,32,128]{4,3,2,1,0:T(8,128)(2,1)}, bf16[8,2,15,32,128]{4,3,2,1,0:T(8,128)(2,1)S(1)}, u32[]{:S(2)}) copy-start(bf16[8,2,15,32,128]{4,3,2,1,0:T(8,128)(2,1)S(1)} %collective-permute-done.7) | copy-start | bytes 5898244
  187.0 24.0 %collective-permute-start.8 = (bf16[4,2,15,32,128]{4,3,2,1,0:T(8,128)(2,1)S(1)}, bf16[4,2,15,32,128]{4,3,2,1,0:T(8,128)(2,1)S(1)}, u32[]{:S(2)}, u32[]{:S(2)}) collective-permute-start(bf16[4,2,15,32,128]{4,3,2,1,0:T(8,128)(2,1)S(1)} %slice.64), channel_id=1, source_target_pairs={{0,4},{4,8},{8,12},{12,0},{1,5},{5,9},{9,13},{13,1},{2,6},{6,10},{... | collective-permute-start | bytes 2949128 | tf_op jit(solution)/shard_map/ppermute | solution.py:66
  187.3 29.5 %copy-start.2 = (bf16[8,2,15,32,128]{4,3,2,1,0:T(8,128)(2,1)}, bf16[8,2,15,32,128]{4,3,2,1,0:T(8,128)(2,1)S(1)}, u32[]{:S(2)}) copy-start(bf16[8,2,15,32,128]{4,3,2,1,0:T(8,128)(2,1)S(1)} %collective-permute-done.6) | copy-start | bytes 5898244
  187.4 23.6 %collective-permute-start.9 = (bf16[4,2,15,32,128]{4,3,2,1,0:T(8,128)(2,1)S(1)}, bf16[4,2,15,32,128]{4,3,2,1,0:T(8,128)(2,1)S(1)}, u32[]{:S(2)}, u32[]{:S(2)}) collective-permute-start(bf16[4,2,15,32,128]{4,3,2,1,0:T(8,128)(2,1)S(1)} %slice.65), channel_id=1, source_target_pairs={{0,12},{4,0},{8,4},{12,8},{1,13},{5,1},{9,5},{13,9},{2,14},{6,2},{... | collective-permute-start | bytes 2949128 | tf_op jit(solution)/shard_map/ppermute | solution.py:67
  211.0 1.0 copy-start.6
  223.2 103.3 %reduce-scatter.5.cloned.1.call-start = ((), (), s32[]{:S(2)}) async-start(), calls=%async_computation.3 | async-start | bytes 2621440 | tf_op jit(solution)/shard_map/reduce_scatter | solution.py:106
  223.2 2.9 copy-start.3
  228.5 2.5 copy-start.1
Sparse Core Ops, SparseCore 0:
  223.3 52.2 reduce-scatter.2
  278.1 48.3 reduce-scatter.4

commit v5 on v4

--- a/solution.py
+++ b/solution.py
@@ -12,7 +12,7 @@
     return pairs
 
 
-def ring4_into(block, axis, n, period, pos, out_axis):
+def ring4_pieces(block, axis, n, period):
     fwd = shift_perm(n, 1, period)
     bwd = shift_perm(n, -1, period)
     from_left = lax.ppermute(block, axis, fwd)
@@ -20,14 +20,17 @@
     half = block.shape[0] // 2
     opp_lo = lax.ppermute(from_left[:half], axis, fwd)
     opp_hi = lax.ppermute(from_right[half:], axis, bwd)
-    width = block.shape[out_axis]
-    shape = list(block.shape)
-    shape[out_axis] = 4 * width
     opp = jnp.concatenate([opp_lo, opp_hi], axis=0)
-    out = jnp.zeros(shape, block.dtype)
-    for step, piece in enumerate([block, from_left, opp, from_right]):
-        out = lax.dynamic_update_slice_in_dim(out, piece, ((pos - step) % 4) * width, axis=out_axis)
-    return out
+    return [block, from_left, opp, from_right]
+
+
+def core_quad(part, core, nrow, hj):
+    keep = jnp.where(core == 0, part[:, :hj], part[:, hj:])
+    send = jnp.where(core == 0, part[:, hj:], part[:, :hj])
+    got = lax.ppermute(send, "row", [(i, i ^ 1) for i in range(nrow)])
+    return jnp.where(
+        core == 0, jnp.concatenate([keep, got], axis=3), jnp.concatenate([got, keep], axis=3)
+    )
 
 
 def gather_amplitudes(t_part, cl):
@@ -36,21 +39,21 @@
     x = r // 4
     zh = (r // 2) % 2
     core = r % 2
-    hj = t_part.shape[1] // 2
+    ng, nj, nk, ncc, nb = t_part.shape
+    hj = nj // 2
     t_zh = lax.ppermute(t_part, "row", [(i, i ^ 2) for i in range(nrow)])
-    pair = jnp.where(
-        zh == 0, jnp.concatenate([t_part, t_zh], axis=3), jnp.concatenate([t_zh, t_part], axis=3)
-    )
-    keep = jnp.where(core == 0, pair[:, :hj], pair[:, hj:])
-    send = jnp.where(core == 0, pair[:, hj:], pair[:, :hj])
-    got = lax.ppermute(send, "row", [(i, i ^ 1) for i in range(nrow)])
-    ng, nh, nk, nzc, nb = keep.shape
-    keep5 = keep.reshape(ng, nh, nk, 2, nzc // 2, nb)
-    got5 = got.reshape(ng, nh, nk, 2, nzc // 2, nb)
-    quad = jnp.where(
-        core == 0, jnp.stack([keep5, got5], axis=4), jnp.stack([got5, keep5], axis=4)
-    ).reshape(ng, nh, nk, 2 * nzc, nb)
-    mine = ring4_into(quad, "row", nrow, 4, x - cl, 3)
+    own = ring4_pieces(core_quad(t_part, core, nrow, hj), "row", nrow, 4)
+    pos = x - cl
+    mine = jnp.zeros((ng, hj, nk, 16 * ncc, nb), t_part.dtype)
+    for step, piece in enumerate(own):
+        mine = lax.dynamic_update_slice_in_dim(
+            mine, piece, ((pos - step) % 4) * 4 * ncc + zh * 2 * ncc, axis=3
+        )
+    far = ring4_pieces(core_quad(t_zh, core, nrow, hj), "row", nrow, 4)
+    for step, piece in enumerate(far):
+        mine = lax.dynamic_update_slice_in_dim(
+            mine, piece, ((pos - step) % 4) * 4 * ncc + (1 - zh) * 2 * ncc, axis=3
+        )
     other = lax.ppermute(mine, "row", [(i, i ^ 1) for i in range(nrow)])
     return mine, other
 

time: 337 us -> 314 us (0.932)
  waiting for transfers between devices: 235 us -> 208 us
  local copies, waits for them, and re-layouts: 18.5 us -> 13.1 us
  other arithmetic: 7.46 us -> 12.6 us
  starting transfers between devices: 38.6 us -> 43.2 us
    ppermute x1, waiting for transfers between devices: 25.9 us -> 5.87 us  [gather_amplitudes(): t_zh = lax.ppermute(t_part, 'row', [(i, i ^ 2) for i in range(nrow)])]
    ppermute x5 -> x10, starting transfers between devices: 22.6 us -> 30.2 us  [the longest x2 17.4 us: ring4_pieces(): from_right = lax.ppermute(block, axis, bwd)]
    dynamic_update_slice x1 -> x4, other arithmetic: 1.68 us -> 7.59 us  [gather_amplitudes(): lax.dynamic_update_slice_in_dim(mine, piece, (pos - step) % 4 * 4 * ncc +...]
    ppermute x5 -> x10, waiting for transfers between devices: 54.1 us -> 50.1 us  [the longest x2 21 us: ring4_pieces(): from_right = lax.ppermute(block, axis, bwd)]
    dynamic_update_slice x3 -> x4, local copies, waits for them, and re-layouts: 8.28 us -> 4.82 us  [gather_amplitudes(): lax.dynamic_update_slice_in_dim(mine, piece, (pos - step) % 4 * 4 * ncc +...]
  transfers between devices with their start and end apart: 13 -> 18, of which waited for: 9 -> 10; matrix products, arithmetic and copies ran while one was open for 11% -> 11% of each run, Pallas kernels for 0% -> 0%
where the time goes in v5:
time: 314 us
  waiting for transfers between devices  208 us (66%)
  starting transfers between devices  43.2 us (14%)
  matrix products  23.2 us (7%)
  between operations  13.7 us (4%)
  local copies, waits for them, and re-layouts  13.1 us (4%)
  other arithmetic  12.6 us (4%)
    reduce_scatter x2, waiting for transfers between devices, body(): sums.append(lax.psum_scatter(part, 'rep', scatter_dimension=0, tiled=True))  88.2 us
    ppermute x1, waiting for transfers between devices, gather_integrals(): from_left = lax.ppermute(w, 'col', fwd)  42.9 us
    dot_general x8, matrix products, body(): jnp.einsum('gikca,gjkcb->giajb', w_blk, t_half[:, :, :, s * width:(s + 1)...  23.2 us
    ppermute x2, waiting for transfers between devices, ring4_pieces(): from_right = lax.ppermute(block, axis, bwd)  21 us
    ppermute x1, waiting for transfers between devices, gather_integrals(): opp_lo = lax.ppermute(from_left[:half], 'col', fwd)  20.9 us
    ppermute x2, starting transfers between devices, ring4_pieces(): from_right = lax.ppermute(block, axis, bwd)  17.4 us
    ppermute x2, waiting for transfers between devices, ring4_pieces(): from_left = lax.ppermute(block, axis, fwd)  16.2 us
    ppermute x2, waiting for transfers between devices, ring4_pieces(): opp_hi = lax.ppermute(from_right[half:], axis, bwd)  8.45 us
  transfers between devices with their start and end apart: 18, of which 10 were waited for; matrix products, arithmetic and copies ran while one was open for 11% of the time, Pallas kernels for 0%

profile of v5, /device:TPU:1, one launch (start us, length us, event | category | flops | bytes accessed | tf_op | source)
XLA Modules:
  0.0 313.9 jit_solution(15631002456422503922)
XLA Ops:
  6.5 1.2 broadcast_select_fusion.3
  7.8 3.3 %collective-permute-start = (bf16[8,2,15,8,128]{4,3,2,1,0:T(8,128)(2,1)S(1)}, bf16[8,2,15,8,128]{4,3,2,1,0:T(8,128)(2,1)S(1)}, u32[]{:S(2)}, u32[]{:S(2)}) collective-permute-start(bf16[8,2,15,8,128]{4,3,2,1,0:T(8,128)(2,1)S(1)} %get-tuple-element.11), channel_id=1, source_target_pairs={{0,16},{16,0},{32,48},{48,32},{64,80},{80,64},{96,112},{112,96},{1... | collective-permute-start | bytes 1474568 | tf_op jit(solution)/shard_map/ppermute | solution.py:30
  11.1 1.5 collective-permute-done
  12.6 5.1 %broadcast_in_dim.56 = bf16[8,2,15,128,128]{4,3,2,1,0:T(8,128)(2,1)} broadcast(bf16[]{:T(256)} %constant.101.clone.1), dimensions={} | broadcast | bytes 7864322 | tf_op jit(solution)/shard_map/broadcast_in_dim | solution.py:47
  17.7 1.5 constant_dynamic-update-slice_fusion.4
  19.2 2.7 collective-permute-start.3
  21.8 5.2 %collective-permute-start.5 = (bf16[8,4,15,8,128]{4,3,2,1,0:T(8,128)(2,1)S(1)}, bf16[8,4,15,8,128]{4,3,2,1,0:T(8,128)(2,1)S(1)}, u32[]{:S(2)}, u32[]{:S(2)}) collective-permute-start(bf16[8,4,15,8,128]{4,3,2,1,0:T(8,128)(2,1)S(1)} %copy-done.5), channel_id=1, source_target_pairs={{0,32},{16,48},{32,0},{48,16},{64,96},{80,112},{96,64},{112,80},{1... | collective-permute-start | bytes 2949128 | tf_op jit(solution)/shard_map/ppermute | solution.py:44
  27.1 16.2 %collective-permute-done.1 = bf16[8,2,15,16,128]{4,3,2,1,0:T(8,128)(2,1)S(1)} collective-permute-done((bf16[8,2,15,16,128]{4,3,2,1,0:T(8,128)(2,1)S(1)}, bf16[8,2,15,16,128]{4,3,2,1,0:T(8,128)(2,1)S(1)}, u32[]{:S(2)}, u32[]{:S(2)}) %collective-permute-start.1) | collective-permute-done | bytes 983072 | tf_op jit(solution)/shard_map/ppermute | solution.py:18
  43.4 0.1 collective-permute-start.2
  43.4 0.0 collective-permute-done.3
  43.5 0.8 slice.77
  44.3 2.7 collective-permute-start.4
  46.9 5.9 %collective-permute-done.5 = bf16[8,4,15,8,128]{4,3,2,1,0:T(8,128)(2,1)S(1)} collective-permute-done((bf16[8,4,15,8,128]{4,3,2,1,0:T(8,128)(2,1)S(1)}, bf16[8,4,15,8,128]{4,3,2,1,0:T(8,128)(2,1)S(1)}, u32[]{:S(2)}, u32[]{:S(2)}) %collective-permute-start.5) | collective-permute-done | bytes 983072 | tf_op jit(solution)/shard_map/ppermute | solution.py:44
  52.8 0.8 broadcast_select_fusion.1
  53.6 3.3 %collective-permute-start.6 = (bf16[8,2,15,8,128]{4,3,2,1,0:T(8,128)(2,1)}, bf16[8,2,15,8,128]{4,3,2,1,0:T(8,128)(2,1)}, u32[]{:S(2)}, u32[]{:S(2)}) collective-permute-start(bf16[8,2,15,8,128]{4,3,2,1,0:T(8,128)(2,1)} %get-tuple-element.9), channel_id=1, source_target_pairs={{0,16},{16,0},{32,48},{48,32},{64,80},{80,64},{96,112},{112,96},{1... | collective-permute-start | bytes 1474568 | tf_op jit(solution)/shard_map/ppermute | solution.py:30
  56.9 1.2 constant_dynamic-update-slice_fusion.3
  58.1 0.0 collective-permute-done.2
  58.1 2.3 maximum_dynamic-update-slice_fusion
  60.4 1.2 constant_dynamic-update-slice_fusion.2
  61.6 0.0 collective-permute-done.6
  61.6 2.7 constant_dynamic-update-slice_fusion.1
  64.3 14.7 %collective-permute-start.9 = (bf16[8,2,15,16,128]{4,3,2,1,0:T(8,128)(2,1)S(1)}, bf16[8,2,15,16,128]{4,3,2,1,0:T(8,128)(2,1)S(1)}, u32[]{:S(2)}, u32[]{:S(2)}) collective-permute-start(bf16[8,2,15,16,128]{4,3,2,1,0:T(8,128)(2,1)S(1)} %get-tuple-element.6), channel_id=1, source_target_pairs={{0,192},{16,208},{32,224},{48,240},{64,0},{80,16},{96,32},{112,48}... | collective-permute-start | bytes 2949128 | tf_op jit(solution)/shard_map/ppermute | solution.py:19
  79.0 0.0 collective-permute-start.7
  79.1 0.1 dynamic_slice.7
  79.1 21.0 %collective-permute-done.9 = bf16[8,2,15,16,128]{4,3,2,1,0:T(8,128)(2,1)S(1)} collective-permute-done((bf16[8,2,15,16,128]{4,3,2,1,0:T(8,128)(2,1)S(1)}, bf16[8,2,15,16,128]{4,3,2,1,0:T(8,128)(2,1)S(1)}, u32[]{:S(2)}, u32[]{:S(2)}) %collective-permute-start.9) | collective-permute-done | bytes 983072 | tf_op jit(solution)/shard_map/ppermute | solution.py:19
  100.2 0.8 slice.81
  101.0 3.4 %collective-permute-start.10 = (bf16[4,2,15,16,128]{4,3,2,1,0:T(8,128)(2,1)}, bf16[4,2,15,16,128]{4,3,2,1,0:T(8,128)(2,1)S(1)}, u32[]{:S(2)}, u32[]{:S(2)}) collective-permute-start(bf16[4,2,15,16,128]{4,3,2,1,0:T(8,128)(2,1)} %slice.81), channel_id=1, source_target_pairs={{0,192},{16,208},{32,224},{48,240},{64,0},{80,16},{96,32},{112,48}... | collective-permute-start | bytes 1474568 | tf_op jit(solution)/shard_map/ppermute | solution.py:22
  104.4 0.1 collective-permute-start.8
  104.6 0.1 select_reduce_fusion
  104.6 0.1 broadcast_compare_fusion
  104.7 1.2 constant_dynamic-update-slice_fusion
  106.0 8.4 %collective-permute-done.10 = bf16[4,2,15,16,128]{4,3,2,1,0:T(8,128)(2,1)S(1)} collective-permute-done((bf16[4,2,15,16,128]{4,3,2,1,0:T(8,128)(2,1)}, bf16[4,2,15,16,128]{4,3,2,1,0:T(8,128)(2,1)S(1)}, u32[]{:S(2)}, u32[]{:S(2)}) %collective-permute-start.10) | collective-permute-done | bytes 491552 | tf_op jit(solution)/shard_map/ppermute | solution.py:22
  114.4 2.9 collective-permute-done.8
  117.3 1.2 maximum_dynamic-update-slice_fusion.1
  118.5 1.2 constant_dynamic-update-slice_fusion.5
  119.7 2.0 collective-permute-start.15
  121.7 0.1 iota_compare_fusion.1
  121.8 0.8 broadcast_and_fusion
  122.5 0.2 broadcast_select_fusion
  122.7 1.4 collective-permute-start.12
  124.1 1.6 collective-permute-start.11
  125.7 42.9 %collective-permute-done.12 = bf16[8,2,15,32,128]{4,3,2,1,0:T(8,128)(2,1)S(1)} collective-permute-done((bf16[8,2,15,32,128]{4,3,2,1,0:T(8,128)(2,1)S(1)}, bf16[8,2,15,32,128]{4,3,2,1,0:T(8,128)(2,1)S(1)}, u32[]{:S(2)}, u32[]{:S(2)}) %collective-permute-start.12) | collective-permute-done | bytes 1966112 | tf_op jit(solution)/shard_map/ppermute | solution.py:66
  168.6 0.1 slice.84
  168.6 0.1 collective-permute-start.13
  168.7 0.1 slice.85
  168.8 2.7 collective-permute-start.14
  171.5 20.9 %collective-permute-done.13 = bf16[4,2,15,32,128]{4,3,2,1,0:T(8,128)(2,1)S(1)} collective-permute-done((bf16[4,2,15,32,128]{4,3,2,1,0:T(8,128)(2,1)S(1)}, bf16[4,2,15,32,128]{4,3,2,1,0:T(8,128)(2,1)S(1)}, u32[]{:S(2)}, u32[]{:S(2)}) %collective-permute-start.13) | collective-permute-done | bytes 983072 | tf_op jit(solution)/shard_map/ppermute | solution.py:69
  192.5 2.7 fusion.5
  195.2 2.4 fusion.7
  197.6 2.4 fusion.6
  200.0 3.9 %bitcast_add_fusion.3 = f32[8,2,128,2,128]{4,2,3,1,0:T(8,128)} fusion(f32[8,2,128,2,128,1]{4,2,5,3,1,0:T(8,128)S(1)} %fusion.5, f32[8,2,128,2,128,1]{4,2,5,3,1,0:T(8,128)S(1)} %fusion.6, f32[8,2,128,2,128,1]{4,2,5,3,1,0:T(8,128)S(1)} %fusion.7, bf16[8,2,15,128,128]{4,3,2,1,0:T(8,128)(2,1)} %constant_dynamic-update-slice_fusion.5, ...), kind=kOutput, calls=%fused_computation.3 | convolution fusion | flops 504889344 | bytes 12320768 | tf_op jit(solution)/shard_map/gikca,gjkcb->giajb/dot_general | solution.py:102
  203.9 0.0 reduce-scatter.3.cloned.1.call-update
  204.0 0.0 reduce-scatter.5.cloned.1.call-start
  204.0 2.8 fusion.1
  206.9 2.4 fusion.2
  209.3 2.5 fusion.3
  211.8 4.0 %bitcast_add_fusion = f32[8,2,128,2,128]{4,2,3,1,0:T(8,128)} fusion(f32[8,2,128,2,128,1]{4,2,5,3,1,0:T(8,128)S(1)} %fusion.1, f32[8,2,128,2,128,1]{4,2,5,3,1,0:T(8,128)S(1)} %fusion.2, f32[8,2,128,2,128,1]{4,2,5,3,1,0:T(8,128)S(1)} %fusion.3, bf16[8,2,15,128,128]{4,3,2,1,0:T(8,128)(2,1)} %collective-permute-done.15, bf16[8,2,15,32,128]{4,3,2,1,0:T(8,128)(2,1)S(1)} %copy-done.1), kind=kOutput, calls=%fused_computation | convolution fusion | flops 504889344 | bytes 12320768 | tf_op jit(solution)/shard_map/gikca,gjkcb->giajb/dot_general | solution.py:102
  215.8 0.0 reduce-scatter.5.cloned.1.call-update
  215.8 0.1 dynamic_slice.6
  215.9 0.1 iota_compare_fusion.2
  216.0 37.3 %reduce-scatter.3.cloned.1.call-done = f32[2,2,128,2,128]{4,2,3,1,0:T(8,128)} async-done(((f32[8,2,128,2,128]{4,2,3,1,0:T(8,128)}), f32[2,2,128,2,128]{4,2,3,1,0:T(8,128)}) %reduce-scatter.3.cloned.1.call-update) | async-done | bytes 524304 | tf_op jit(solution)/shard_map/reduce_scatter | solution.py:109
  253.3 50.9 %reduce-scatter.5.cloned.1.call-done = f32[2,2,128,2,128]{4,2,3,1,0:T(8,128)} async-done(((f32[8,2,128,2,128]{4,2,3,1,0:T(8,128)}), f32[2,2,128,2,128]{4,2,3,1,0:T(8,128)}) %reduce-scatter.5.cloned.1.call-update) | async-done | bytes 524304 | tf_op jit(solution)/shard_map/reduce_scatter | solution.py:109
  304.2 1.7 fusion.19
  305.9 1.2 copy.6
  (27 shorter events, 0.1 us)
Async XLA Ops:
  6.5 246.7 %reduce-scatter.3.cloned.1.call-start = ((), (), s32[]{:S(2)}) async-start(), calls=%async_computation.2 | async-start | bytes 2621440 | tf_op jit(solution)/shard_map/reduce_scatter | solution.py:109
  7.8 4.8 %collective-permute-start = (bf16[8,2,15,8,128]{4,3,2,1,0:T(8,128)(2,1)S(1)}, bf16[8,2,15,8,128]{4,3,2,1,0:T(8,128)(2,1)S(1)}, u32[]{:S(2)}, u32[]{:S(2)}) collective-permute-start(bf16[8,2,15,8,128]{4,3,2,1,0:T(8,128)(2,1)S(1)} %get-tuple-element.11), channel_id=1, source_target_pairs={{0,16},{16,0},{32,48},{48,32},{64,80},{80,64},{96,112},{112,96},{1... | collective-permute-start | bytes 1474568 | tf_op jit(solution)/shard_map/ppermute | solution.py:30
  17.7 4.2 %copy-start.5 = (bf16[8,4,15,8,128]{4,3,2,1,0:T(8,128)(2,1)S(1)}, bf16[8,4,15,8,128]{4,3,2,1,0:T(8,128)(2,1)}, u32[]{:S(2)}) copy-start(bf16[8,4,15,8,128]{4,3,2,1,0:T(8,128)(2,1)} %param.5) | copy-start | bytes 2949124
  19.2 24.2 %collective-permute-start.1 = (bf16[8,2,15,16,128]{4,3,2,1,0:T(8,128)(2,1)S(1)}, bf16[8,2,15,16,128]{4,3,2,1,0:T(8,128)(2,1)S(1)}, u32[]{:S(2)}, u32[]{:S(2)}) collective-permute-start(bf16[8,2,15,16,128]{4,3,2,1,0:T(8,128)(2,1)S(1)} %get-tuple-element.8), channel_id=1, source_target_pairs={{0,64},{16,80},{32,96},{48,112},{64,128},{80,144},{96,160},{112,17... | collective-permute-start | bytes 2949128 | tf_op jit(solution)/shard_map/ppermute | solution.py:18
  19.2 24.3 %collective-permute-start.3 = (bf16[8,2,15,16,128]{4,3,2,1,0:T(8,128)(2,1)S(1)}, bf16[8,2,15,16,128]{4,3,2,1,0:T(8,128)(2,1)S(1)}, u32[]{:S(2)}, u32[]{:S(2)}) collective-permute-start(bf16[8,2,15,16,128]{4,3,2,1,0:T(8,128)(2,1)S(1)} %get-tuple-element.8), channel_id=1, source_target_pairs={{0,192},{16,208},{32,224},{48,240},{64,0},{80,16},{96,32},{112,48}... | collective-permute-start | bytes 2949128 | tf_op jit(solution)/shard_map/ppermute | solution.py:19
  21.8 30.9 %collective-permute-start.5 = (bf16[8,4,15,8,128]{4,3,2,1,0:T(8,128)(2,1)S(1)}, bf16[8,4,15,8,128]{4,3,2,1,0:T(8,128)(2,1)S(1)}, u32[]{:S(2)}, u32[]{:S(2)}) collective-permute-start(bf16[8,4,15,8,128]{4,3,2,1,0:T(8,128)(2,1)S(1)} %copy-done.5), channel_id=1, source_target_pairs={{0,32},{16,48},{32,0},{48,16},{64,96},{80,112},{96,64},{112,80},{1... | collective-permute-start | bytes 2949128 | tf_op jit(solution)/shard_map/ppermute | solution.py:44
  43.4 14.7 %collective-permute-start.2 = (bf16[4,2,15,16,128]{4,3,2,1,0:T(8,128)(2,1)S(1)}, bf16[4,2,15,16,128]{4,3,2,1,0:T(8,128)(2,1)S(1)}, u32[]{:S(2)}, u32[]{:S(2)}) collective-permute-start(bf16[4,2,15,16,128]{4,3,2,1,0:T(8,128)(2,1)S(1)} %slice.76), channel_id=1, source_target_pairs={{0,64},{16,80},{32,96},{48,112},{64,128},{80,144},{96,160},{112,17... | collective-permute-start | bytes 1474568 | tf_op jit(solution)/shard_map/ppermute | solution.py:21
  44.3 13.8 %collective-permute-start.4 = (bf16[4,2,15,16,128]{4,3,2,1,0:T(8,128)(2,1)}, bf16[4,2,15,16,128]{4,3,2,1,0:T(8,128)(2,1)}, u32[]{:S(2)}, u32[]{:S(2)}) collective-permute-start(bf16[4,2,15,16,128]{4,3,2,1,0:T(8,128)(2,1)} %slice.77), channel_id=1, source_target_pairs={{0,192},{16,208},{32,224},{48,240},{64,0},{80,16},{96,32},{112,48}... | collective-permute-start | bytes 1474568 | tf_op jit(solution)/shard_map/ppermute | solution.py:22
  53.6 8.0 %collective-permute-start.6 = (bf16[8,2,15,8,128]{4,3,2,1,0:T(8,128)(2,1)}, bf16[8,2,15,8,128]{4,3,2,1,0:T(8,128)(2,1)}, u32[]{:S(2)}, u32[]{:S(2)}) collective-permute-start(bf16[8,2,15,8,128]{4,3,2,1,0:T(8,128)(2,1)} %get-tuple-element.9), channel_id=1, source_target_pairs={{0,16},{16,0},{32,48},{48,32},{64,80},{80,64},{96,112},{112,96},{1... | collective-permute-start | bytes 1474568 | tf_op jit(solution)/shard_map/ppermute | solution.py:30
  60.4 18.7 %copy-start.7 = (s32[60]{0:T(128)S(1)}, s32[60]{0:T(128)}, u32[]{:S(2)}) copy-start(s32[60]{0:T(128)} %param.7) | copy-start | bytes 724
  61.6 42.9 %copy-start.6 = (s32[8]{0:T(128)S(1)}, s32[8]{0:T(128)}, u32[]{:S(2)}) copy-start(s32[8]{0:T(128)} %param.6) | copy-start | bytes 100
  64.3 35.9 %collective-permute-start.9 = (bf16[8,2,15,16,128]{4,3,2,1,0:T(8,128)(2,1)S(1)}, bf16[8,2,15,16,128]{4,3,2,1,0:T(8,128)(2,1)S(1)}, u32[]{:S(2)}, u32[]{:S(2)}) collective-permute-start(bf16[8,2,15,16,128]{4,3,2,1,0:T(8,128)(2,1)S(1)} %get-tuple-element.6), channel_id=1, source_target_pairs={{0,192},{16,208},{32,224},{48,240},{64,0},{80,16},{96,32},{112,48}... | collective-permute-start | bytes 2949128 | tf_op jit(solution)/shard_map/ppermute | solution.py:19
  79.0 25.3 %collective-permute-start.7 = (bf16[8,2,15,16,128]{4,3,2,1,0:T(8,128)(2,1)S(1)}, bf16[8,2,15,16,128]{4,3,2,1,0:T(8,128)(2,1)S(1)}, u32[]{:S(2)}, u32[]{:S(2)}) collective-permute-start(bf16[8,2,15,16,128]{4,3,2,1,0:T(8,128)(2,1)S(1)} %get-tuple-element.6), channel_id=1, source_target_pairs={{0,64},{16,80},{32,96},{48,112},{64,128},{80,144},{96,160},{112,17... | collective-permute-start | bytes 2949128 | tf_op jit(solution)/shard_map/ppermute | solution.py:18
  101.0 13.4 %collective-permute-start.10 = (bf16[4,2,15,16,128]{4,3,2,1,0:T(8,128)(2,1)}, bf16[4,2,15,16,128]{4,3,2,1,0:T(8,128)(2,1)S(1)}, u32[]{:S(2)}, u32[]{:S(2)}) collective-permute-start(bf16[4,2,15,16,128]{4,3,2,1,0:T(8,128)(2,1)} %slice.81), channel_id=1, source_target_pairs={{0,192},{16,208},{32,224},{48,240},{64,0},{80,16},{96,32},{112,48}... | collective-permute-start | bytes 1474568 | tf_op jit(solution)/shard_map/ppermute | solution.py:22
  104.4 12.9 %collective-permute-start.8 = (bf16[4,2,15,16,128]{4,3,2,1,0:T(8,128)(2,1)S(1)}, bf16[4,2,15,16,128]{4,3,2,1,0:T(8,128)(2,1)S(1)}, u32[]{:S(2)}, u32[]{:S(2)}) collective-permute-start(bf16[4,2,15,16,128]{4,3,2,1,0:T(8,128)(2,1)S(1)} %slice.80), channel_id=1, source_target_pairs={{0,64},{16,80},{32,96},{48,112},{64,128},{80,144},{96,160},{112,17... | collective-permute-start | bytes 1474568 | tf_op jit(solution)/shard_map/ppermute | solution.py:21
  106.0 16.6 %copy-start.4 = (bf16[8,2,15,32,128]{4,3,2,1,0:T(8,128)(2,1)S(1)}, bf16[8,2,15,32,128]{4,3,2,1,0:T(8,128)(2,1)}, u32[]{:S(2)}) copy-start(bf16[8,2,15,32,128]{4,3,2,1,0:T(8,128)(2,1)} %param.4) | copy-start | bytes 5898244
  119.7 84.3 %collective-permute-start.15 = (bf16[8,2,15,128,128]{4,3,2,1,0:T(8,128)(2,1)}, bf16[8,2,15,128,128]{4,3,2,1,0:T(8,128)(2,1)}, u32[]{:S(2)}, u32[]{:S(2)}) collective-permute-start(bf16[8,2,15,128,128]{4,3,2,1,0:T(8,128)(2,1)} %constant_dynamic-update-slice_fusion.5), channel_id=1, source_target_pairs={{0,16},{16,0},{32,48},{48,32},{64,80},{80,64},{96,112},{112,96},{1... | collective-permute-start | bytes 23592968 | tf_op jit(solution)/shard_map/ppermute | solution.py:57
  122.7 45.8 %collective-permute-start.12 = (bf16[8,2,15,32,128]{4,3,2,1,0:T(8,128)(2,1)S(1)}, bf16[8,2,15,32,128]{4,3,2,1,0:T(8,128)(2,1)S(1)}, u32[]{:S(2)}, u32[]{:S(2)}) collective-permute-start(bf16[8,2,15,32,128]{4,3,2,1,0:T(8,128)(2,1)S(1)} %broadcast_select_fusion), channel_id=1, source_target_pairs={{0,4},{4,8},{8,12},{12,0},{1,5},{5,9},{9,13},{13,1},{2,6},{6,10},{... | collective-permute-start | bytes 5898248 | tf_op jit(solution)/shard_map/ppermute | solution.py:66
  124.1 44.6 %collective-permute-start.11 = (bf16[8,2,15,32,128]{4,3,2,1,0:T(8,128)(2,1)S(1)}, bf16[8,2,15,32,128]{4,3,2,1,0:T(8,128)(2,1)S(1)}, u32[]{:S(2)}, u32[]{:S(2)}) collective-permute-start(bf16[8,2,15,32,128]{4,3,2,1,0:T(8,128)(2,1)S(1)} %broadcast_select_fusion), channel_id=1, source_target_pairs={{0,12},{4,0},{8,4},{12,8},{1,13},{5,1},{9,5},{13,9},{2,14},{6,2},{... | collective-permute-start | bytes 5898248 | tf_op jit(solution)/shard_map/ppermute | solution.py:67
  168.6 31.4 %copy-start = (bf16[8,2,15,32,128]{4,3,2,1,0:T(8,128)(2,1)}, bf16[8,2,15,32,128]{4,3,2,1,0:T(8,128)(2,1)S(1)}, u32[]{:S(2)}) copy-start(bf16[8,2,15,32,128]{4,3,2,1,0:T(8,128)(2,1)S(1)} %collective-permute-done.12) | copy-start | bytes 5898244
  168.6 23.8 %collective-permute-start.13 = (bf16[4,2,15,32,128]{4,3,2,1,0:T(8,128)(2,1)S(1)}, bf16[4,2,15,32,128]{4,3,2,1,0:T(8,128)(2,1)S(1)}, u32[]{:S(2)}, u32[]{:S(2)}) collective-permute-start(bf16[4,2,15,32,128]{4,3,2,1,0:T(8,128)(2,1)S(1)} %slice.84), channel_id=1, source_target_pairs={{0,4},{4,8},{8,12},{12,0},{1,5},{5,9},{9,13},{13,1},{2,6},{6,10},{... | collective-permute-start | bytes 2949128 | tf_op jit(solution)/shard_map/ppermute | solution.py:69
  168.7 28.8 %copy-start.2 = (bf16[8,2,15,32,128]{4,3,2,1,0:T(8,128)(2,1)}, bf16[8,2,15,32,128]{4,3,2,1,0:T(8,128)(2,1)S(1)}, u32[]{:S(2)}) copy-start(bf16[8,2,15,32,128]{4,3,2,1,0:T(8,128)(2,1)S(1)} %collective-permute-done.11) | copy-start | bytes 5898244
  168.8 23.6 %collective-permute-start.14 = (bf16[4,2,15,32,128]{4,3,2,1,0:T(8,128)(2,1)S(1)}, bf16[4,2,15,32,128]{4,3,2,1,0:T(8,128)(2,1)}, u32[]{:S(2)}, u32[]{:S(2)}) collective-permute-start(bf16[4,2,15,32,128]{4,3,2,1,0:T(8,128)(2,1)S(1)} %slice.85), channel_id=1, source_target_pairs={{0,12},{4,0},{8,4},{12,8},{1,13},{5,1},{9,5},{13,9},{2,14},{6,2},{... | collective-permute-start | bytes 2949128 | tf_op jit(solution)/shard_map/ppermute | solution.py:70
  204.0 100.2 %reduce-scatter.5.cloned.1.call-start = ((), (), s32[]{:S(2)}) async-start(), calls=%async_computation.3 | async-start | bytes 2621440 | tf_op jit(solution)/shard_map/reduce_scatter | solution.py:109
  204.0 2.8 copy-start.3
  209.3 2.5 copy-start.1
Sparse Core Ops, SparseCore 0:
  204.1 49.1 reduce-scatter.2
  255.8 48.3 reduce-scatter.4

commit v6 on v5

--- a/solution.py
+++ b/solution.py
@@ -72,6 +72,21 @@
     return [w, from_right, opp, from_left]
 
 
+def ring_reduce_scatter(part):
+    n = lax.axis_size("rep")
+    d = lax.axis_index("rep")
+    width = part.shape[0] // n
+    fwd = [(i, (i + 1) % n) for i in range(n)]
+
+    def chunk(t):
+        return lax.dynamic_slice_in_dim(part, (t % n) * width, width, axis=0)
+
+    acc = chunk(d + n - 1)
+    for step in range(1, n):
+        acc = lax.ppermute(acc, "rep", fwd) + chunk(d + 2 * n - step - 1)
+    return acc
+
+
 def body(integrals, amplitudes, virt_count, occ_irrep):
     ngroup = integrals.shape[0]
     k_local = integrals.shape[2]
@@ -95,7 +110,7 @@
     w_blocks = gather_integrals(masked)
     t_mine, t_other = gather_amplitudes(amplitudes, col_index)
     sums = []
-    for t_half in (t_mine, t_other):
+    for t_half, name in ((t_mine, "em"), (t_other, "eo")):
         width = c_local
         part = None
         for s, w_blk in enumerate(w_blocks):
@@ -106,7 +121,10 @@
                 preferred_element_type=jnp.float32,
             )
             part = term if part is None else part + term
-        sums.append(lax.psum_scatter(part, "rep", scatter_dimension=0, tiled=True))
+        if name == "em":
+            sums.append(ring_reduce_scatter(part))
+        else:
+            sums.append(lax.psum_scatter(part, "rep", scatter_dimension=0, tiled=True))
     summed = jnp.where(
         core == 0, jnp.concatenate(sums, axis=3), jnp.concatenate(sums[::-1], axis=3)
     )

time: 314 us -> 294 us (0.936); the launches traced: 314 us -> 291 us
  waiting for transfers between devices: 208 us -> 169 us
  starting transfers between devices: 43.2 us -> 57.7 us
    reduce_scatter x2 -> x1, waiting for transfers between devices: 88.2 us -> 0.02 us  [body(): sums.append(lax.psum_scatter(part, 'rep', scatter_dimension=0, tiled=True))]
    ppermute x0 -> x3, waiting for transfers between devices: none -> 53.7 us  [ring_reduce_scatter(): acc = lax.ppermute(acc, 'rep', fwd) + chunk(d + 2 * n - step - 1)]
    ppermute x0 -> x3, starting transfers between devices: none -> 15 us  [ring_reduce_scatter(): acc = lax.ppermute(acc, 'rep', fwd) + chunk(d + 2 * n - step - 1)]
    ppermute x1, waiting for transfers between devices: 20.9 us -> 16 us  [gather_integrals(): opp_lo = lax.ppermute(from_left[:half], 'col', fwd)]
  transfers between devices with their start and end apart: 18 -> 20, of which waited for: 10 -> 11; matrix products, arithmetic and copies ran while one was open for 11% -> 10% of each run, Pallas kernels for 0% -> 0%
where the time goes in v6:
time: 294 us; the launch traced here: 291 us
  waiting for transfers between devices  169 us (57%)
  starting transfers between devices  57.7 us (20%)
  matrix products  21.6 us (7%)
  local copies, waits for them, and re-layouts  14.9 us (5%)
  other arithmetic  14 us (5%)
  between operations  13.6 us (5%)
    ppermute x3, waiting for transfers between devices, ring_reduce_scatter(): acc = lax.ppermute(acc, 'rep', fwd) + chunk(d + 2 * n - step - 1)  53.7 us
    ppermute x1, waiting for transfers between devices, gather_integrals(): from_left = lax.ppermute(w, 'col', fwd)  42.8 us
    dot_general x8, matrix products, body(): jnp.einsum('gikca,gjkcb->giajb', w_blk, t_half[:, :, :, s * width:(s + 1)...  21.6 us
    ppermute x2, waiting for transfers between devices, ring4_pieces(): from_right = lax.ppermute(block, axis, bwd)  21.1 us
    ppermute x2, starting transfers between devices, ring4_pieces(): from_right = lax.ppermute(block, axis, bwd)  17.1 us
    ppermute x2, waiting for transfers between devices, ring4_pieces(): from_left = lax.ppermute(block, axis, fwd)  16.3 us
    ppermute x1, waiting for transfers between devices, gather_integrals(): opp_lo = lax.ppermute(from_left[:half], 'col', fwd)  16 us
    ppermute x3, starting transfers between devices, ring_reduce_scatter(): acc = lax.ppermute(acc, 'rep', fwd) + chunk(d + 2 * n - step - 1)  15 us
  transfers between devices with their start and end apart: 20, of which 11 were waited for; matrix products, arithmetic and copies ran while one was open for 10% of the time, Pallas kernels for 0%

profile of v6, /device:TPU:1, one launch (start us, length us, event | category | flops | bytes accessed | tf_op | source)
XLA Modules:
  0.0 290.7 jit_solution(885629641154042360)
XLA Ops:
  6.5 1.2 broadcast_select_fusion.3
  7.8 3.3 %collective-permute-start = (bf16[8,2,15,8,128]{4,3,2,1,0:T(8,128)(2,1)S(1)}, bf16[8,2,15,8,128]{4,3,2,1,0:T(8,128)(2,1)S(1)}, u32[]{:S(2)}, u32[]{:S(2)}) collective-permute-start(bf16[8,2,15,8,128]{4,3,2,1,0:T(8,128)(2,1)S(1)} %get-tuple-element.11), channel_id=1, source_target_pairs={{0,16},{16,0},{32,48},{48,32},{64,80},{80,64},{96,112},{112,96},{1... | collective-permute-start | bytes 1474568 | tf_op jit(solution)/shard_map/ppermute | solution.py:30
  11.1 1.5 collective-permute-done
  12.6 5.1 %broadcast_in_dim.56 = bf16[8,2,15,128,128]{4,3,2,1,0:T(8,128)(2,1)} broadcast(bf16[]{:T(256)} %constant.131.clone.1), dimensions={} | broadcast | bytes 7864322 | tf_op jit(solution)/shard_map/broadcast_in_dim | solution.py:47
  17.7 1.6 constant_dynamic-update-slice_fusion.5
  19.2 2.7 collective-permute-start.3
  21.9 5.1 %collective-permute-start.5 = (bf16[8,4,15,8,128]{4,3,2,1,0:T(8,128)(2,1)S(1)}, bf16[8,4,15,8,128]{4,3,2,1,0:T(8,128)(2,1)S(1)}, u32[]{:S(2)}, u32[]{:S(2)}) collective-permute-start(bf16[8,4,15,8,128]{4,3,2,1,0:T(8,128)(2,1)S(1)} %copy-done.4), channel_id=1, source_target_pairs={{0,32},{16,48},{32,0},{48,16},{64,96},{80,112},{96,64},{112,80},{1... | collective-permute-start | bytes 2949128 | tf_op jit(solution)/shard_map/ppermute | solution.py:44
  27.1 16.3 %collective-permute-done.1 = bf16[8,2,15,16,128]{4,3,2,1,0:T(8,128)(2,1)S(1)} collective-permute-done((bf16[8,2,15,16,128]{4,3,2,1,0:T(8,128)(2,1)S(1)}, bf16[8,2,15,16,128]{4,3,2,1,0:T(8,128)(2,1)S(1)}, u32[]{:S(2)}, u32[]{:S(2)}) %collective-permute-start.1) | collective-permute-done | bytes 983072 | tf_op jit(solution)/shard_map/ppermute | solution.py:18
  43.4 0.8 slice.76
  44.2 0.8 slice.77
  45.0 2.7 collective-permute-start.4
  47.7 5.4 %collective-permute-done.5 = bf16[8,4,15,8,128]{4,3,2,1,0:T(8,128)(2,1)S(1)} collective-permute-done((bf16[8,4,15,8,128]{4,3,2,1,0:T(8,128)(2,1)S(1)}, bf16[8,4,15,8,128]{4,3,2,1,0:T(8,128)(2,1)S(1)}, u32[]{:S(2)}, u32[]{:S(2)}) %collective-permute-start.5) | collective-permute-done | bytes 983072 | tf_op jit(solution)/shard_map/ppermute | solution.py:44
  53.1 0.9 broadcast_select_fusion.1
  54.0 3.4 %collective-permute-start.6 = (bf16[8,2,15,8,128]{4,3,2,1,0:T(8,128)(2,1)}, bf16[8,2,15,8,128]{4,3,2,1,0:T(8,128)(2,1)S(1)}, u32[]{:S(2)}, u32[]{:S(2)}) collective-permute-start(bf16[8,2,15,8,128]{4,3,2,1,0:T(8,128)(2,1)} %get-tuple-element.9), channel_id=1, source_target_pairs={{0,16},{16,0},{32,48},{48,32},{64,80},{80,64},{96,112},{112,96},{1... | collective-permute-start | bytes 1474568 | tf_op jit(solution)/shard_map/ppermute | solution.py:30
  57.3 1.2 constant_dynamic-update-slice_fusion.4
  58.6 2.2 maximum_dynamic-update-slice_fusion
  60.8 1.2 constant_dynamic-update-slice_fusion.3
  61.9 1.5 constant_dynamic-update-slice_fusion.2
  63.4 14.5 %collective-permute-start.9 = (bf16[8,2,15,16,128]{4,3,2,1,0:T(8,128)(2,1)S(1)}, bf16[8,2,15,16,128]{4,3,2,1,0:T(8,128)(2,1)S(1)}, u32[]{:S(2)}, u32[]{:S(2)}) collective-permute-start(bf16[8,2,15,16,128]{4,3,2,1,0:T(8,128)(2,1)S(1)} %get-tuple-element.6), channel_id=1, source_target_pairs={{0,192},{16,208},{32,224},{48,240},{64,0},{80,16},{96,32},{112,48}... | collective-permute-start | bytes 2949128 | tf_op jit(solution)/shard_map/ppermute | solution.py:19
  77.9 21.1 %collective-permute-done.9 = bf16[8,2,15,16,128]{4,3,2,1,0:T(8,128)(2,1)S(1)} collective-permute-done((bf16[8,2,15,16,128]{4,3,2,1,0:T(8,128)(2,1)S(1)}, bf16[8,2,15,16,128]{4,3,2,1,0:T(8,128)(2,1)S(1)}, u32[]{:S(2)}, u32[]{:S(2)}) %collective-permute-start.9) | collective-permute-done | bytes 983072 | tf_op jit(solution)/shard_map/ppermute | solution.py:19
  99.0 3.5 %collective-permute-start.10 = (bf16[4,2,15,16,128]{4,3,2,1,0:T(8,128)(2,1)S(1)}, bf16[4,2,15,16,128]{4,3,2,1,0:T(8,128)(2,1)S(1)}, u32[]{:S(2)}, u32[]{:S(2)}) collective-permute-start(bf16[4,2,15,16,128]{4,3,2,1,0:T(8,128)(2,1)S(1)} %slice.81), channel_id=1, source_target_pairs={{0,192},{16,208},{32,224},{48,240},{64,0},{80,16},{96,32},{112,48}... | collective-permute-start | bytes 1474568 | tf_op jit(solution)/shard_map/ppermute | solution.py:22
  102.5 0.8 slice.80
  103.3 1.2 constant_dynamic-update-slice_fusion.1
  104.5 7.7 %collective-permute-done.10 = bf16[4,2,15,16,128]{4,3,2,1,0:T(8,128)(2,1)S(1)} collective-permute-done((bf16[4,2,15,16,128]{4,3,2,1,0:T(8,128)(2,1)S(1)}, bf16[4,2,15,16,128]{4,3,2,1,0:T(8,128)(2,1)S(1)}, u32[]{:S(2)}, u32[]{:S(2)}) %collective-permute-start.10) | collective-permute-done | bytes 491552 | tf_op jit(solution)/shard_map/ppermute | solution.py:22
  112.2 4.2 %collective-permute-done.8 = bf16[4,2,15,16,128]{4,3,2,1,0:T(8,128)(2,1)S(1)} collective-permute-done((bf16[4,2,15,16,128]{4,3,2,1,0:T(8,128)(2,1)}, bf16[4,2,15,16,128]{4,3,2,1,0:T(8,128)(2,1)S(1)}, u32[]{:S(2)}, u32[]{:S(2)}) %collective-permute-start.8) | collective-permute-done | bytes 491552 | tf_op jit(solution)/shard_map/ppermute | solution.py:21
  116.4 1.2 maximum_dynamic-update-slice_fusion.1
  117.6 1.2 constant_dynamic-update-slice_fusion
  118.8 2.0 collective-permute-start.18
  120.8 0.1 dynamic_slice.19
  120.9 0.1 select_reduce_fusion
  121.0 0.1 iota_compare_fusion.1
  121.0 0.1 broadcast_compare_fusion
  121.1 0.8 broadcast_and_fusion
  121.9 1.7 broadcast_select_fusion
  123.7 1.4 collective-permute-start.12
  125.0 1.5 collective-permute-start.11
  126.5 42.8 %collective-permute-done.12 = bf16[8,2,15,32,128]{4,3,2,1,0:T(8,128)(2,1)S(1)} collective-permute-done((bf16[8,2,15,32,128]{4,3,2,1,0:T(8,128)(2,1)S(1)}, bf16[8,2,15,32,128]{4,3,2,1,0:T(8,128)(2,1)S(1)}, u32[]{:S(2)}, u32[]{:S(2)}) %collective-permute-start.12) | collective-permute-done | bytes 1966112 | tf_op jit(solution)/shard_map/ppermute | solution.py:66
  169.4 0.1 slice.84
  169.4 0.1 collective-permute-start.13
  169.6 0.1 slice.85
  169.6 2.7 collective-permute-start.14
  172.3 2.4 fusion.2
  174.8 2.4 fusion.3
  177.2 16.0 %collective-permute-done.13 = bf16[4,2,15,32,128]{4,3,2,1,0:T(8,128)(2,1)S(1)} collective-permute-done((bf16[4,2,15,32,128]{4,3,2,1,0:T(8,128)(2,1)S(1)}, bf16[4,2,15,32,128]{4,3,2,1,0:T(8,128)(2,1)S(1)}, u32[]{:S(2)}, u32[]{:S(2)}) %collective-permute-start.13) | collective-permute-done | bytes 983072 | tf_op jit(solution)/shard_map/ppermute | solution.py:69
  193.2 1.0 copy-done.6
  194.2 2.4 fusion.1
  196.6 3.9 %bitcast_add_fusion = f32[8,2,128,2,128]{4,2,3,1,0:T(8,128)} fusion(f32[8,2,128,2,128,1]{4,2,5,3,1,0:T(8,128)S(1)} %fusion.1, f32[8,2,128,2,128,1]{4,2,5,3,1,0:T(8,128)S(1)} %fusion.2, f32[8,2,128,2,128,1]{4,2,5,3,1,0:T(8,128)S(1)} %fusion.3, bf16[8,2,15,128,128]{4,3,2,1,0:T(8,128)(2,1)} %collective-permute-done.18, ...), kind=kOutput, calls=%fused_computation | convolution fusion | flops 504889344 | bytes 12320768 | tf_op jit(solution)/shard_map/gikca,gjkcb->giajb/dot_general | solution.py:117
  200.6 2.7 fusion.5
  203.3 2.6 fusion.7
  205.9 2.6 fusion.6
  208.5 2.6 bitcast_add_fusion.3
  211.1 2.2 collective-permute-start.15
  213.3 22.0 %collective-permute-done.15 = f32[2,2,128,2,128]{4,2,3,1,0:T(8,128)S(1)} collective-permute-done((f32[2,2,128,2,128]{4,2,3,1,0:T(8,128)S(1)}, f32[2,2,128,2,128]{4,2,3,1,0:T(8,128)S(1)}, u32[]{:S(2)}, u32[]{:S(2)}) %collective-permute-start.15) | collective-permute-done | bytes 524320 | tf_op jit(solution)/shard_map/ppermute | solution.py:86
  235.3 0.1 dynamic-slice_add_fusion.2
  235.4 10.3 %collective-permute-start.16 = (f32[2,2,128,2,128]{4,2,3,1,0:T(8,128)S(1)}, f32[2,2,128,2,128]{4,2,3,1,0:T(8,128)}, u32[]{:S(2)}, u32[]{:S(2)}) collective-permute-start(f32[2,2,128,2,128]{4,2,3,1,0:T(8,128)S(1)} %dynamic-slice_add_fusion.2), channel_id=1, source_target_pairs={{0,1},{1,2},{2,3},{3,0},{4,5},{5,6},{6,7},{7,4},{8,9},{9,10},{10,1... | collective-permute-start | bytes 1572872 | tf_op jit(solution)/shard_map/ppermute | solution.py:86
  245.7 21.3 %collective-permute-done.16 = f32[2,2,128,2,128]{4,2,3,1,0:T(8,128)} collective-permute-done((f32[2,2,128,2,128]{4,2,3,1,0:T(8,128)S(1)}, f32[2,2,128,2,128]{4,2,3,1,0:T(8,128)}, u32[]{:S(2)}, u32[]{:S(2)}) %collective-permute-start.16) | collective-permute-done | bytes 524320 | tf_op jit(solution)/shard_map/ppermute | solution.py:86
  267.1 1.1 dynamic-slice_add_fusion.1
  268.2 2.5 collective-permute-start.17
  270.7 0.1 dynamic_slice.18
  270.7 0.1 iota_compare_fusion.2
  270.8 10.3 %collective-permute-done.17 = f32[2,2,128,2,128]{4,2,3,1,0:T(8,128)S(1)} collective-permute-done((f32[2,2,128,2,128]{4,2,3,1,0:T(8,128)S(1)}, f32[2,2,128,2,128]{4,2,3,1,0:T(8,128)S(1)}, u32[]{:S(2)}, u32[]{:S(2)}) %collective-permute-start.17) | collective-permute-done | bytes 524320 | tf_op jit(solution)/shard_map/ppermute | solution.py:86
  281.1 0.1 dynamic-slice_add_fusion
  281.2 1.4 fusion.19
  282.6 1.2 copy.6
  (34 shorter events, 0.2 us)
Async XLA Ops:
  6.5 274.6 %reduce-scatter.2.cloned.1.call-start = ((), (), s32[]{:S(2)}) async-start(), calls=%async_computation.1 | async-start | bytes 2621440 | tf_op jit(solution)/shard_map/reduce_scatter | solution.py:127
  7.8 4.8 %collective-permute-start = (bf16[8,2,15,8,128]{4,3,2,1,0:T(8,128)(2,1)S(1)}, bf16[8,2,15,8,128]{4,3,2,1,0:T(8,128)(2,1)S(1)}, u32[]{:S(2)}, u32[]{:S(2)}) collective-permute-start(bf16[8,2,15,8,128]{4,3,2,1,0:T(8,128)(2,1)S(1)} %get-tuple-element.11), channel_id=1, source_target_pairs={{0,16},{16,0},{32,48},{48,32},{64,80},{80,64},{96,112},{112,96},{1... | collective-permute-start | bytes 1474568 | tf_op jit(solution)/shard_map/ppermute | solution.py:30
  17.7 4.2 %copy-start.4 = (bf16[8,4,15,8,128]{4,3,2,1,0:T(8,128)(2,1)S(1)}, bf16[8,4,15,8,128]{4,3,2,1,0:T(8,128)(2,1)}, u32[]{:S(2)}) copy-start(bf16[8,4,15,8,128]{4,3,2,1,0:T(8,128)(2,1)} %param.5) | copy-start | bytes 2949124
  19.2 24.2 %collective-permute-start.1 = (bf16[8,2,15,16,128]{4,3,2,1,0:T(8,128)(2,1)S(1)}, bf16[8,2,15,16,128]{4,3,2,1,0:T(8,128)(2,1)S(1)}, u32[]{:S(2)}, u32[]{:S(2)}) collective-permute-start(bf16[8,2,15,16,128]{4,3,2,1,0:T(8,128)(2,1)S(1)} %get-tuple-element.8), channel_id=1, source_target_pairs={{0,64},{16,80},{32,96},{48,112},{64,128},{80,144},{96,160},{112,17... | collective-permute-start | bytes 2949128 | tf_op jit(solution)/shard_map/ppermute | solution.py:18
  19.2 25.0 %collective-permute-start.3 = (bf16[8,2,15,16,128]{4,3,2,1,0:T(8,128)(2,1)S(1)}, bf16[8,2,15,16,128]{4,3,2,1,0:T(8,128)(2,1)S(1)}, u32[]{:S(2)}, u32[]{:S(2)}) collective-permute-start(bf16[8,2,15,16,128]{4,3,2,1,0:T(8,128)(2,1)S(1)} %get-tuple-element.8), channel_id=1, source_target_pairs={{0,192},{16,208},{32,224},{48,240},{64,0},{80,16},{96,32},{112,48}... | collective-permute-start | bytes 2949128 | tf_op jit(solution)/shard_map/ppermute | solution.py:19
  21.9 31.2 %collective-permute-start.5 = (bf16[8,4,15,8,128]{4,3,2,1,0:T(8,128)(2,1)S(1)}, bf16[8,4,15,8,128]{4,3,2,1,0:T(8,128)(2,1)S(1)}, u32[]{:S(2)}, u32[]{:S(2)}) collective-permute-start(bf16[8,4,15,8,128]{4,3,2,1,0:T(8,128)(2,1)S(1)} %copy-done.4), channel_id=1, source_target_pairs={{0,32},{16,48},{32,0},{48,16},{64,96},{80,112},{96,64},{112,80},{1... | collective-permute-start | bytes 2949128 | tf_op jit(solution)/shard_map/ppermute | solution.py:44
  44.2 14.4 %collective-permute-start.2 = (bf16[4,2,15,16,128]{4,3,2,1,0:T(8,128)(2,1)}, bf16[4,2,15,16,128]{4,3,2,1,0:T(8,128)(2,1)S(1)}, u32[]{:S(2)}, u32[]{:S(2)}) collective-permute-start(bf16[4,2,15,16,128]{4,3,2,1,0:T(8,128)(2,1)} %slice.76), channel_id=1, source_target_pairs={{0,64},{16,80},{32,96},{48,112},{64,128},{80,144},{96,160},{112,17... | collective-permute-start | bytes 1474568 | tf_op jit(solution)/shard_map/ppermute | solution.py:21
  45.0 13.6 %collective-permute-start.4 = (bf16[4,2,15,16,128]{4,3,2,1,0:T(8,128)(2,1)}, bf16[4,2,15,16,128]{4,3,2,1,0:T(8,128)(2,1)}, u32[]{:S(2)}, u32[]{:S(2)}) collective-permute-start(bf16[4,2,15,16,128]{4,3,2,1,0:T(8,128)(2,1)} %slice.77), channel_id=1, source_target_pairs={{0,192},{16,208},{32,224},{48,240},{64,0},{80,16},{96,32},{112,48}... | collective-permute-start | bytes 1474568 | tf_op jit(solution)/shard_map/ppermute | solution.py:22
  54.0 8.0 %collective-permute-start.6 = (bf16[8,2,15,8,128]{4,3,2,1,0:T(8,128)(2,1)}, bf16[8,2,15,8,128]{4,3,2,1,0:T(8,128)(2,1)S(1)}, u32[]{:S(2)}, u32[]{:S(2)}) collective-permute-start(bf16[8,2,15,8,128]{4,3,2,1,0:T(8,128)(2,1)} %get-tuple-element.9), channel_id=1, source_target_pairs={{0,16},{16,0},{32,48},{48,32},{64,80},{80,64},{96,112},{112,96},{1... | collective-permute-start | bytes 1474568 | tf_op jit(solution)/shard_map/ppermute | solution.py:30
  63.4 35.6 %collective-permute-start.9 = (bf16[8,2,15,16,128]{4,3,2,1,0:T(8,128)(2,1)S(1)}, bf16[8,2,15,16,128]{4,3,2,1,0:T(8,128)(2,1)S(1)}, u32[]{:S(2)}, u32[]{:S(2)}) collective-permute-start(bf16[8,2,15,16,128]{4,3,2,1,0:T(8,128)(2,1)S(1)} %get-tuple-element.6), channel_id=1, source_target_pairs={{0,192},{16,208},{32,224},{48,240},{64,0},{80,16},{96,32},{112,48}... | collective-permute-start | bytes 2949128 | tf_op jit(solution)/shard_map/ppermute | solution.py:19
  77.9 24.6 %collective-permute-start.7 = (bf16[8,2,15,16,128]{4,3,2,1,0:T(8,128)(2,1)S(1)}, bf16[8,2,15,16,128]{4,3,2,1,0:T(8,128)(2,1)S(1)}, u32[]{:S(2)}, u32[]{:S(2)}) collective-permute-start(bf16[8,2,15,16,128]{4,3,2,1,0:T(8,128)(2,1)S(1)} %get-tuple-element.6), channel_id=1, source_target_pairs={{0,64},{16,80},{32,96},{48,112},{64,128},{80,144},{96,160},{112,17... | collective-permute-start | bytes 2949128 | tf_op jit(solution)/shard_map/ppermute | solution.py:18
  99.0 13.2 %collective-permute-start.10 = (bf16[4,2,15,16,128]{4,3,2,1,0:T(8,128)(2,1)S(1)}, bf16[4,2,15,16,128]{4,3,2,1,0:T(8,128)(2,1)S(1)}, u32[]{:S(2)}, u32[]{:S(2)}) collective-permute-start(bf16[4,2,15,16,128]{4,3,2,1,0:T(8,128)(2,1)S(1)} %slice.81), channel_id=1, source_target_pairs={{0,192},{16,208},{32,224},{48,240},{64,0},{80,16},{96,32},{112,48}... | collective-permute-start | bytes 1474568 | tf_op jit(solution)/shard_map/ppermute | solution.py:22
  103.3 13.1 %collective-permute-start.8 = (bf16[4,2,15,16,128]{4,3,2,1,0:T(8,128)(2,1)}, bf16[4,2,15,16,128]{4,3,2,1,0:T(8,128)(2,1)S(1)}, u32[]{:S(2)}, u32[]{:S(2)}) collective-permute-start(bf16[4,2,15,16,128]{4,3,2,1,0:T(8,128)(2,1)} %slice.80), channel_id=1, source_target_pairs={{0,64},{16,80},{32,96},{48,112},{64,128},{80,144},{96,160},{112,17... | collective-permute-start | bytes 1474568 | tf_op jit(solution)/shard_map/ppermute | solution.py:21
  104.5 16.3 %copy-start.7 = (s32[60]{0:T(128)S(1)}, s32[60]{0:T(128)}, u32[]{:S(2)}) copy-start(s32[60]{0:T(128)} %param.7) | copy-start | bytes 724
  104.5 16.4 %copy-start.5 = (s32[8]{0:T(128)S(1)}, s32[8]{0:T(128)}, u32[]{:S(2)}) copy-start(s32[8]{0:T(128)} %param.6) | copy-start | bytes 100
  118.8 53.5 %collective-permute-start.18 = (bf16[8,2,15,128,128]{4,3,2,1,0:T(8,128)(2,1)}, bf16[8,2,15,128,128]{4,3,2,1,0:T(8,128)(2,1)}, u32[]{:S(2)}, u32[]{:S(2)}) collective-permute-start(bf16[8,2,15,128,128]{4,3,2,1,0:T(8,128)(2,1)} %constant_dynamic-update-slice_fusion), channel_id=1, source_target_pairs={{0,16},{16,0},{32,48},{48,32},{64,80},{80,64},{96,112},{112,96},{1... | collective-permute-start | bytes 23592968 | tf_op jit(solution)/shard_map/ppermute | solution.py:57
  123.7 45.7 %collective-permute-start.12 = (bf16[8,2,15,32,128]{4,3,2,1,0:T(8,128)(2,1)S(1)}, bf16[8,2,15,32,128]{4,3,2,1,0:T(8,128)(2,1)S(1)}, u32[]{:S(2)}, u32[]{:S(2)}) collective-permute-start(bf16[8,2,15,32,128]{4,3,2,1,0:T(8,128)(2,1)S(1)} %broadcast_select_fusion), channel_id=1, source_target_pairs={{0,4},{4,8},{8,12},{12,0},{1,5},{5,9},{9,13},{13,1},{2,6},{6,10},{... | collective-permute-start | bytes 5898248 | tf_op jit(solution)/shard_map/ppermute | solution.py:66
  125.0 44.5 %collective-permute-start.11 = (bf16[8,2,15,32,128]{4,3,2,1,0:T(8,128)(2,1)S(1)}, bf16[8,2,15,32,128]{4,3,2,1,0:T(8,128)(2,1)S(1)}, u32[]{:S(2)}, u32[]{:S(2)}) collective-permute-start(bf16[8,2,15,32,128]{4,3,2,1,0:T(8,128)(2,1)S(1)} %broadcast_select_fusion), channel_id=1, source_target_pairs={{0,12},{4,0},{8,4},{12,8},{1,13},{5,1},{9,5},{13,9},{2,14},{6,2},{... | collective-permute-start | bytes 5898248 | tf_op jit(solution)/shard_map/ppermute | solution.py:67
  169.4 27.2 %copy-start = (bf16[8,2,15,32,128]{4,3,2,1,0:T(8,128)(2,1)}, bf16[8,2,15,32,128]{4,3,2,1,0:T(8,128)(2,1)S(1)}, u32[]{:S(2)}) copy-start(bf16[8,2,15,32,128]{4,3,2,1,0:T(8,128)(2,1)S(1)} %collective-permute-done.12) | copy-start | bytes 5898244
  169.4 23.8 %collective-permute-start.13 = (bf16[4,2,15,32,128]{4,3,2,1,0:T(8,128)(2,1)S(1)}, bf16[4,2,15,32,128]{4,3,2,1,0:T(8,128)(2,1)S(1)}, u32[]{:S(2)}, u32[]{:S(2)}) collective-permute-start(bf16[4,2,15,32,128]{4,3,2,1,0:T(8,128)(2,1)S(1)} %slice.84), channel_id=1, source_target_pairs={{0,4},{4,8},{8,12},{12,0},{1,5},{5,9},{9,13},{13,1},{2,6},{6,10},{... | collective-permute-start | bytes 2949128 | tf_op jit(solution)/shard_map/ppermute | solution.py:69
  169.6 5.2 %copy-start.2 = (bf16[8,2,15,32,128]{4,3,2,1,0:T(8,128)(2,1)}, bf16[8,2,15,32,128]{4,3,2,1,0:T(8,128)(2,1)S(1)}, u32[]{:S(2)}) copy-start(bf16[8,2,15,32,128]{4,3,2,1,0:T(8,128)(2,1)S(1)} %collective-permute-done.11) | copy-start | bytes 5898244
  169.6 23.6 %collective-permute-start.14 = (bf16[4,2,15,32,128]{4,3,2,1,0:T(8,128)(2,1)S(1)}, bf16[4,2,15,32,128]{4,3,2,1,0:T(8,128)(2,1)S(1)}, u32[]{:S(2)}, u32[]{:S(2)}) collective-permute-start(bf16[4,2,15,32,128]{4,3,2,1,0:T(8,128)(2,1)S(1)} %slice.85), channel_id=1, source_target_pairs={{0,12},{4,0},{8,4},{12,8},{1,13},{5,1},{9,5},{13,9},{2,14},{6,2},{... | collective-permute-start | bytes 2949128 | tf_op jit(solution)/shard_map/ppermute | solution.py:70
  193.2 1.0 copy-start.6
  203.3 2.6 copy-start.3
  205.9 2.6 copy-start.1
  211.1 24.2 %collective-permute-start.15 = (f32[2,2,128,2,128]{4,2,3,1,0:T(8,128)S(1)}, f32[2,2,128,2,128]{4,2,3,1,0:T(8,128)S(1)}, u32[]{:S(2)}, u32[]{:S(2)}) collective-permute-start(f32[2,2,128,2,128]{4,2,3,1,0:T(8,128)S(1)} %constant_dynamic-slice_fusion), channel_id=1, source_target_pairs={{0,1},{1,2},{2,3},{3,0},{4,5},{5,6},{6,7},{7,4},{8,9},{9,10},{10,1... | collective-permute-start | bytes 1572872 | tf_op jit(solution)/shard_map/ppermute | solution.py:86
  235.4 31.7 %collective-permute-start.16 = (f32[2,2,128,2,128]{4,2,3,1,0:T(8,128)S(1)}, f32[2,2,128,2,128]{4,2,3,1,0:T(8,128)}, u32[]{:S(2)}, u32[]{:S(2)}) collective-permute-start(f32[2,2,128,2,128]{4,2,3,1,0:T(8,128)S(1)} %dynamic-slice_add_fusion.2), channel_id=1, source_target_pairs={{0,1},{1,2},{2,3},{3,0},{4,5},{5,6},{6,7},{7,4},{8,9},{9,10},{10,1... | collective-permute-start | bytes 1572872 | tf_op jit(solution)/shard_map/ppermute | solution.py:86
  268.2 12.9 %collective-permute-start.17 = (f32[2,2,128,2,128]{4,2,3,1,0:T(8,128)S(1)}, f32[2,2,128,2,128]{4,2,3,1,0:T(8,128)S(1)}, u32[]{:S(2)}, u32[]{:S(2)}) collective-permute-start(f32[2,2,128,2,128]{4,2,3,1,0:T(8,128)S(1)} %dynamic-slice_add_fusion.1), channel_id=1, source_target_pairs={{0,1},{1,2},{2,3},{3,0},{4,5},{5,6},{6,7},{7,4},{8,9},{9,10},{10,1... | collective-permute-start | bytes 1572872 | tf_op jit(solution)/shard_map/ppermute | solution.py:86
Sparse Core Ops, SparseCore 0:
  200.7 70.5 reduce-scatter.1

commit v7 on v6

--- a/solution.py
+++ b/solution.py
@@ -33,6 +33,31 @@
     )
 
 
+def z_shift_perm(nrow, nrep, step):
+    pairs = []
+    for r in range(nrow):
+        zh = (r >> 1) & 1
+        for zl in range(nrep):
+            z = (zh * nrep + zl + step) % (2 * nrep)
+            dst_row = (r & ~2) | ((z // nrep) << 1)
+            pairs.append((r * nrep + zl, dst_row * nrep + z % nrep))
+    return pairs
+
+
+def zh_swap(part, nrow):
+    nrep = lax.axis_size("rep")
+    plus = z_shift_perm(nrow, nrep, 2)
+    minus = z_shift_perm(nrow, nrep, -2)
+    half = part.shape[0] // 2
+    lo = part[:half]
+    hi = part[half:]
+    lo = lax.ppermute(lo, ("row", "rep"), plus)
+    hi = lax.ppermute(hi, ("row", "rep"), minus)
+    lo = lax.ppermute(lo, ("row", "rep"), plus)
+    hi = lax.ppermute(hi, ("row", "rep"), minus)
+    return jnp.concatenate([lo, hi], axis=0)
+
+
 def gather_amplitudes(t_part, cl):
     nrow = lax.axis_size("row")
     r = lax.axis_index("row")
@@ -41,7 +66,7 @@
     core = r % 2
     ng, nj, nk, ncc, nb = t_part.shape
     hj = nj // 2
-    t_zh = lax.ppermute(t_part, "row", [(i, i ^ 2) for i in range(nrow)])
+    t_zh = zh_swap(t_part, nrow)
     own = ring4_pieces(core_quad(t_part, core, nrow, hj), "row", nrow, 4)
     pos = x - cl
     mine = jnp.zeros((ng, hj, nk, 16 * ncc, nb), t_part.dtype)

time: 294 us -> 295 us (level)
  waiting for transfers between devices: 169 us -> 190 us
  starting transfers between devices: 57.7 us -> 38.6 us
    ppermute x1 -> x4, waiting for transfers between devices: 5.41 us -> 32.3 us  [the longest x2 21.6 us: zh_swap(): hi = lax.ppermute(hi, ('row', 'rep'), minus)]
    ppermute x2, waiting for transfers between devices: 21.1 us -> 0.01 us  [ring4_pieces(): from_right = lax.ppermute(block, axis, bwd)]
    ppermute x3, waiting for transfers between devices: 53.7 us -> 68.5 us  [ring_reduce_scatter(): acc = lax.ppermute(acc, 'rep', fwd) + chunk(d + 2 * n - step - 1)]
    ppermute x3, starting transfers between devices: 15 us -> 0.25 us  [ring_reduce_scatter(): acc = lax.ppermute(acc, 'rep', fwd) + chunk(d + 2 * n - step - 1)]
    ppermute x2, starting transfers between devices: 17.1 us -> 4.09 us  [ring4_pieces(): from_right = lax.ppermute(block, axis, bwd)]
    ppermute x1 -> x4, starting transfers between devices: 5.14 us -> 15.6 us  [the longest x2 7.83 us: zh_swap(): hi = lax.ppermute(hi, ('row', 'rep'), minus)]
    ppermute x2, waiting for transfers between devices: 7.71 us -> 0.12 us  [ring4_pieces(): opp_hi = lax.ppermute(from_right[half:], axis, bwd)]
    ppermute x2, waiting for transfers between devices: 16.3 us -> 21.8 us  [ring4_pieces(): from_left = lax.ppermute(block, axis, fwd)]
  transfers between devices with their start and end apart: 20 -> 23, of which waited for: 11 -> 12; matrix products, arithmetic and copies ran while one was open for 10% -> 12% of each run, Pallas kernels for 0% -> 0%
where the time goes in v7:
time: 295 us; the launch traced here: 293 us
  waiting for transfers between devices  190 us (64%)
  starting transfers between devices  38.6 us (13%)
  matrix products  21.8 us (7%)
  other arithmetic  15.2 us (5%)
  between operations  13.7 us (5%)
  local copies, waits for them, and re-layouts  13.3 us (5%)
    ppermute x3, waiting for transfers between devices, ring_reduce_scatter(): acc = lax.ppermute(acc, 'rep', fwd) + chunk(d + 2 * n - step - 1)  68.5 us
    ppermute x1, waiting for transfers between devices, gather_integrals(): from_left = lax.ppermute(w, 'col', fwd)  42.9 us
    ppermute x2, waiting for transfers between devices, ring4_pieces(): from_left = lax.ppermute(block, axis, fwd)  21.8 us
    dot_general x8, matrix products, body(): jnp.einsum('gikca,gjkcb->giajb', w_blk, t_half[:, :, :, s * width:(s + 1)...  21.8 us
    ppermute x2, waiting for transfers between devices, zh_swap(): hi = lax.ppermute(hi, ('row', 'rep'), minus)  21.6 us
    ppermute x1, waiting for transfers between devices, gather_integrals(): opp_lo = lax.ppermute(from_left[:half], 'col', fwd)  15.9 us
    ppermute x2, waiting for transfers between devices, zh_swap(): lo = lax.ppermute(lo, ('row', 'rep'), plus)  10.7 us
    ppermute x2, waiting for transfers between devices, ring4_pieces(): opp_lo = lax.ppermute(from_left[:half], axis, fwd)  8.42 us
  transfers between devices with their start and end apart: 23, of which 12 were waited for; matrix products, arithmetic and copies ran while one was open for 12% of the time, Pallas kernels for 0%

profile of v7, /device:TPU:1, one launch (start us, length us, event | category | flops | bytes accessed | tf_op | source)
XLA Modules:
  0.0 292.7 jit_solution(15635548522698283635)
XLA Ops:
  6.5 1.3 broadcast_select_fusion.3
  7.9 3.3 %collective-permute-start = (bf16[8,2,15,8,128]{4,3,2,1,0:T(8,128)(2,1)S(1)}, bf16[8,2,15,8,128]{4,3,2,1,0:T(8,128)(2,1)S(1)}, u32[]{:S(2)}, u32[]{:S(2)}) collective-permute-start(bf16[8,2,15,8,128]{4,3,2,1,0:T(8,128)(2,1)S(1)} %get-tuple-element.13), channel_id=1, source_target_pairs={{0,16},{16,0},{32,48},{48,32},{64,80},{80,64},{96,112},{112,96},{1... | collective-permute-start | bytes 1474568 | tf_op jit(solution)/shard_map/ppermute | solution.py:30
  11.2 1.4 collective-permute-start.5
  12.7 5.1 %broadcast_in_dim.56 = bf16[8,2,15,128,128]{4,3,2,1,0:T(8,128)(2,1)} broadcast(bf16[]{:T(256)} %constant.131.clone.1), dimensions={} | broadcast | bytes 7864322 | tf_op jit(solution)/shard_map/broadcast_in_dim | solution.py:72
  17.8 1.5 constant_dynamic-update-slice_fusion.7
  19.2 1.3 collective-permute-start.1
  20.5 1.4 collective-permute-start.3
  21.9 4.3 %collective-permute-start.7 = (bf16[4,4,15,8,128]{4,3,2,1,0:T(8,128)(2,1)S(1)}, bf16[4,4,15,8,128]{4,3,2,1,0:T(8,128)(2,1)S(1)}, u32[]{:S(2)}, u32[]{:S(2)}) collective-permute-start(bf16[4,4,15,8,128]{4,3,2,1,0:T(8,128)(2,1)S(1)} %get-tuple-element.11), channel_id=1, source_target_pairs={{0,34},{1,35},{2,0},{3,1},{16,50},{17,51},{18,16},{19,17},{32,2},{... | collective-permute-start | bytes 1474568 | tf_op jit(solution)/shard_map/ppermute | solution.py:55
  26.3 5.1 %collective-permute-done.5 = bf16[4,4,15,8,128]{4,3,2,1,0:T(8,128)(2,1)} collective-permute-done((bf16[4,4,15,8,128]{4,3,2,1,0:T(8,128)(2,1)S(1)}, bf16[4,4,15,8,128]{4,3,2,1,0:T(8,128)(2,1)}, u32[]{:S(2)}, u32[]{:S(2)}) %collective-permute-start.5) | collective-permute-done | bytes 491552 | tf_op jit(solution)/shard_map/ppermute | solution.py:54
  31.4 6.4 %collective-permute-start.6 = (bf16[4,4,15,8,128]{4,3,2,1,0:T(8,128)(2,1)}, bf16[4,4,15,8,128]{4,3,2,1,0:T(8,128)(2,1)S(1)}, u32[]{:S(2)}, u32[]{:S(2)}) collective-permute-start(bf16[4,4,15,8,128]{4,3,2,1,0:T(8,128)(2,1)} %collective-permute-done.5), channel_id=1, source_target_pairs={{0,2},{1,3},{2,32},{3,33},{16,18},{17,19},{18,48},{19,49},{32,34},... | collective-permute-start | bytes 1474568 | tf_op jit(solution)/shard_map/ppermute | solution.py:56
  37.8 10.6 %collective-permute-done.7 = bf16[4,4,15,8,128]{4,3,2,1,0:T(8,128)(2,1)S(1)} collective-permute-done((bf16[4,4,15,8,128]{4,3,2,1,0:T(8,128)(2,1)S(1)}, bf16[4,4,15,8,128]{4,3,2,1,0:T(8,128)(2,1)S(1)}, u32[]{:S(2)}, u32[]{:S(2)}) %collective-permute-start.7) | collective-permute-done | bytes 491552 | tf_op jit(solution)/shard_map/ppermute | solution.py:55
  48.5 3.5 %collective-permute-start.8 = (bf16[4,4,15,8,128]{4,3,2,1,0:T(8,128)(2,1)S(1)}, bf16[4,4,15,8,128]{4,3,2,1,0:T(8,128)(2,1)S(1)}, u32[]{:S(2)}, u32[]{:S(2)}) collective-permute-start(bf16[4,4,15,8,128]{4,3,2,1,0:T(8,128)(2,1)S(1)} %collective-permute-done.7), channel_id=1, source_target_pairs={{0,34},{1,35},{2,0},{3,1},{16,50},{17,51},{18,16},{19,17},{32,2},{... | collective-permute-start | bytes 1474568 | tf_op jit(solution)/shard_map/ppermute | solution.py:57
  52.0 5.6 %collective-permute-done.6 = bf16[4,4,15,8,128]{4,3,2,1,0:T(8,128)(2,1)S(1)} collective-permute-done((bf16[4,4,15,8,128]{4,3,2,1,0:T(8,128)(2,1)}, bf16[4,4,15,8,128]{4,3,2,1,0:T(8,128)(2,1)S(1)}, u32[]{:S(2)}, u32[]{:S(2)}) %collective-permute-start.6) | collective-permute-done | bytes 491552 | tf_op jit(solution)/shard_map/ppermute | solution.py:56
  57.6 1.3 collective-permute-start.2
  58.9 0.8 slice.85
  59.7 1.5 collective-permute-start.4
  61.2 10.9 %collective-permute-done.8 = bf16[4,4,15,8,128]{4,3,2,1,0:T(8,128)(2,1)S(1)} collective-permute-done((bf16[4,4,15,8,128]{4,3,2,1,0:T(8,128)(2,1)S(1)}, bf16[4,4,15,8,128]{4,3,2,1,0:T(8,128)(2,1)S(1)}, u32[]{:S(2)}, u32[]{:S(2)}) %collective-permute-start.8) | collective-permute-done | bytes 491552 | tf_op jit(solution)/shard_map/ppermute | solution.py:57
  72.2 0.9 broadcast_select_fusion.1
  73.1 0.5 collective-permute-start.9
  73.6 1.2 constant_dynamic-update-slice_fusion.6
  74.7 2.3 maximum_dynamic-update-slice_fusion
  77.0 1.2 constant_dynamic-update-slice_fusion.5
  78.2 2.6 constant_dynamic-update-slice_fusion.4
  80.8 2.7 collective-permute-start.12
  83.5 21.8 %collective-permute-done.10 = bf16[8,2,15,16,128]{4,3,2,1,0:T(8,128)(2,1)S(1)} collective-permute-done((bf16[8,2,15,16,128]{4,3,2,1,0:T(8,128)(2,1)S(1)}, bf16[8,2,15,16,128]{4,3,2,1,0:T(8,128)(2,1)S(1)}, u32[]{:S(2)}, u32[]{:S(2)}) %collective-permute-start.10) | collective-permute-done | bytes 983072 | tf_op jit(solution)/shard_map/ppermute | solution.py:18
  105.4 0.3 collective-permute-start.11
  105.7 0.8 slice.89
  106.5 2.7 collective-permute-start.13
  109.1 1.2 constant_dynamic-update-slice_fusion.3
  110.3 8.4 %collective-permute-done.11 = bf16[4,2,15,16,128]{4,3,2,1,0:T(8,128)(2,1)S(1)} collective-permute-done((bf16[4,2,15,16,128]{4,3,2,1,0:T(8,128)(2,1)S(1)}, bf16[4,2,15,16,128]{4,3,2,1,0:T(8,128)(2,1)S(1)}, u32[]{:S(2)}, u32[]{:S(2)}) %collective-permute-start.11) | collective-permute-done | bytes 491552 | tf_op jit(solution)/shard_map/ppermute | solution.py:21
  118.8 0.1 collective-permute-done.13
  118.9 1.2 maximum_dynamic-update-slice_fusion.1
  120.1 1.2 constant_dynamic-update-slice_fusion.2
  121.3 2.0 collective-permute-start.21
  123.3 0.1 dynamic_slice.19
  123.4 0.1 select_reduce_fusion
  123.5 0.1 broadcast_compare_fusion
  123.6 0.8 broadcast_and_fusion
  124.4 1.7 broadcast_select_fusion
  126.2 1.4 collective-permute-start.15
  127.5 1.5 collective-permute-start.14
  129.1 42.9 %collective-permute-done.15 = bf16[8,2,15,32,128]{4,3,2,1,0:T(8,128)(2,1)S(1)} collective-permute-done((bf16[8,2,15,32,128]{4,3,2,1,0:T(8,128)(2,1)S(1)}, bf16[8,2,15,32,128]{4,3,2,1,0:T(8,128)(2,1)S(1)}, u32[]{:S(2)}, u32[]{:S(2)}) %collective-permute-start.15) | collective-permute-done | bytes 1966112 | tf_op jit(solution)/shard_map/ppermute | solution.py:91
  172.0 0.1 collective-permute-start.16
  172.2 2.9 %collective-permute-start.17 = (bf16[4,2,15,32,128]{4,3,2,1,0:T(8,128)(2,1)S(1)}, bf16[4,2,15,32,128]{4,3,2,1,0:T(8,128)(2,1)}, u32[]{:S(2)}, u32[]{:S(2)}) collective-permute-start(bf16[4,2,15,32,128]{4,3,2,1,0:T(8,128)(2,1)S(1)} %slice.93), channel_id=1, source_target_pairs={{0,12},{4,0},{8,4},{12,8},{1,13},{5,1},{9,5},{13,9},{2,14},{6,2},{... | collective-permute-start | bytes 2949128 | tf_op jit(solution)/shard_map/ppermute | solution.py:95
  175.2 2.4 fusion.2
  177.6 2.4 fusion.3
  180.0 15.9 %collective-permute-done.16 = bf16[4,2,15,32,128]{4,3,2,1,0:T(8,128)(2,1)S(1)} collective-permute-done((bf16[4,2,15,32,128]{4,3,2,1,0:T(8,128)(2,1)S(1)}, bf16[4,2,15,32,128]{4,3,2,1,0:T(8,128)(2,1)S(1)}, u32[]{:S(2)}, u32[]{:S(2)}) %collective-permute-start.16) | collective-permute-done | bytes 983072 | tf_op jit(solution)/shard_map/ppermute | solution.py:94
  195.9 2.7 fusion.1
  198.6 3.9 %bitcast_add_fusion = f32[8,2,128,2,128]{4,2,3,1,0:T(8,128)} fusion(f32[8,2,128,2,128,1]{4,2,5,3,1,0:T(8,128)S(1)} %fusion.1, f32[8,2,128,2,128,1]{4,2,5,3,1,0:T(8,128)S(1)} %fusion.2, f32[8,2,128,2,128,1]{4,2,5,3,1,0:T(8,128)S(1)} %fusion.3, bf16[8,2,15,128,128]{4,3,2,1,0:T(8,128)(2,1)} %collective-permute-done.21, ...), kind=kOutput, calls=%fused_computation | convolution fusion | flops 504889344 | bytes 12320768 | tf_op jit(solution)/shard_map/gikca,gjkcb->giajb/dot_general | solution.py:142
  202.6 2.7 fusion.5
  205.3 2.5 fusion.7
  207.8 2.6 fusion.6
  210.4 2.6 bitcast_add_fusion.3
  213.1 0.1 collective-permute-start.18
  213.2 23.3 %collective-permute-done.18 = f32[2,2,128,2,128]{4,2,3,1,0:T(8,128)S(1)} collective-permute-done((f32[2,2,128,2,128]{4,2,3,1,0:T(8,128)S(1)}, f32[2,2,128,2,128]{4,2,3,1,0:T(8,128)S(1)}, u32[]{:S(2)}, u32[]{:S(2)}) %collective-permute-start.18) | collective-permute-done | bytes 524320 | tf_op jit(solution)/shard_map/ppermute | solution.py:111
  236.6 0.1 collective-permute-start.19
  236.7 25.6 %collective-permute-done.19 = f32[2,2,128,2,128]{4,2,3,1,0:T(8,128)} collective-permute-done((f32[2,2,128,2,128]{4,2,3,1,0:T(8,128)S(1)}, f32[2,2,128,2,128]{4,2,3,1,0:T(8,128)}, u32[]{:S(2)}, u32[]{:S(2)}) %collective-permute-start.19) | collective-permute-done | bytes 524320 | tf_op jit(solution)/shard_map/ppermute | solution.py:111
  262.2 1.1 dynamic-slice_add_fusion.1
  263.3 0.1 collective-permute-start.20
  263.4 0.1 dynamic_slice.18
  263.5 0.1 iota_compare_fusion.2
  263.6 19.7 %collective-permute-done.20 = f32[2,2,128,2,128]{4,2,3,1,0:T(8,128)S(1)} collective-permute-done((f32[2,2,128,2,128]{4,2,3,1,0:T(8,128)S(1)}, f32[2,2,128,2,128]{4,2,3,1,0:T(8,128)S(1)}, u32[]{:S(2)}, u32[]{:S(2)}) %collective-permute-start.20) | collective-permute-done | bytes 524320 | tf_op jit(solution)/shard_map/ppermute | solution.py:111
  283.3 1.4 fusion.19
  284.7 1.2 copy.6
  (41 shorter events, 0.8 us)
Async XLA Ops:
  6.5 4.6 %copy-start.4 = (bf16[8,4,15,8,128]{4,3,2,1,0:T(8,128)(2,1)S(1)}, bf16[8,4,15,8,128]{4,3,2,1,0:T(8,128)(2,1)}, u32[]{:S(2)}) copy-start(bf16[8,4,15,8,128]{4,3,2,1,0:T(8,128)(2,1)} %param.5) | copy-start | bytes 2949124
  6.5 276.8 %reduce-scatter.2.cloned.1.call-start = ((), (), s32[]{:S(2)}) async-start(), calls=%async_computation.1 | async-start | bytes 2621440 | tf_op jit(solution)/shard_map/reduce_scatter | solution.py:152
  7.9 4.8 %collective-permute-start = (bf16[8,2,15,8,128]{4,3,2,1,0:T(8,128)(2,1)S(1)}, bf16[8,2,15,8,128]{4,3,2,1,0:T(8,128)(2,1)S(1)}, u32[]{:S(2)}, u32[]{:S(2)}) collective-permute-start(bf16[8,2,15,8,128]{4,3,2,1,0:T(8,128)(2,1)S(1)} %get-tuple-element.13), channel_id=1, source_target_pairs={{0,16},{16,0},{32,48},{48,32},{64,80},{80,64},{96,112},{112,96},{1... | collective-permute-start | bytes 1474568 | tf_op jit(solution)/shard_map/ppermute | solution.py:30
  11.2 20.2 %collective-permute-start.5 = (bf16[4,4,15,8,128]{4,3,2,1,0:T(8,128)(2,1)S(1)}, bf16[4,4,15,8,128]{4,3,2,1,0:T(8,128)(2,1)}, u32[]{:S(2)}, u32[]{:S(2)}) collective-permute-start(bf16[4,4,15,8,128]{4,3,2,1,0:T(8,128)(2,1)S(1)} %get-tuple-element.12), channel_id=1, source_target_pairs={{0,2},{1,3},{2,32},{3,33},{16,18},{17,19},{18,48},{19,49},{32,34},... | collective-permute-start | bytes 1474568 | tf_op jit(solution)/shard_map/ppermute | solution.py:54
  19.2 38.3 %collective-permute-start.1 = (bf16[8,2,15,16,128]{4,3,2,1,0:T(8,128)(2,1)S(1)}, bf16[8,2,15,16,128]{4,3,2,1,0:T(8,128)(2,1)S(1)}, u32[]{:S(2)}, u32[]{:S(2)}) collective-permute-start(bf16[8,2,15,16,128]{4,3,2,1,0:T(8,128)(2,1)S(1)} %get-tuple-element.8), channel_id=1, source_target_pairs={{0,64},{16,80},{32,96},{48,112},{64,128},{80,144},{96,160},{112,17... | collective-permute-start | bytes 2949128 | tf_op jit(solution)/shard_map/ppermute | solution.py:18
  20.5 38.4 %collective-permute-start.3 = (bf16[8,2,15,16,128]{4,3,2,1,0:T(8,128)(2,1)S(1)}, bf16[8,2,15,16,128]{4,3,2,1,0:T(8,128)(2,1)S(1)}, u32[]{:S(2)}, u32[]{:S(2)}) collective-permute-start(bf16[8,2,15,16,128]{4,3,2,1,0:T(8,128)(2,1)S(1)} %get-tuple-element.8), channel_id=1, source_target_pairs={{0,192},{16,208},{32,224},{48,240},{64,0},{80,16},{96,32},{112,48}... | collective-permute-start | bytes 2949128 | tf_op jit(solution)/shard_map/ppermute | solution.py:19
  21.9 26.6 %collective-permute-start.7 = (bf16[4,4,15,8,128]{4,3,2,1,0:T(8,128)(2,1)S(1)}, bf16[4,4,15,8,128]{4,3,2,1,0:T(8,128)(2,1)S(1)}, u32[]{:S(2)}, u32[]{:S(2)}) collective-permute-start(bf16[4,4,15,8,128]{4,3,2,1,0:T(8,128)(2,1)S(1)} %get-tuple-element.11), channel_id=1, source_target_pairs={{0,34},{1,35},{2,0},{3,1},{16,50},{17,51},{18,16},{19,17},{32,2},{... | collective-permute-start | bytes 1474568 | tf_op jit(solution)/shard_map/ppermute | solution.py:55
  31.4 26.1 %collective-permute-start.6 = (bf16[4,4,15,8,128]{4,3,2,1,0:T(8,128)(2,1)}, bf16[4,4,15,8,128]{4,3,2,1,0:T(8,128)(2,1)S(1)}, u32[]{:S(2)}, u32[]{:S(2)}) collective-permute-start(bf16[4,4,15,8,128]{4,3,2,1,0:T(8,128)(2,1)} %collective-permute-done.5), channel_id=1, source_target_pairs={{0,2},{1,3},{2,32},{3,33},{16,18},{17,19},{18,48},{19,49},{32,34},... | collective-permute-start | bytes 1474568 | tf_op jit(solution)/shard_map/ppermute | solution.py:56
  48.5 23.7 %collective-permute-start.8 = (bf16[4,4,15,8,128]{4,3,2,1,0:T(8,128)(2,1)S(1)}, bf16[4,4,15,8,128]{4,3,2,1,0:T(8,128)(2,1)S(1)}, u32[]{:S(2)}, u32[]{:S(2)}) collective-permute-start(bf16[4,4,15,8,128]{4,3,2,1,0:T(8,128)(2,1)S(1)} %collective-permute-done.7), channel_id=1, source_target_pairs={{0,34},{1,35},{2,0},{3,1},{16,50},{17,51},{18,16},{19,17},{32,2},{... | collective-permute-start | bytes 1474568 | tf_op jit(solution)/shard_map/ppermute | solution.py:57
  57.6 17.1 %collective-permute-start.2 = (bf16[4,2,15,16,128]{4,3,2,1,0:T(8,128)(2,1)S(1)}, bf16[4,2,15,16,128]{4,3,2,1,0:T(8,128)(2,1)S(1)}, u32[]{:S(2)}, u32[]{:S(2)}) collective-permute-start(bf16[4,2,15,16,128]{4,3,2,1,0:T(8,128)(2,1)S(1)} %slice.84), channel_id=1, source_target_pairs={{0,64},{16,80},{32,96},{48,112},{64,128},{80,144},{96,160},{112,17... | collective-permute-start | bytes 1474568 | tf_op jit(solution)/shard_map/ppermute | solution.py:21
  59.7 15.0 %collective-permute-start.4 = (bf16[4,2,15,16,128]{4,3,2,1,0:T(8,128)(2,1)}, bf16[4,2,15,16,128]{4,3,2,1,0:T(8,128)(2,1)}, u32[]{:S(2)}, u32[]{:S(2)}) collective-permute-start(bf16[4,2,15,16,128]{4,3,2,1,0:T(8,128)(2,1)} %slice.85), channel_id=1, source_target_pairs={{0,192},{16,208},{32,224},{48,240},{64,0},{80,16},{96,32},{112,48}... | collective-permute-start | bytes 1474568 | tf_op jit(solution)/shard_map/ppermute | solution.py:22
  73.1 5.2 %collective-permute-start.9 = (bf16[8,2,15,8,128]{4,3,2,1,0:T(8,128)(2,1)}, bf16[8,2,15,8,128]{4,3,2,1,0:T(8,128)(2,1)}, u32[]{:S(2)}, u32[]{:S(2)}) collective-permute-start(bf16[8,2,15,8,128]{4,3,2,1,0:T(8,128)(2,1)} %get-tuple-element.9), channel_id=1, source_target_pairs={{0,16},{16,0},{32,48},{48,32},{64,80},{80,64},{96,112},{112,96},{1... | collective-permute-start | bytes 1474568 | tf_op jit(solution)/shard_map/ppermute | solution.py:30
  80.8 24.5 %collective-permute-start.10 = (bf16[8,2,15,16,128]{4,3,2,1,0:T(8,128)(2,1)S(1)}, bf16[8,2,15,16,128]{4,3,2,1,0:T(8,128)(2,1)S(1)}, u32[]{:S(2)}, u32[]{:S(2)}) collective-permute-start(bf16[8,2,15,16,128]{4,3,2,1,0:T(8,128)(2,1)S(1)} %get-tuple-element.6), channel_id=1, source_target_pairs={{0,64},{16,80},{32,96},{48,112},{64,128},{80,144},{96,160},{112,17... | collective-permute-start | bytes 2949128 | tf_op jit(solution)/shard_map/ppermute | solution.py:18
  80.8 24.8 %collective-permute-start.12 = (bf16[8,2,15,16,128]{4,3,2,1,0:T(8,128)(2,1)S(1)}, bf16[8,2,15,16,128]{4,3,2,1,0:T(8,128)(2,1)S(1)}, u32[]{:S(2)}, u32[]{:S(2)}) collective-permute-start(bf16[8,2,15,16,128]{4,3,2,1,0:T(8,128)(2,1)S(1)} %get-tuple-element.6), channel_id=1, source_target_pairs={{0,192},{16,208},{32,224},{48,240},{64,0},{80,16},{96,32},{112,48}... | collective-permute-start | bytes 2949128 | tf_op jit(solution)/shard_map/ppermute | solution.py:19
  105.4 13.4 %collective-permute-start.11 = (bf16[4,2,15,16,128]{4,3,2,1,0:T(8,128)(2,1)S(1)}, bf16[4,2,15,16,128]{4,3,2,1,0:T(8,128)(2,1)S(1)}, u32[]{:S(2)}, u32[]{:S(2)}) collective-permute-start(bf16[4,2,15,16,128]{4,3,2,1,0:T(8,128)(2,1)S(1)} %slice.88), channel_id=1, source_target_pairs={{0,64},{16,80},{32,96},{48,112},{64,128},{80,144},{96,160},{112,17... | collective-permute-start | bytes 1474568 | tf_op jit(solution)/shard_map/ppermute | solution.py:21
  106.5 12.4 %collective-permute-start.13 = (bf16[4,2,15,16,128]{4,3,2,1,0:T(8,128)(2,1)}, bf16[4,2,15,16,128]{4,3,2,1,0:T(8,128)(2,1)S(1)}, u32[]{:S(2)}, u32[]{:S(2)}) collective-permute-start(bf16[4,2,15,16,128]{4,3,2,1,0:T(8,128)(2,1)} %slice.89), channel_id=1, source_target_pairs={{0,192},{16,208},{32,224},{48,240},{64,0},{80,16},{96,32},{112,48}... | collective-permute-start | bytes 1474568 | tf_op jit(solution)/shard_map/ppermute | solution.py:22
  110.3 12.9 %copy-start.6 = (s32[60]{0:T(128)S(1)}, s32[60]{0:T(128)}, u32[]{:S(2)}) copy-start(s32[60]{0:T(128)} %param.7) | copy-start | bytes 724
  110.3 13.0 %copy-start.5 = (s32[8]{0:T(128)S(1)}, s32[8]{0:T(128)}, u32[]{:S(2)}) copy-start(s32[8]{0:T(128)} %param.6) | copy-start | bytes 100
  121.3 53.9 %collective-permute-start.21 = (bf16[8,2,15,128,128]{4,3,2,1,0:T(8,128)(2,1)}, bf16[8,2,15,128,128]{4,3,2,1,0:T(8,128)(2,1)}, u32[]{:S(2)}, u32[]{:S(2)}) collective-permute-start(bf16[8,2,15,128,128]{4,3,2,1,0:T(8,128)(2,1)} %constant_dynamic-update-slice_fusion.2), channel_id=1, source_target_pairs={{0,16},{16,0},{32,48},{48,32},{64,80},{80,64},{96,112},{112,96},{1... | collective-permute-start | bytes 23592968 | tf_op jit(solution)/shard_map/ppermute | solution.py:82
  126.2 45.8 %collective-permute-start.15 = (bf16[8,2,15,32,128]{4,3,2,1,0:T(8,128)(2,1)S(1)}, bf16[8,2,15,32,128]{4,3,2,1,0:T(8,128)(2,1)S(1)}, u32[]{:S(2)}, u32[]{:S(2)}) collective-permute-start(bf16[8,2,15,32,128]{4,3,2,1,0:T(8,128)(2,1)S(1)} %broadcast_select_fusion), channel_id=1, source_target_pairs={{0,4},{4,8},{8,12},{12,0},{1,5},{5,9},{9,13},{13,1},{2,6},{6,10},{... | collective-permute-start | bytes 5898248 | tf_op jit(solution)/shard_map/ppermute | solution.py:91
  127.5 44.6 %collective-permute-start.14 = (bf16[8,2,15,32,128]{4,3,2,1,0:T(8,128)(2,1)S(1)}, bf16[8,2,15,32,128]{4,3,2,1,0:T(8,128)(2,1)S(1)}, u32[]{:S(2)}, u32[]{:S(2)}) collective-permute-start(bf16[8,2,15,32,128]{4,3,2,1,0:T(8,128)(2,1)S(1)} %broadcast_select_fusion), channel_id=1, source_target_pairs={{0,12},{4,0},{8,4},{12,8},{1,13},{5,1},{9,5},{13,9},{2,14},{6,2},{... | collective-permute-start | bytes 5898248 | tf_op jit(solution)/shard_map/ppermute | solution.py:92
  172.0 26.6 %copy-start = (bf16[8,2,15,32,128]{4,3,2,1,0:T(8,128)(2,1)}, bf16[8,2,15,32,128]{4,3,2,1,0:T(8,128)(2,1)S(1)}, u32[]{:S(2)}) copy-start(bf16[8,2,15,32,128]{4,3,2,1,0:T(8,128)(2,1)S(1)} %collective-permute-done.15) | copy-start | bytes 5898244
  172.0 23.8 %collective-permute-start.16 = (bf16[4,2,15,32,128]{4,3,2,1,0:T(8,128)(2,1)S(1)}, bf16[4,2,15,32,128]{4,3,2,1,0:T(8,128)(2,1)S(1)}, u32[]{:S(2)}, u32[]{:S(2)}) collective-permute-start(bf16[4,2,15,32,128]{4,3,2,1,0:T(8,128)(2,1)S(1)} %slice.92), channel_id=1, source_target_pairs={{0,4},{4,8},{8,12},{12,0},{1,5},{5,9},{9,13},{13,1},{2,6},{6,10},{... | collective-permute-start | bytes 2949128 | tf_op jit(solution)/shard_map/ppermute | solution.py:94
  172.1 5.4 %copy-start.2 = (bf16[8,2,15,32,128]{4,3,2,1,0:T(8,128)(2,1)}, bf16[8,2,15,32,128]{4,3,2,1,0:T(8,128)(2,1)S(1)}, u32[]{:S(2)}) copy-start(bf16[8,2,15,32,128]{4,3,2,1,0:T(8,128)(2,1)S(1)} %collective-permute-done.14) | copy-start | bytes 5898244
  172.2 23.6 %collective-permute-start.17 = (bf16[4,2,15,32,128]{4,3,2,1,0:T(8,128)(2,1)S(1)}, bf16[4,2,15,32,128]{4,3,2,1,0:T(8,128)(2,1)}, u32[]{:S(2)}, u32[]{:S(2)}) collective-permute-start(bf16[4,2,15,32,128]{4,3,2,1,0:T(8,128)(2,1)S(1)} %slice.93), channel_id=1, source_target_pairs={{0,12},{4,0},{8,4},{12,8},{1,13},{5,1},{9,5},{13,9},{2,14},{6,2},{... | collective-permute-start | bytes 2949128 | tf_op jit(solution)/shard_map/ppermute | solution.py:95
  205.3 2.5 copy-start.3
  207.8 2.6 copy-start.1
  213.1 23.4 %collective-permute-start.18 = (f32[2,2,128,2,128]{4,2,3,1,0:T(8,128)S(1)}, f32[2,2,128,2,128]{4,2,3,1,0:T(8,128)S(1)}, u32[]{:S(2)}, u32[]{:S(2)}) collective-permute-start(f32[2,2,128,2,128]{4,2,3,1,0:T(8,128)S(1)} %constant_dynamic-slice_fusion), channel_id=1, source_target_pairs={{0,1},{1,2},{2,3},{3,0},{4,5},{5,6},{6,7},{7,4},{8,9},{9,10},{10,1... | collective-permute-start | bytes 1572872 | tf_op jit(solution)/shard_map/ppermute | solution.py:111
  236.6 25.7 %collective-permute-start.19 = (f32[2,2,128,2,128]{4,2,3,1,0:T(8,128)S(1)}, f32[2,2,128,2,128]{4,2,3,1,0:T(8,128)}, u32[]{:S(2)}, u32[]{:S(2)}) collective-permute-start(f32[2,2,128,2,128]{4,2,3,1,0:T(8,128)S(1)} %dynamic-slice_add_fusion.2), channel_id=1, source_target_pairs={{0,1},{1,2},{2,3},{3,0},{4,5},{5,6},{6,7},{7,4},{8,9},{9,10},{10,1... | collective-permute-start | bytes 1572872 | tf_op jit(solution)/shard_map/ppermute | solution.py:111
  263.3 19.9 %collective-permute-start.20 = (f32[2,2,128,2,128]{4,2,3,1,0:T(8,128)S(1)}, f32[2,2,128,2,128]{4,2,3,1,0:T(8,128)S(1)}, u32[]{:S(2)}, u32[]{:S(2)}) collective-permute-start(f32[2,2,128,2,128]{4,2,3,1,0:T(8,128)S(1)} %dynamic-slice_add_fusion.1), channel_id=1, source_target_pairs={{0,1},{1,2},{2,3},{3,0},{4,5},{5,6},{6,7},{7,4},{8,9},{9,10},{10,1... | collective-permute-start | bytes 1572872 | tf_op jit(solution)/shard_map/ppermute | solution.py:111
Sparse Core Ops, SparseCore 0:
  202.7 73.7 reduce-scatter.1

commit v8 on v6

--- a/solution.py
+++ b/solution.py
@@ -41,19 +41,24 @@
     core = r % 2
     ng, nj, nk, ncc, nb = t_part.shape
     hj = nj // 2
-    t_zh = lax.ppermute(t_part, "row", [(i, i ^ 2) for i in range(nrow)])
+    hg = ng // 2
+    swap = [(i, i ^ 2) for i in range(nrow)]
+    zh_lo = lax.ppermute(t_part[:hg], "row", swap)
+    zh_hi = lax.ppermute(t_part[hg:], "row", swap)
     own = ring4_pieces(core_quad(t_part, core, nrow, hj), "row", nrow, 4)
     pos = x - cl
     mine = jnp.zeros((ng, hj, nk, 16 * ncc, nb), t_part.dtype)
-    for step, piece in enumerate(own):
+    for step in (1, 2, 3, 0):
+        piece = own[step]
         mine = lax.dynamic_update_slice_in_dim(
             mine, piece, ((pos - step) % 4) * 4 * ncc + zh * 2 * ncc, axis=3
         )
-    far = ring4_pieces(core_quad(t_zh, core, nrow, hj), "row", nrow, 4)
-    for step, piece in enumerate(far):
-        mine = lax.dynamic_update_slice_in_dim(
-            mine, piece, ((pos - step) % 4) * 4 * ncc + (1 - zh) * 2 * ncc, axis=3
-        )
+    for goff, zpart in ((0, zh_lo), (hg, zh_hi)):
+        far = ring4_pieces(core_quad(zpart, core, nrow, hj), "row", nrow, 4)
+        for step, piece in enumerate(far):
+            mine = lax.dynamic_update_slice(
+                mine, piece, (goff, 0, 0, ((pos - step) % 4) * 4 * ncc + (1 - zh) * 2 * ncc, 0)
+            )
     other = lax.ppermute(mine, "row", [(i, i ^ 1) for i in range(nrow)])
     return mine, other
 

time: 294 us -> 287 us (0.976)
  waiting for transfers between devices: 169 us -> 146 us
  starting transfers between devices: 57.7 us -> 70.1 us
    ppermute x2 -> x3, waiting for transfers between devices: 21.1 us -> 2.97 us  [ring4_pieces(): from_right = lax.ppermute(block, axis, bwd)]
    ppermute x2 -> x3, starting transfers between devices: 17.1 us -> 8.03 us  [ring4_pieces(): from_right = lax.ppermute(block, axis, bwd)]
    ppermute x2 -> x3, waiting for transfers between devices: 16.3 us -> 24.8 us  [ring4_pieces(): from_left = lax.ppermute(block, axis, fwd)]
    ppermute x3, starting transfers between devices: 15 us -> 22.9 us  [ring_reduce_scatter(): acc = lax.ppermute(acc, 'rep', fwd) + chunk(d + 2 * n - step - 1)]
    ppermute x2 -> x3, waiting for transfers between devices: 7.71 us -> 0.77 us  [ring4_pieces(): opp_hi = lax.ppermute(from_right[half:], axis, bwd)]
    ppermute x1 -> x2, starting transfers between devices: 5.14 us -> 10.5 us  [the longest x1 5.25 us: gather_amplitudes(): zh_hi = lax.ppermute(t_part[hg:], 'row', swap)]
    dynamic_update_slice x4 -> x1, other arithmetic: 6.43 us -> 2.27 us  [gather_amplitudes(): lax.dynamic_update_slice_in_dim(mine, piece, (pos - step) % 4 * 4 * ncc +...]
    dynamic_update_slice x0 -> x4, other arithmetic: none -> 3.94 us  [gather_amplitudes(): lax.dynamic_update_slice(mine, piece, (goff, 0, 0, (pos - step) % 4 * 4 *...]
  transfers between devices with their start and end apart: 20 -> 26, of which waited for: 11 -> 13; matrix products, arithmetic and copies ran while one was open for 10% -> 13% of each run, Pallas kernels for 0% -> 0%
where the time goes in v8:
time: 287 us; the launch traced here: 283 us
  waiting for transfers between devices  146 us (51%)
  starting transfers between devices  70.1 us (24%)
  matrix products  21.6 us (8%)
  local copies, waits for them, and re-layouts  17.6 us (6%)
  between operations  13.7 us (5%)
  other arithmetic  13.5 us (5%)
    ppermute x3, waiting for transfers between devices, ring_reduce_scatter(): acc = lax.ppermute(acc, 'rep', fwd) + chunk(d + 2 * n - step - 1)  50 us
    ppermute x1, waiting for transfers between devices, gather_integrals(): from_left = lax.ppermute(w, 'col', fwd)  43.1 us
    ppermute x3, waiting for transfers between devices, ring4_pieces(): from_left = lax.ppermute(block, axis, fwd)  24.8 us
    ppermute x3, starting transfers between devices, ring_reduce_scatter(): acc = lax.ppermute(acc, 'rep', fwd) + chunk(d + 2 * n - step - 1)  22.9 us
    dot_general x8, matrix products, body(): jnp.einsum('gikca,gjkcb->giajb', w_blk, t_half[:, :, :, s * width:(s + 1)...  21.6 us
    ppermute x1, waiting for transfers between devices, gather_integrals(): opp_lo = lax.ppermute(from_left[:half], 'col', fwd)  16 us
    ppermute x3, starting transfers between devices, core_quad(): got = lax.ppermute(send, 'row', [(i, i ^ 1) for i in range(nrow)])  10.2 us
    ppermute x3, starting transfers between devices, ring4_pieces(): opp_hi = lax.ppermute(from_right[half:], axis, bwd)  8.52 us
  transfers between devices with their start and end apart: 26, of which 13 were waited for; matrix products, arithmetic and copies ran while one was open for 13% of the time, Pallas kernels for 0%

profile of v8, /device:TPU:1, one launch (start us, length us, event | category | flops | bytes accessed | tf_op | source)
XLA Modules:
  0.0 283.0 jit_solution(16889571114043264200)
XLA Ops:
  6.5 1.3 broadcast_select_fusion.2
  7.9 3.3 %collective-permute-start = (bf16[8,2,15,8,128]{4,3,2,1,0:T(8,128)(2,1)S(1)}, bf16[8,2,15,8,128]{4,3,2,1,0:T(8,128)(2,1)S(1)}, u32[]{:S(2)}, u32[]{:S(2)}) collective-permute-start(bf16[8,2,15,8,128]{4,3,2,1,0:T(8,128)(2,1)S(1)} %get-tuple-element.12), channel_id=1, source_target_pairs={{0,16},{16,0},{32,48},{48,32},{64,80},{80,64},{96,112},{112,96},{1... | collective-permute-start | bytes 1474568 | tf_op jit(solution)/shard_map/ppermute | solution.py:30
  11.2 1.5 collective-permute-done
  12.7 0.4 maximum_select_fusion.1
  13.0 0.1 collective-permute-start.1
  13.1 2.7 collective-permute-start.3
  15.8 1.1 fusion.22
  16.9 5.2 %collective-permute-start.5 = (bf16[4,4,15,8,128]{4,3,2,1,0:T(8,128)(2,1)}, bf16[4,4,15,8,128]{4,3,2,1,0:T(8,128)(2,1)S(1)}, u32[]{:S(2)}, u32[]{:S(2)}) collective-permute-start(bf16[4,4,15,8,128]{4,3,2,1,0:T(8,128)(2,1)} %get-tuple-element.10), channel_id=1, source_target_pairs={{0,32},{16,48},{32,0},{48,16},{64,96},{80,112},{96,64},{112,80},{1... | collective-permute-start | bytes 1474568 | tf_op jit(solution)/shard_map/ppermute | solution.py:46
  22.1 15.2 %collective-permute-done.1 = bf16[8,2,15,16,128]{4,3,2,1,0:T(8,128)(2,1)S(1)} collective-permute-done((bf16[8,2,15,16,128]{4,3,2,1,0:T(8,128)(2,1)S(1)}, bf16[8,2,15,16,128]{4,3,2,1,0:T(8,128)(2,1)S(1)}, u32[]{:S(2)}, u32[]{:S(2)}) %collective-permute-start.1) | collective-permute-done | bytes 983072 | tf_op jit(solution)/shard_map/ppermute | solution.py:18
  37.4 0.8 copy-done.5
  38.2 0.8 slice.103
  39.0 1.8 collective-permute-start.4
  40.9 1.9 collective-permute-start.6
  42.8 5.1 %broadcast_in_dim.56 = bf16[8,2,15,128,128]{4,3,2,1,0:T(8,128)(2,1)} broadcast(bf16[]{:T(256)} %constant.139.clone.1), dimensions={} | broadcast | bytes 7864322 | tf_op jit(solution)/shard_map/broadcast_in_dim | solution.py:50
  47.9 1.2 constant_dynamic-update-slice_fusion.8
  49.0 1.1 collective-permute-done.2
  50.1 0.8 collective-permute-done.4
  50.9 2.3 maximum_dynamic-update-slice_fusion
  53.2 1.2 constant_dynamic-update-slice_fusion.7
  54.4 1.2 constant_dynamic-update-slice_fusion.6
  55.6 1.0 constant_dynamic-update-slice_fusion.5
  56.6 2.7 collective-permute-start.9
  59.3 5.2 %collective-permute-start.11 = (bf16[4,4,15,8,128]{4,3,2,1,0:T(8,128)(2,1)S(1)}, bf16[4,4,15,8,128]{4,3,2,1,0:T(8,128)(2,1)S(1)}, u32[]{:S(2)}, u32[]{:S(2)}) collective-permute-start(bf16[4,4,15,8,128]{4,3,2,1,0:T(8,128)(2,1)S(1)} %copy-done.7), channel_id=1, source_target_pairs={{0,32},{16,48},{32,0},{48,16},{64,96},{80,112},{96,64},{112,80},{1... | collective-permute-start | bytes 1474568 | tf_op jit(solution)/shard_map/ppermute | solution.py:47
  64.5 3.0 %collective-permute-done.9 = bf16[4,2,15,16,128]{4,3,2,1,0:T(8,128)(2,1)S(1)} collective-permute-done((bf16[4,2,15,16,128]{4,3,2,1,0:T(8,128)(2,1)S(1)}, bf16[4,2,15,16,128]{4,3,2,1,0:T(8,128)(2,1)S(1)}, u32[]{:S(2)}, u32[]{:S(2)}) %collective-permute-start.9) | collective-permute-done | bytes 491552 | tf_op jit(solution)/shard_map/ppermute | solution.py:19
  67.5 3.5 %collective-permute-start.10 = (bf16[2,2,15,16,128]{4,3,2,1,0:T(8,128)(2,1)S(1)}, bf16[2,2,15,16,128]{4,3,2,1,0:T(8,128)(2,1)S(1)}, u32[]{:S(2)}, u32[]{:S(2)}) collective-permute-start(bf16[2,2,15,16,128]{4,3,2,1,0:T(8,128)(2,1)S(1)} %slice.107), channel_id=1, source_target_pairs={{0,192},{16,208},{32,224},{48,240},{64,0},{80,16},{96,32},{112,48}... | collective-permute-start | bytes 737288 | tf_op jit(solution)/shard_map/ppermute | solution.py:22
  71.1 3.2 %collective-permute-done.11 = bf16[4,4,15,8,128]{4,3,2,1,0:T(8,128)(2,1)S(1)} collective-permute-done((bf16[4,4,15,8,128]{4,3,2,1,0:T(8,128)(2,1)S(1)}, bf16[4,4,15,8,128]{4,3,2,1,0:T(8,128)(2,1)S(1)}, u32[]{:S(2)}, u32[]{:S(2)}) %collective-permute-start.11) | collective-permute-done | bytes 491552 | tf_op jit(solution)/shard_map/ppermute | solution.py:47
  74.4 5.0 %collective-permute-start.12 = (bf16[4,2,15,8,128]{4,3,2,1,0:T(8,128)(2,1)S(1)}, bf16[4,2,15,8,128]{4,3,2,1,0:T(8,128)(2,1)S(1)}, u32[]{:S(2)}, u32[]{:S(2)}) collective-permute-start(bf16[4,2,15,8,128]{4,3,2,1,0:T(8,128)(2,1)S(1)} %get-tuple-element.13), channel_id=1, source_target_pairs={{0,16},{16,0},{32,48},{48,32},{64,80},{80,64},{96,112},{112,96},{1... | collective-permute-start | bytes 737288 | tf_op jit(solution)/shard_map/ppermute | solution.py:30
  79.4 0.9 constant_dynamic-update-slice_fusion.4
  80.3 0.9 maximum_dynamic-update-slice_fusion.1
  81.2 0.9 constant_dynamic-update-slice_fusion.3
  82.2 1.1 constant_dynamic-update-slice_fusion.2
  83.2 2.7 collective-permute-start.15
  85.9 9.6 %collective-permute-done.13 = bf16[4,2,15,16,128]{4,3,2,1,0:T(8,128)(2,1)S(1)} collective-permute-done((bf16[4,2,15,16,128]{4,3,2,1,0:T(8,128)(2,1)S(1)}, bf16[4,2,15,16,128]{4,3,2,1,0:T(8,128)(2,1)S(1)}, u32[]{:S(2)}, u32[]{:S(2)}) %collective-permute-start.13) | collective-permute-done | bytes 491552 | tf_op jit(solution)/shard_map/ppermute | solution.py:18
  95.7 3.2 %collective-permute-start.16 = (bf16[2,2,15,16,128]{4,3,2,1,0:T(8,128)(2,1)S(1)}, bf16[2,2,15,16,128]{4,3,2,1,0:T(8,128)(2,1)S(1)}, u32[]{:S(2)}, u32[]{:S(2)}) collective-permute-start(bf16[2,2,15,16,128]{4,3,2,1,0:T(8,128)(2,1)S(1)} %slice.111), channel_id=1, source_target_pairs={{0,192},{16,208},{32,224},{48,240},{64,0},{80,16},{96,32},{112,48}... | collective-permute-start | bytes 737288 | tf_op jit(solution)/shard_map/ppermute | solution.py:22
  98.9 0.9 constant_dynamic-update-slice_fusion.1
  99.8 2.9 %collective-permute-done.14 = bf16[2,2,15,16,128]{4,3,2,1,0:T(8,128)(2,1)S(1)} collective-permute-done((bf16[2,2,15,16,128]{4,3,2,1,0:T(8,128)(2,1)S(1)}, bf16[2,2,15,16,128]{4,3,2,1,0:T(8,128)(2,1)S(1)}, u32[]{:S(2)}, u32[]{:S(2)}) %collective-permute-start.14) | collective-permute-done | bytes 245792 | tf_op jit(solution)/shard_map/ppermute | solution.py:21
  102.7 0.9 maximum_dynamic-update-slice_fusion.2
  103.7 0.9 constant_dynamic-update-slice_fusion
  104.6 2.9 %collective-permute-start.24 = (bf16[8,2,15,128,128]{4,3,2,1,0:T(8,128)(2,1)}, bf16[8,2,15,128,128]{4,3,2,1,0:T(8,128)(2,1)}, u32[]{:S(2)}, u32[]{:S(2)}) collective-permute-start(bf16[8,2,15,128,128]{4,3,2,1,0:T(8,128)(2,1)} %constant_dynamic-update-slice_fusion), channel_id=1, source_target_pairs={{0,16},{16,0},{32,48},{48,32},{64,80},{80,64},{96,112},{112,96},{1... | collective-permute-start | bytes 23592968 | tf_op jit(solution)/shard_map/ppermute | solution.py:62
  107.9 0.8 broadcast_and_fusion
  108.6 1.7 broadcast_select_fusion
  110.4 2.4 collective-permute-start.18
  112.8 1.3 collective-permute-start.17
  114.1 43.1 %collective-permute-done.18 = bf16[8,2,15,32,128]{4,3,2,1,0:T(8,128)(2,1)S(1)} collective-permute-done((bf16[8,2,15,32,128]{4,3,2,1,0:T(8,128)(2,1)S(1)}, bf16[8,2,15,32,128]{4,3,2,1,0:T(8,128)(2,1)S(1)}, u32[]{:S(2)}, u32[]{:S(2)}) %collective-permute-start.18) | collective-permute-done | bytes 1966112 | tf_op jit(solution)/shard_map/ppermute | solution.py:71
  157.5 2.9 %collective-permute-start.20 = (bf16[4,2,15,32,128]{4,3,2,1,0:T(8,128)(2,1)S(1)}, bf16[4,2,15,32,128]{4,3,2,1,0:T(8,128)(2,1)S(1)}, u32[]{:S(2)}, u32[]{:S(2)}) collective-permute-start(bf16[4,2,15,32,128]{4,3,2,1,0:T(8,128)(2,1)S(1)} %slice.115), channel_id=1, source_target_pairs={{0,12},{4,0},{8,4},{12,8},{1,13},{5,1},{9,5},{13,9},{2,14},{6,2},{... | collective-permute-start | bytes 2949128 | tf_op jit(solution)/shard_map/ppermute | solution.py:75
  160.4 2.4 fusion.2
  162.9 2.4 fusion.3
  165.3 16.0 %collective-permute-done.19 = bf16[4,2,15,32,128]{4,3,2,1,0:T(8,128)(2,1)S(1)} collective-permute-done((bf16[4,2,15,32,128]{4,3,2,1,0:T(8,128)(2,1)S(1)}, bf16[4,2,15,32,128]{4,3,2,1,0:T(8,128)(2,1)S(1)}, u32[]{:S(2)}, u32[]{:S(2)}) %collective-permute-start.19) | collective-permute-done | bytes 983072 | tf_op jit(solution)/shard_map/ppermute | solution.py:74
  181.3 1.0 copy-done.9
  182.3 2.4 fusion.1
  184.7 3.9 %bitcast_add_fusion = f32[8,2,128,2,128]{4,2,3,1,0:T(8,128)} fusion(f32[8,2,128,2,128,1]{4,2,5,3,1,0:T(8,128)S(1)} %fusion.1, f32[8,2,128,2,128,1]{4,2,5,3,1,0:T(8,128)S(1)} %fusion.2, f32[8,2,128,2,128,1]{4,2,5,3,1,0:T(8,128)S(1)} %fusion.3, bf16[8,2,15,128,128]{4,3,2,1,0:T(8,128)(2,1)} %collective-permute-done.24, ...), kind=kOutput, calls=%fused_computation | convolution fusion | flops 504889344 | bytes 12320768 | tf_op jit(solution)/shard_map/gikca,gjkcb->giajb/dot_general | solution.py:122
  188.7 2.7 fusion.5
  191.4 2.6 fusion.7
  194.0 2.6 fusion.6
  196.6 2.6 bitcast_add_fusion.3
  199.3 9.0 %collective-permute-start.21 = (f32[2,2,128,2,128]{4,2,3,1,0:T(8,128)S(1)}, f32[2,2,128,2,128]{4,2,3,1,0:T(8,128)S(1)}, u32[]{:S(2)}, u32[]{:S(2)}) collective-permute-start(f32[2,2,128,2,128]{4,2,3,1,0:T(8,128)S(1)} %constant_dynamic-slice_fusion), channel_id=1, source_target_pairs={{0,1},{1,2},{2,3},{3,0},{4,5},{5,6},{6,7},{7,4},{8,9},{9,10},{10,1... | collective-permute-start | bytes 1572872 | tf_op jit(solution)/shard_map/ppermute | solution.py:91
  208.2 17.5 %collective-permute-done.21 = f32[2,2,128,2,128]{4,2,3,1,0:T(8,128)S(1)} collective-permute-done((f32[2,2,128,2,128]{4,2,3,1,0:T(8,128)S(1)}, f32[2,2,128,2,128]{4,2,3,1,0:T(8,128)S(1)}, u32[]{:S(2)}, u32[]{:S(2)}) %collective-permute-start.21) | collective-permute-done | bytes 524320 | tf_op jit(solution)/shard_map/ppermute | solution.py:91
  225.8 5.4 %collective-permute-start.22 = (f32[2,2,128,2,128]{4,2,3,1,0:T(8,128)S(1)}, f32[2,2,128,2,128]{4,2,3,1,0:T(8,128)}, u32[]{:S(2)}, u32[]{:S(2)}) collective-permute-start(f32[2,2,128,2,128]{4,2,3,1,0:T(8,128)S(1)} %dynamic-slice_add_fusion.2), channel_id=1, source_target_pairs={{0,1},{1,2},{2,3},{3,0},{4,5},{5,6},{6,7},{7,4},{8,9},{9,10},{10,1... | collective-permute-start | bytes 1572872 | tf_op jit(solution)/shard_map/ppermute | solution.py:91
  231.2 21.9 %collective-permute-done.22 = f32[2,2,128,2,128]{4,2,3,1,0:T(8,128)} collective-permute-done((f32[2,2,128,2,128]{4,2,3,1,0:T(8,128)S(1)}, f32[2,2,128,2,128]{4,2,3,1,0:T(8,128)}, u32[]{:S(2)}, u32[]{:S(2)}) %collective-permute-start.22) | collective-permute-done | bytes 524320 | tf_op jit(solution)/shard_map/ppermute | solution.py:91
  253.0 1.1 dynamic-slice_add_fusion.1
  254.2 8.5 %collective-permute-start.23 = (f32[2,2,128,2,128]{4,2,3,1,0:T(8,128)S(1)}, f32[2,2,128,2,128]{4,2,3,1,0:T(8,128)S(1)}, u32[]{:S(2)}, u32[]{:S(2)}) collective-permute-start(f32[2,2,128,2,128]{4,2,3,1,0:T(8,128)S(1)} %dynamic-slice_add_fusion.1), channel_id=1, source_target_pairs={{0,1},{1,2},{2,3},{3,0},{4,5},{5,6},{6,7},{7,4},{8,9},{9,10},{10,1... | collective-permute-start | bytes 1572872 | tf_op jit(solution)/shard_map/ppermute | solution.py:91
  262.8 10.6 %collective-permute-done.23 = f32[2,2,128,2,128]{4,2,3,1,0:T(8,128)S(1)} collective-permute-done((f32[2,2,128,2,128]{4,2,3,1,0:T(8,128)S(1)}, f32[2,2,128,2,128]{4,2,3,1,0:T(8,128)S(1)}, u32[]{:S(2)}, u32[]{:S(2)}) %collective-permute-start.23) | collective-permute-done | bytes 524320 | tf_op jit(solution)/shard_map/ppermute | solution.py:91
  273.5 1.4 fusion.19
  275.0 1.2 copy.6
  (61 shorter events, 1.4 us)
Async XLA Ops:
  6.5 9.3 %copy-start.4 = (bf16[8,4,15,8,128]{4,3,2,1,0:T(8,128)(2,1)S(1)}, bf16[8,4,15,8,128]{4,3,2,1,0:T(8,128)(2,1)}, u32[]{:S(2)}) copy-start(bf16[8,4,15,8,128]{4,3,2,1,0:T(8,128)(2,1)} %param.5) | copy-start | bytes 2949124
  6.5 267.0 %reduce-scatter.2.cloned.1.call-start = ((), (), s32[]{:S(2)}) async-start(), calls=%async_computation.1 | async-start | bytes 2621440 | tf_op jit(solution)/shard_map/reduce_scatter | solution.py:132
  7.9 4.8 %collective-permute-start = (bf16[8,2,15,8,128]{4,3,2,1,0:T(8,128)(2,1)S(1)}, bf16[8,2,15,8,128]{4,3,2,1,0:T(8,128)(2,1)S(1)}, u32[]{:S(2)}, u32[]{:S(2)}) collective-permute-start(bf16[8,2,15,8,128]{4,3,2,1,0:T(8,128)(2,1)S(1)} %get-tuple-element.12), channel_id=1, source_target_pairs={{0,16},{16,0},{32,48},{48,32},{64,80},{80,64},{96,112},{112,96},{1... | collective-permute-start | bytes 1474568 | tf_op jit(solution)/shard_map/ppermute | solution.py:30
  13.0 24.2 %collective-permute-start.1 = (bf16[8,2,15,16,128]{4,3,2,1,0:T(8,128)(2,1)S(1)}, bf16[8,2,15,16,128]{4,3,2,1,0:T(8,128)(2,1)S(1)}, u32[]{:S(2)}, u32[]{:S(2)}) collective-permute-start(bf16[8,2,15,16,128]{4,3,2,1,0:T(8,128)(2,1)S(1)} %maximum_select_fusion.1), channel_id=1, source_target_pairs={{0,64},{16,80},{32,96},{48,112},{64,128},{80,144},{96,160},{112,17... | collective-permute-start | bytes 2949128 | tf_op jit(solution)/shard_map/ppermute | solution.py:18
  13.1 24.3 %collective-permute-start.3 = (bf16[8,2,15,16,128]{4,3,2,1,0:T(8,128)(2,1)S(1)}, bf16[8,2,15,16,128]{4,3,2,1,0:T(8,128)(2,1)S(1)}, u32[]{:S(2)}, u32[]{:S(2)}) collective-permute-start(bf16[8,2,15,16,128]{4,3,2,1,0:T(8,128)(2,1)S(1)} %maximum_select_fusion.1), channel_id=1, source_target_pairs={{0,192},{16,208},{32,224},{48,240},{64,0},{80,16},{96,32},{112,48}... | collective-permute-start | bytes 2949128 | tf_op jit(solution)/shard_map/ppermute | solution.py:19
  16.9 24.0 %collective-permute-start.5 = (bf16[4,4,15,8,128]{4,3,2,1,0:T(8,128)(2,1)}, bf16[4,4,15,8,128]{4,3,2,1,0:T(8,128)(2,1)S(1)}, u32[]{:S(2)}, u32[]{:S(2)}) collective-permute-start(bf16[4,4,15,8,128]{4,3,2,1,0:T(8,128)(2,1)} %get-tuple-element.10), channel_id=1, source_target_pairs={{0,32},{16,48},{32,0},{48,16},{64,96},{80,112},{96,64},{112,80},{1... | collective-permute-start | bytes 1474568 | tf_op jit(solution)/shard_map/ppermute | solution.py:46
  37.3 1.0 copy-start.5
  37.3 12.8 %collective-permute-start.2 = (bf16[4,2,15,16,128]{4,3,2,1,0:T(8,128)(2,1)S(1)}, bf16[4,2,15,16,128]{4,3,2,1,0:T(8,128)(2,1)S(1)}, u32[]{:S(2)}, u32[]{:S(2)}) collective-permute-start(bf16[4,2,15,16,128]{4,3,2,1,0:T(8,128)(2,1)S(1)} %slice.102), channel_id=1, source_target_pairs={{0,64},{16,80},{32,96},{48,112},{64,128},{80,144},{96,160},{112,17... | collective-permute-start | bytes 1474568 | tf_op jit(solution)/shard_map/ppermute | solution.py:21
  39.0 11.9 %collective-permute-start.4 = (bf16[4,2,15,16,128]{4,3,2,1,0:T(8,128)(2,1)}, bf16[4,2,15,16,128]{4,3,2,1,0:T(8,128)(2,1)}, u32[]{:S(2)}, u32[]{:S(2)}) collective-permute-start(bf16[4,2,15,16,128]{4,3,2,1,0:T(8,128)(2,1)} %slice.103), channel_id=1, source_target_pairs={{0,192},{16,208},{32,224},{48,240},{64,0},{80,16},{96,32},{112,48}... | collective-permute-start | bytes 1474568 | tf_op jit(solution)/shard_map/ppermute | solution.py:22
  40.9 7.0 %copy-start.6 = (bf16[8,2,15,16,128]{4,3,2,1,0:T(8,128)(2,1)S(1)}, bf16[8,2,15,16,128]{4,3,2,1,0:T(8,128)(2,1)}, u32[]{:S(2)}) copy-start(bf16[8,2,15,16,128]{4,3,2,1,0:T(8,128)(2,1)} %copy-done.5) | copy-start | bytes 2949124
  40.9 14.6 %collective-permute-start.6 = (bf16[4,2,15,8,128]{4,3,2,1,0:T(8,128)(2,1)S(1)}, bf16[4,2,15,8,128]{4,3,2,1,0:T(8,128)(2,1)S(1)}, u32[]{:S(2)}, u32[]{:S(2)}) collective-permute-start(bf16[4,2,15,8,128]{4,3,2,1,0:T(8,128)(2,1)S(1)} %get-tuple-element.15), channel_id=1, source_target_pairs={{0,16},{16,0},{32,48},{48,32},{64,80},{80,64},{96,112},{112,96},{1... | collective-permute-start | bytes 737288 | tf_op jit(solution)/shard_map/ppermute | solution.py:30
  54.4 4.9 %copy-start.7 = (bf16[4,4,15,8,128]{4,3,2,1,0:T(8,128)(2,1)S(1)}, bf16[4,4,15,8,128]{4,3,2,1,0:T(8,128)(2,1)}, u32[]{:S(2)}) copy-start(bf16[4,4,15,8,128]{4,3,2,1,0:T(8,128)(2,1)} %get-tuple-element.9) | copy-start | bytes 1474564
  56.6 10.9 %collective-permute-start.9 = (bf16[4,2,15,16,128]{4,3,2,1,0:T(8,128)(2,1)S(1)}, bf16[4,2,15,16,128]{4,3,2,1,0:T(8,128)(2,1)S(1)}, u32[]{:S(2)}, u32[]{:S(2)}) collective-permute-start(bf16[4,2,15,16,128]{4,3,2,1,0:T(8,128)(2,1)S(1)} %get-tuple-element.8), channel_id=1, source_target_pairs={{0,192},{16,208},{32,224},{48,240},{64,0},{80,16},{96,32},{112,48}... | collective-permute-start | bytes 1474568 | tf_op jit(solution)/shard_map/ppermute | solution.py:19
  59.3 11.7 %collective-permute-start.7 = (bf16[4,2,15,16,128]{4,3,2,1,0:T(8,128)(2,1)S(1)}, bf16[4,2,15,16,128]{4,3,2,1,0:T(8,128)(2,1)S(1)}, u32[]{:S(2)}, u32[]{:S(2)}) collective-permute-start(bf16[4,2,15,16,128]{4,3,2,1,0:T(8,128)(2,1)S(1)} %get-tuple-element.8), channel_id=1, source_target_pairs={{0,64},{16,80},{32,96},{48,112},{64,128},{80,144},{96,160},{112,17... | collective-permute-start | bytes 1474568 | tf_op jit(solution)/shard_map/ppermute | solution.py:18
  59.3 15.1 %collective-permute-start.11 = (bf16[4,4,15,8,128]{4,3,2,1,0:T(8,128)(2,1)S(1)}, bf16[4,4,15,8,128]{4,3,2,1,0:T(8,128)(2,1)S(1)}, u32[]{:S(2)}, u32[]{:S(2)}) collective-permute-start(bf16[4,4,15,8,128]{4,3,2,1,0:T(8,128)(2,1)S(1)} %copy-done.7), channel_id=1, source_target_pairs={{0,32},{16,48},{32,0},{48,16},{64,96},{80,112},{96,64},{112,80},{1... | collective-permute-start | bytes 1474568 | tf_op jit(solution)/shard_map/ppermute | solution.py:47
  67.5 12.8 %collective-permute-start.10 = (bf16[2,2,15,16,128]{4,3,2,1,0:T(8,128)(2,1)S(1)}, bf16[2,2,15,16,128]{4,3,2,1,0:T(8,128)(2,1)S(1)}, u32[]{:S(2)}, u32[]{:S(2)}) collective-permute-start(bf16[2,2,15,16,128]{4,3,2,1,0:T(8,128)(2,1)S(1)} %slice.107), channel_id=1, source_target_pairs={{0,192},{16,208},{32,224},{48,240},{64,0},{80,16},{96,32},{112,48}... | collective-permute-start | bytes 737288 | tf_op jit(solution)/shard_map/ppermute | solution.py:22
  71.0 9.3 %collective-permute-start.8 = (bf16[2,2,15,16,128]{4,3,2,1,0:T(8,128)(2,1)S(1)}, bf16[2,2,15,16,128]{4,3,2,1,0:T(8,128)(2,1)S(1)}, u32[]{:S(2)}, u32[]{:S(2)}) collective-permute-start(bf16[2,2,15,16,128]{4,3,2,1,0:T(8,128)(2,1)S(1)} %slice.106), channel_id=1, source_target_pairs={{0,64},{16,80},{32,96},{48,112},{64,128},{80,144},{96,160},{112,17... | collective-permute-start | bytes 737288 | tf_op jit(solution)/shard_map/ppermute | solution.py:21
  74.4 7.8 %collective-permute-start.12 = (bf16[4,2,15,8,128]{4,3,2,1,0:T(8,128)(2,1)S(1)}, bf16[4,2,15,8,128]{4,3,2,1,0:T(8,128)(2,1)S(1)}, u32[]{:S(2)}, u32[]{:S(2)}) collective-permute-start(bf16[4,2,15,8,128]{4,3,2,1,0:T(8,128)(2,1)S(1)} %get-tuple-element.13), channel_id=1, source_target_pairs={{0,16},{16,0},{32,48},{48,32},{64,80},{80,64},{96,112},{112,96},{1... | collective-permute-start | bytes 737288 | tf_op jit(solution)/shard_map/ppermute | solution.py:30
  83.2 24.3 %copy-start.10 = (s32[60]{0:T(128)S(1)}, s32[60]{0:T(128)}, u32[]{:S(2)}) copy-start(s32[60]{0:T(128)} %param.7) | copy-start | bytes 724
  83.2 24.4 %copy-start.8 = (s32[8]{0:T(128)S(1)}, s32[8]{0:T(128)}, u32[]{:S(2)}) copy-start(s32[8]{0:T(128)} %param.6) | copy-start | bytes 100
  83.2 12.3 %collective-permute-start.13 = (bf16[4,2,15,16,128]{4,3,2,1,0:T(8,128)(2,1)S(1)}, bf16[4,2,15,16,128]{4,3,2,1,0:T(8,128)(2,1)S(1)}, u32[]{:S(2)}, u32[]{:S(2)}) collective-permute-start(bf16[4,2,15,16,128]{4,3,2,1,0:T(8,128)(2,1)S(1)} %get-tuple-element.6), channel_id=1, source_target_pairs={{0,64},{16,80},{32,96},{48,112},{64,128},{80,144},{96,160},{112,17... | collective-permute-start | bytes 1474568 | tf_op jit(solution)/shard_map/ppermute | solution.py:18
  83.2 12.4 %collective-permute-start.15 = (bf16[4,2,15,16,128]{4,3,2,1,0:T(8,128)(2,1)S(1)}, bf16[4,2,15,16,128]{4,3,2,1,0:T(8,128)(2,1)S(1)}, u32[]{:S(2)}, u32[]{:S(2)}) collective-permute-start(bf16[4,2,15,16,128]{4,3,2,1,0:T(8,128)(2,1)S(1)} %get-tuple-element.6), channel_id=1, source_target_pairs={{0,192},{16,208},{32,224},{48,240},{64,0},{80,16},{96,32},{112,48}... | collective-permute-start | bytes 1474568 | tf_op jit(solution)/shard_map/ppermute | solution.py:19
  95.6 7.2 %collective-permute-start.14 = (bf16[2,2,15,16,128]{4,3,2,1,0:T(8,128)(2,1)S(1)}, bf16[2,2,15,16,128]{4,3,2,1,0:T(8,128)(2,1)S(1)}, u32[]{:S(2)}, u32[]{:S(2)}) collective-permute-start(bf16[2,2,15,16,128]{4,3,2,1,0:T(8,128)(2,1)S(1)} %slice.110), channel_id=1, source_target_pairs={{0,64},{16,80},{32,96},{48,112},{64,128},{80,144},{96,160},{112,17... | collective-permute-start | bytes 737288 | tf_op jit(solution)/shard_map/ppermute | solution.py:21
  95.7 7.0 %collective-permute-start.16 = (bf16[2,2,15,16,128]{4,3,2,1,0:T(8,128)(2,1)S(1)}, bf16[2,2,15,16,128]{4,3,2,1,0:T(8,128)(2,1)S(1)}, u32[]{:S(2)}, u32[]{:S(2)}) collective-permute-start(bf16[2,2,15,16,128]{4,3,2,1,0:T(8,128)(2,1)S(1)} %slice.111), channel_id=1, source_target_pairs={{0,192},{16,208},{32,224},{48,240},{64,0},{80,16},{96,32},{112,48}... | collective-permute-start | bytes 737288 | tf_op jit(solution)/shard_map/ppermute | solution.py:22
  104.6 55.9 %collective-permute-start.24 = (bf16[8,2,15,128,128]{4,3,2,1,0:T(8,128)(2,1)}, bf16[8,2,15,128,128]{4,3,2,1,0:T(8,128)(2,1)}, u32[]{:S(2)}, u32[]{:S(2)}) collective-permute-start(bf16[8,2,15,128,128]{4,3,2,1,0:T(8,128)(2,1)} %constant_dynamic-update-slice_fusion), channel_id=1, source_target_pairs={{0,16},{16,0},{32,48},{48,32},{64,80},{80,64},{96,112},{112,96},{1... | collective-permute-start | bytes 23592968 | tf_op jit(solution)/shard_map/ppermute | solution.py:62
  110.4 46.9 %collective-permute-start.18 = (bf16[8,2,15,32,128]{4,3,2,1,0:T(8,128)(2,1)S(1)}, bf16[8,2,15,32,128]{4,3,2,1,0:T(8,128)(2,1)S(1)}, u32[]{:S(2)}, u32[]{:S(2)}) collective-permute-start(bf16[8,2,15,32,128]{4,3,2,1,0:T(8,128)(2,1)S(1)} %broadcast_select_fusion), channel_id=1, source_target_pairs={{0,4},{4,8},{8,12},{12,0},{1,5},{5,9},{9,13},{13,1},{2,6},{6,10},{... | collective-permute-start | bytes 5898248 | tf_op jit(solution)/shard_map/ppermute | solution.py:71
  112.8 44.6 %collective-permute-start.17 = (bf16[8,2,15,32,128]{4,3,2,1,0:T(8,128)(2,1)S(1)}, bf16[8,2,15,32,128]{4,3,2,1,0:T(8,128)(2,1)S(1)}, u32[]{:S(2)}, u32[]{:S(2)}) collective-permute-start(bf16[8,2,15,32,128]{4,3,2,1,0:T(8,128)(2,1)S(1)} %broadcast_select_fusion), channel_id=1, source_target_pairs={{0,12},{4,0},{8,4},{12,8},{1,13},{5,1},{9,5},{13,9},{2,14},{6,2},{... | collective-permute-start | bytes 5898248 | tf_op jit(solution)/shard_map/ppermute | solution.py:72
  157.2 27.5 %copy-start = (bf16[8,2,15,32,128]{4,3,2,1,0:T(8,128)(2,1)}, bf16[8,2,15,32,128]{4,3,2,1,0:T(8,128)(2,1)S(1)}, u32[]{:S(2)}) copy-start(bf16[8,2,15,32,128]{4,3,2,1,0:T(8,128)(2,1)S(1)} %collective-permute-done.18) | copy-start | bytes 5898244
  157.3 24.0 %collective-permute-start.19 = (bf16[4,2,15,32,128]{4,3,2,1,0:T(8,128)(2,1)S(1)}, bf16[4,2,15,32,128]{4,3,2,1,0:T(8,128)(2,1)S(1)}, u32[]{:S(2)}, u32[]{:S(2)}) collective-permute-start(bf16[4,2,15,32,128]{4,3,2,1,0:T(8,128)(2,1)S(1)} %slice.114), channel_id=1, source_target_pairs={{0,4},{4,8},{8,12},{12,0},{1,5},{5,9},{9,13},{13,1},{2,6},{6,10},{... | collective-permute-start | bytes 2949128 | tf_op jit(solution)/shard_map/ppermute | solution.py:74
  157.4 5.4 %copy-start.2 = (bf16[8,2,15,32,128]{4,3,2,1,0:T(8,128)(2,1)}, bf16[8,2,15,32,128]{4,3,2,1,0:T(8,128)(2,1)S(1)}, u32[]{:S(2)}) copy-start(bf16[8,2,15,32,128]{4,3,2,1,0:T(8,128)(2,1)S(1)} %collective-permute-done.17) | copy-start | bytes 5898244
  157.5 23.8 %collective-permute-start.20 = (bf16[4,2,15,32,128]{4,3,2,1,0:T(8,128)(2,1)S(1)}, bf16[4,2,15,32,128]{4,3,2,1,0:T(8,128)(2,1)S(1)}, u32[]{:S(2)}, u32[]{:S(2)}) collective-permute-start(bf16[4,2,15,32,128]{4,3,2,1,0:T(8,128)(2,1)S(1)} %slice.115), channel_id=1, source_target_pairs={{0,12},{4,0},{8,4},{12,8},{1,13},{5,1},{9,5},{13,9},{2,14},{6,2},{... | collective-permute-start | bytes 2949128 | tf_op jit(solution)/shard_map/ppermute | solution.py:75
  181.3 1.0 copy-start.9
  191.4 2.6 copy-start.3
  194.0 2.6 copy-start.1
  199.3 26.5 %collective-permute-start.21 = (f32[2,2,128,2,128]{4,2,3,1,0:T(8,128)S(1)}, f32[2,2,128,2,128]{4,2,3,1,0:T(8,128)S(1)}, u32[]{:S(2)}, u32[]{:S(2)}) collective-permute-start(f32[2,2,128,2,128]{4,2,3,1,0:T(8,128)S(1)} %constant_dynamic-slice_fusion), channel_id=1, source_target_pairs={{0,1},{1,2},{2,3},{3,0},{4,5},{5,6},{6,7},{7,4},{8,9},{9,10},{10,1... | collective-permute-start | bytes 1572872 | tf_op jit(solution)/shard_map/ppermute | solution.py:91
  225.8 27.2 %collective-permute-start.22 = (f32[2,2,128,2,128]{4,2,3,1,0:T(8,128)S(1)}, f32[2,2,128,2,128]{4,2,3,1,0:T(8,128)}, u32[]{:S(2)}, u32[]{:S(2)}) collective-permute-start(f32[2,2,128,2,128]{4,2,3,1,0:T(8,128)S(1)} %dynamic-slice_add_fusion.2), channel_id=1, source_target_pairs={{0,1},{1,2},{2,3},{3,0},{4,5},{5,6},{6,7},{7,4},{8,9},{9,10},{10,1... | collective-permute-start | bytes 1572872 | tf_op jit(solution)/shard_map/ppermute | solution.py:91
  254.2 19.3 %collective-permute-start.23 = (f32[2,2,128,2,128]{4,2,3,1,0:T(8,128)S(1)}, f32[2,2,128,2,128]{4,2,3,1,0:T(8,128)S(1)}, u32[]{:S(2)}, u32[]{:S(2)}) collective-permute-start(f32[2,2,128,2,128]{4,2,3,1,0:T(8,128)S(1)} %dynamic-slice_add_fusion.1), channel_id=1, source_target_pairs={{0,1},{1,2},{2,3},{3,0},{4,5},{5,6},{6,7},{7,4},{8,9},{9,10},{10,1... | collective-permute-start | bytes 1572872 | tf_op jit(solution)/shard_map/ppermute | solution.py:91
Sparse Core Ops, SparseCore 0:
  188.8 77.5 reduce-scatter.1

commit v9 on v8

--- a/solution.py
+++ b/solution.py
@@ -77,18 +77,18 @@
     return [w, from_right, opp, from_left]
 
 
-def ring_reduce_scatter(part):
+def ring_reduce_scatter(part, dirn, head):
     n = lax.axis_size("rep")
     d = lax.axis_index("rep")
     width = part.shape[0] // n
-    fwd = [(i, (i + 1) % n) for i in range(n)]
+    perm = [(i, (i + dirn) % n) for i in range(n)]
 
     def chunk(t):
         return lax.dynamic_slice_in_dim(part, (t % n) * width, width, axis=0)
 
-    acc = chunk(d + n - 1)
+    acc = head
     for step in range(1, n):
-        acc = lax.ppermute(acc, "rep", fwd) + chunk(d + 2 * n - step - 1)
+        acc = lax.ppermute(acc, "rep", perm) + chunk(d + 2 * n - (step + 1) * dirn)
     return acc
 
 
@@ -114,11 +114,13 @@
     owned = ngroup // lax.axis_size("rep")
     w_blocks = gather_integrals(masked)
     t_mine, t_other = gather_amplitudes(amplitudes, col_index)
-    sums = []
-    for t_half, name in ((t_mine, "em"), (t_other, "eo")):
-        width = c_local
+    nrep = lax.axis_size("rep")
+    cw = ngroup // nrep
+    width = c_local
+
+    def dots(w_list, t_half):
         part = None
-        for s, w_blk in enumerate(w_blocks):
+        for s, w_blk in enumerate(w_list):
             term = jnp.einsum(
                 "gikca,gjkcb->giajb",
                 w_blk,
@@ -126,10 +128,17 @@
                 preferred_element_type=jnp.float32,
             )
             part = term if part is None else part + term
-        if name == "em":
-            sums.append(ring_reduce_scatter(part))
-        else:
-            sums.append(lax.psum_scatter(part, "rep", scatter_dimension=0, tiled=True))
+        return part
+
+    sums = []
+    for t_half, dirn in ((t_mine, 1), (t_other, -1)):
+        first = ((rep_index + nrep - dirn) % nrep) * cw
+        head = dots(
+            [lax.dynamic_slice_in_dim(w, first, cw, axis=0) for w in w_blocks],
+            lax.dynamic_slice_in_dim(t_half, first, cw, axis=0),
+        )
+        part = dots(w_blocks, t_half)
+        sums.append(ring_reduce_scatter(part, dirn, head))
     summed = jnp.where(
         core == 0, jnp.concatenate(sums, axis=3), jnp.concatenate(sums[::-1], axis=3)
     )

time: 287 us -> 274 us (0.955)
  the two profiles are of different devices: /device:TPU:1 before, /device:TPU:230 now
where the time goes in v9:
time: 274 us; the launch traced here: 273 us
  waiting for transfers between devices  158 us (58%)
  starting transfers between devices  47.7 us (17%)
  matrix products  31.1 us (11%)
  local copies, waits for them, and re-layouts  20.1 us (7%)
  other arithmetic  15.9 us (6%)
    ppermute x1, waiting for transfers between devices, gather_integrals(): from_left = lax.ppermute(w, 'col', fwd)  43.2 us
    dot_general x16, matrix products, dots(): jnp.einsum('gikca,gjkcb->giajb', w_blk, t_half[:, :, :, s * width:(s + 1)...  31.1 us
    ppermute x3, waiting for transfers between devices, ring4_pieces(): from_left = lax.ppermute(block, axis, fwd)  30.9 us
    ppermute x6, waiting for transfers between devices, ring_reduce_scatter(): acc = lax.ppermute(acc, 'rep', perm) + chunk(d + 2 * n - (step + 1) * dirn)  30.6 us
    ppermute x6, starting transfers between devices, ring_reduce_scatter(): acc = lax.ppermute(acc, 'rep', perm) + chunk(d + 2 * n - (step + 1) * dirn)  22.8 us
    ppermute x1, waiting for transfers between devices, gather_integrals(): opp_lo = lax.ppermute(from_left[:half], 'col', fwd)  19.9 us
    ppermute x1, waiting for transfers between devices, gather_amplitudes(): zh_hi = lax.ppermute(t_part[hg:], 'row', swap)  9.22 us
    ppermute x3, waiting for transfers between devices, ring4_pieces(): from_right = lax.ppermute(block, axis, bwd)  7.8 us
  transfers between devices with their start and end apart: 28, of which 17 were waited for; matrix products, arithmetic and copies ran while one was open for 21% of the time, Pallas kernels for 0%

profile of v9, /device:TPU:230, one launch (start us, length us, event | category | flops | bytes accessed | tf_op | source)
XLA Modules:
  0.0 273.3 jit_solution(14900737164363540139)
XLA Ops:
  0.0 1.3 broadcast_select_fusion.2
  1.4 1.9 collective-permute-done
  4.2 1.5 collective-permute-start.3
  5.8 1.0 fusion.52
  6.8 1.4 collective-permute-start.5
  8.3 19.3 %collective-permute-done.1 = bf16[8,2,15,16,128]{4,3,2,1,0:T(8,128)(2,1)S(1)} collective-permute-done((bf16[8,2,15,16,128]{4,3,2,1,0:T(8,128)(2,1)S(1)}, bf16[8,2,15,16,128]{4,3,2,1,0:T(8,128)(2,1)S(1)}, u32[]{:S(2)}, u32[]{:S(2)}) %collective-permute-start.1) | collective-permute-done | bytes 983072 | tf_op jit(solution)/shard_map/ppermute | solution.py:18
  27.6 1.8 collective-permute-start.2
  31.0 5.1 %broadcast_in_dim.56 = bf16[8,2,15,128,128]{4,3,2,1,0:T(8,128)(2,1)} broadcast(bf16[]{:T(256)} %constant.161.clone.1), dimensions={} | broadcast | bytes 7864322 | tf_op jit(solution)/shard_map/broadcast_in_dim | solution.py:50
  36.1 1.2 constant_dynamic-update-slice_fusion.8
  37.3 2.8 %collective-permute-done.2 = bf16[4,2,15,16,128]{4,3,2,1,0:T(8,128)(2,1)S(1)} collective-permute-done((bf16[4,2,15,16,128]{4,3,2,1,0:T(8,128)(2,1)S(1)}, bf16[4,2,15,16,128]{4,3,2,1,0:T(8,128)(2,1)S(1)}, u32[]{:S(2)}, u32[]{:S(2)}) %collective-permute-start.2) | collective-permute-done | bytes 491552 | tf_op jit(solution)/shard_map/ppermute | solution.py:21
  40.1 3.8 %collective-permute-done.4 = bf16[4,2,15,16,128]{4,3,2,1,0:T(8,128)(2,1)} collective-permute-done((bf16[4,2,15,16,128]{4,3,2,1,0:T(8,128)(2,1)}, bf16[4,2,15,16,128]{4,3,2,1,0:T(8,128)(2,1)}, u32[]{:S(2)}, u32[]{:S(2)}) %collective-permute-start.4) | collective-permute-done | bytes 491552 | tf_op jit(solution)/shard_map/ppermute | solution.py:22
  43.8 2.2 maximum_dynamic-update-slice_fusion
  46.1 1.2 constant_dynamic-update-slice_fusion.7
  47.3 1.2 constant_dynamic-update-slice_fusion.6
  48.5 1.1 constant_dynamic-update-slice_fusion.5
  49.5 3.2 %collective-permute-start.7 = (bf16[4,2,15,16,128]{4,3,2,1,0:T(8,128)(2,1)S(1)}, bf16[4,2,15,16,128]{4,3,2,1,0:T(8,128)(2,1)S(1)}, u32[]{:S(2)}, u32[]{:S(2)}) collective-permute-start(bf16[4,2,15,16,128]{4,3,2,1,0:T(8,128)(2,1)S(1)} %get-tuple-element.8), channel_id=1, source_target_pairs={{0,64},{16,80},{32,96},{48,112},{64,128},{80,144},{96,160},{112,17... | collective-permute-start | bytes 1474568 | tf_op jit(solution)/shard_map/ppermute | solution.py:18
  52.8 1.5 collective-permute-start.11
  54.2 7.8 %collective-permute-done.9 = bf16[4,2,15,16,128]{4,3,2,1,0:T(8,128)(2,1)S(1)} collective-permute-done((bf16[4,2,15,16,128]{4,3,2,1,0:T(8,128)(2,1)S(1)}, bf16[4,2,15,16,128]{4,3,2,1,0:T(8,128)(2,1)S(1)}, u32[]{:S(2)}, u32[]{:S(2)}) %collective-permute-start.9) | collective-permute-done | bytes 491552 | tf_op jit(solution)/shard_map/ppermute | solution.py:19
  62.2 3.3 %collective-permute-start.8 = (bf16[2,2,15,16,128]{4,3,2,1,0:T(8,128)(2,1)S(1)}, bf16[2,2,15,16,128]{4,3,2,1,0:T(8,128)(2,1)S(1)}, u32[]{:S(2)}, u32[]{:S(2)}) collective-permute-start(bf16[2,2,15,16,128]{4,3,2,1,0:T(8,128)(2,1)S(1)} %slice.138), channel_id=1, source_target_pairs={{0,64},{16,80},{32,96},{48,112},{64,128},{80,144},{96,160},{112,17... | collective-permute-start | bytes 737288 | tf_op jit(solution)/shard_map/ppermute | solution.py:21
  65.4 9.2 %collective-permute-done.11 = bf16[4,4,15,8,128]{4,3,2,1,0:T(8,128)(2,1)S(1)} collective-permute-done((bf16[4,4,15,8,128]{4,3,2,1,0:T(8,128)(2,1)S(1)}, bf16[4,4,15,8,128]{4,3,2,1,0:T(8,128)(2,1)S(1)}, u32[]{:S(2)}, u32[]{:S(2)}) %collective-permute-start.11) | collective-permute-done | bytes 491552 | tf_op jit(solution)/shard_map/ppermute | solution.py:47
  76.8 0.9 constant_dynamic-update-slice_fusion.3
  77.7 1.1 constant_dynamic-update-slice_fusion.2
  79.1 1.7 collective-permute-start.15
  80.8 11.6 %collective-permute-done.13 = bf16[4,2,15,16,128]{4,3,2,1,0:T(8,128)(2,1)S(1)} collective-permute-done((bf16[4,2,15,16,128]{4,3,2,1,0:T(8,128)(2,1)S(1)}, bf16[4,2,15,16,128]{4,3,2,1,0:T(8,128)(2,1)S(1)}, u32[]{:S(2)}, u32[]{:S(2)}) %collective-permute-start.13) | collective-permute-done | bytes 491552 | tf_op jit(solution)/shard_map/ppermute | solution.py:18
  92.4 1.6 collective-permute-start.14
  95.5 4.4 %collective-permute-done.14 = bf16[2,2,15,16,128]{4,3,2,1,0:T(8,128)(2,1)S(1)} collective-permute-done((bf16[2,2,15,16,128]{4,3,2,1,0:T(8,128)(2,1)S(1)}, bf16[2,2,15,16,128]{4,3,2,1,0:T(8,128)(2,1)S(1)}, u32[]{:S(2)}, u32[]{:S(2)}) %collective-permute-start.14) | collective-permute-done | bytes 245792 | tf_op jit(solution)/shard_map/ppermute | solution.py:21
  100.0 2.6 collective-permute-done.16
  103.5 1.0 constant_dynamic-update-slice_fusion
  105.6 1.7 broadcast_select_fusion
  107.3 1.8 collective-permute-start.18
  109.1 1.5 collective-permute-start.17
  110.6 43.2 %collective-permute-done.18 = bf16[8,2,15,32,128]{4,3,2,1,0:T(8,128)(2,1)S(1)} collective-permute-done((bf16[8,2,15,32,128]{4,3,2,1,0:T(8,128)(2,1)S(1)}, bf16[8,2,15,32,128]{4,3,2,1,0:T(8,128)(2,1)S(1)}, u32[]{:S(2)}, u32[]{:S(2)}) %collective-permute-start.18) | collective-permute-done | bytes 1966112 | tf_op jit(solution)/shard_map/ppermute | solution.py:71
  153.8 1.1 slice.144
  155.5 1.1 slice.145
  157.1 2.7 collective-permute-start.20
  159.8 19.9 %collective-permute-done.19 = bf16[4,2,15,32,128]{4,3,2,1,0:T(8,128)(2,1)S(1)} collective-permute-done((bf16[4,2,15,32,128]{4,3,2,1,0:T(8,128)(2,1)}, bf16[4,2,15,32,128]{4,3,2,1,0:T(8,128)(2,1)S(1)}, u32[]{:S(2)}, u32[]{:S(2)}) %collective-permute-start.19) | collective-permute-done | bytes 983072 | tf_op jit(solution)/shard_map/ppermute | solution.py:74
  180.7 1.6 constant_dynamic-update-slice_fusion.9
  182.3 1.4 convolution_bitcast_fusion.5
  183.7 1.4 convolution_bitcast_fusion.4
  185.1 1.4 convolution_bitcast_fusion.6
  186.5 1.4 fusion.22
  187.9 5.1 %collective-permute-start.21 = (f32[2,2,128,2,128]{4,2,3,1,0:T(8,128)S(1)}, f32[2,2,128,2,128]{4,2,3,1,0:T(8,128)S(1)}, u32[]{:S(2)}, u32[]{:S(2)}) collective-permute-start(f32[2,2,128,2,128]{4,2,3,1,0:T(8,128)S(1)} %fusion.22), channel_id=1, source_target_pairs={{0,1},{1,2},{2,3},{3,0},{4,5},{5,6},{6,7},{7,4},{8,9},{9,10},{10,1... | collective-permute-start | bytes 1572872 | tf_op jit(solution)/shard_map/ppermute | solution.py:91
  193.1 2.4 fusion.5
  195.5 2.4 fusion.7
  197.9 2.4 fusion.6
  200.3 2.6 bitcast_add_fusion.3
  203.6 4.4 %collective-permute-start.22 = (f32[2,2,128,2,128]{4,2,3,1,0:T(8,128)S(1)}, f32[2,2,128,2,128]{4,2,3,1,0:T(8,128)S(1)}, u32[]{:S(2)}, u32[]{:S(2)}) collective-permute-start(f32[2,2,128,2,128]{4,2,3,1,0:T(8,128)S(1)} %dynamic-slice_add_fusion.5), channel_id=1, source_target_pairs={{0,1},{1,2},{2,3},{3,0},{4,5},{5,6},{6,7},{7,4},{8,9},{9,10},{10,1... | collective-permute-start | bytes 1572872 | tf_op jit(solution)/shard_map/ppermute | solution.py:91
  207.9 1.4 convolution_bitcast_fusion.1
  209.3 1.4 convolution_bitcast_fusion.2
  210.7 1.4 convolution_bitcast_fusion
  212.2 1.4 fusion.25
  213.7 2.4 fusion.1
  216.1 2.4 fusion.2
  218.5 2.4 fusion.3
  220.9 2.8 %bitcast_add_fusion = f32[8,2,128,2,128]{4,2,3,1,0:T(8,128)S(1)} fusion(f32[8,2,128,2,128,1]{4,2,5,3,1,0:T(8,128)S(1)} %fusion.1, f32[8,2,128,2,128,1]{4,2,5,3,1,0:T(8,128)S(1)} %fusion.2, f32[8,2,128,2,128,1]{4,2,5,3,1,0:T(8,128)S(1)} %fusion.3, bf16[8,2,15,128,128]{4,3,2,1,0:T(8,128)(2,1)} %collective-permute-done.24, ...), kind=kOutput, calls=%fused_computation | convolution fusion | flops 504889344 | bytes 12320768 | tf_op jit(solution)/shard_map/gikca,gjkcb->giajb/dot_general | solution.py:124
  223.7 5.8 %collective-permute-done.25 = f32[2,2,128,2,128]{4,2,3,1,0:T(8,128)S(1)} collective-permute-done((f32[2,2,128,2,128]{4,2,3,1,0:T(8,128)S(1)}, f32[2,2,128,2,128]{4,2,3,1,0:T(8,128)S(1)}, u32[]{:S(2)}, u32[]{:S(2)}) %collective-permute-start.25) | collective-permute-done | bytes 524320 | tf_op jit(solution)/shard_map/ppermute | solution.py:91
  230.3 1.8 collective-permute-start.26
  233.0 2.0 collective-permute-start.23
  235.0 12.2 %collective-permute-done.26 = f32[2,2,128,2,128]{4,2,3,1,0:T(8,128)} collective-permute-done((f32[2,2,128,2,128]{4,2,3,1,0:T(8,128)}, f32[2,2,128,2,128]{4,2,3,1,0:T(8,128)}, u32[]{:S(2)}, u32[]{:S(2)}) %collective-permute-start.26) | collective-permute-done | bytes 524320 | tf_op jit(solution)/shard_map/ppermute | solution.py:91
  247.3 2.0 dynamic-slice_add_fusion.1
  249.3 9.4 %collective-permute-start.27 = (f32[2,2,128,2,128]{4,2,3,1,0:T(8,128)}, f32[2,2,128,2,128]{4,2,3,1,0:T(8,128)S(1)}, u32[]{:S(2)}, u32[]{:S(2)}) collective-permute-start(f32[2,2,128,2,128]{4,2,3,1,0:T(8,128)} %dynamic-slice_add_fusion.1), channel_id=1, source_target_pairs={{0,3},{1,0},{2,1},{3,2},{4,7},{5,4},{6,5},{7,6},{8,11},{9,8},{10,9... | collective-permute-start | bytes 1572872 | tf_op jit(solution)/shard_map/ppermute | solution.py:91
  258.9 12.0 %collective-permute-done.27 = f32[2,2,128,2,128]{4,2,3,1,0:T(8,128)S(1)} collective-permute-done((f32[2,2,128,2,128]{4,2,3,1,0:T(8,128)}, f32[2,2,128,2,128]{4,2,3,1,0:T(8,128)S(1)}, u32[]{:S(2)}, u32[]{:S(2)}) %collective-permute-start.27) | collective-permute-done | bytes 524320 | tf_op jit(solution)/shard_map/ppermute | solution.py:91
  270.9 1.1 dynamic-slice_add_fusion
  272.1 1.2 copy.6
  (80 shorter events, 13.7 us)
Async XLA Ops:
  0.0 5.8 %copy-start.7 = (bf16[8,4,15,8,128]{4,3,2,1,0:T(8,128)(2,1)S(1)}, bf16[8,4,15,8,128]{4,3,2,1,0:T(8,128)(2,1)}, u32[]{:S(2)}) copy-start(bf16[8,4,15,8,128]{4,3,2,1,0:T(8,128)(2,1)} %param.5) | copy-start | bytes 2949124
  1.3 1.9 collective-permute-start
  3.7 23.9 %collective-permute-start.1 = (bf16[8,2,15,16,128]{4,3,2,1,0:T(8,128)(2,1)S(1)}, bf16[8,2,15,16,128]{4,3,2,1,0:T(8,128)(2,1)S(1)}, u32[]{:S(2)}, u32[]{:S(2)}) collective-permute-start(bf16[8,2,15,16,128]{4,3,2,1,0:T(8,128)(2,1)S(1)} %maximum_select_fusion.1), channel_id=1, source_target_pairs={{0,64},{16,80},{32,96},{48,112},{64,128},{80,144},{96,160},{112,17... | collective-permute-start | bytes 2949128 | tf_op jit(solution)/shard_map/ppermute | solution.py:18
  4.2 25.1 %collective-permute-start.3 = (bf16[8,2,15,16,128]{4,3,2,1,0:T(8,128)(2,1)S(1)}, bf16[8,2,15,16,128]{4,3,2,1,0:T(8,128)(2,1)S(1)}, u32[]{:S(2)}, u32[]{:S(2)}) collective-permute-start(bf16[8,2,15,16,128]{4,3,2,1,0:T(8,128)(2,1)S(1)} %maximum_select_fusion.1), channel_id=1, source_target_pairs={{0,192},{16,208},{32,224},{48,240},{64,0},{80,16},{96,32},{112,48}... | collective-permute-start | bytes 2949128 | tf_op jit(solution)/shard_map/ppermute | solution.py:19
  6.8 24.1 %collective-permute-start.5 = (bf16[4,4,15,8,128]{4,3,2,1,0:T(8,128)(2,1)}, bf16[4,4,15,8,128]{4,3,2,1,0:T(8,128)(2,1)S(1)}, u32[]{:S(2)}, u32[]{:S(2)}) collective-permute-start(bf16[4,4,15,8,128]{4,3,2,1,0:T(8,128)(2,1)} %get-tuple-element.10), channel_id=1, source_target_pairs={{0,32},{16,48},{32,0},{48,16},{64,96},{80,112},{96,64},{112,80},{1... | collective-permute-start | bytes 1474568 | tf_op jit(solution)/shard_map/ppermute | solution.py:46
  27.5 1.8 copy-start.8
  27.6 12.5 %collective-permute-start.2 = (bf16[4,2,15,16,128]{4,3,2,1,0:T(8,128)(2,1)S(1)}, bf16[4,2,15,16,128]{4,3,2,1,0:T(8,128)(2,1)S(1)}, u32[]{:S(2)}, u32[]{:S(2)}) collective-permute-start(bf16[4,2,15,16,128]{4,3,2,1,0:T(8,128)(2,1)S(1)} %slice.134), channel_id=1, source_target_pairs={{0,64},{16,80},{32,96},{48,112},{64,128},{80,144},{96,160},{112,17... | collective-permute-start | bytes 1474568 | tf_op jit(solution)/shard_map/ppermute | solution.py:21
  30.2 13.7 %collective-permute-start.4 = (bf16[4,2,15,16,128]{4,3,2,1,0:T(8,128)(2,1)}, bf16[4,2,15,16,128]{4,3,2,1,0:T(8,128)(2,1)}, u32[]{:S(2)}, u32[]{:S(2)}) collective-permute-start(bf16[4,2,15,16,128]{4,3,2,1,0:T(8,128)(2,1)} %slice.135), channel_id=1, source_target_pairs={{0,192},{16,208},{32,224},{48,240},{64,0},{80,16},{96,32},{112,48}... | collective-permute-start | bytes 1474568 | tf_op jit(solution)/shard_map/ppermute | solution.py:22
  30.9 5.2 %copy-start.9 = (bf16[8,2,15,16,128]{4,3,2,1,0:T(8,128)(2,1)S(1)}, bf16[8,2,15,16,128]{4,3,2,1,0:T(8,128)(2,1)}, u32[]{:S(2)}) copy-start(bf16[8,2,15,16,128]{4,3,2,1,0:T(8,128)(2,1)} %copy-done.8) | copy-start | bytes 2949124
  30.9 17.5 %collective-permute-start.6 = (bf16[4,2,15,8,128]{4,3,2,1,0:T(8,128)(2,1)S(1)}, bf16[4,2,15,8,128]{4,3,2,1,0:T(8,128)(2,1)S(1)}, u32[]{:S(2)}, u32[]{:S(2)}) collective-permute-start(bf16[4,2,15,8,128]{4,3,2,1,0:T(8,128)(2,1)S(1)} %get-tuple-element.15), channel_id=1, source_target_pairs={{0,16},{16,0},{32,48},{48,32},{64,80},{80,64},{96,112},{112,96},{1... | collective-permute-start | bytes 737288 | tf_op jit(solution)/shard_map/ppermute | solution.py:30
  47.3 5.5 %copy-start.10 = (bf16[4,4,15,8,128]{4,3,2,1,0:T(8,128)(2,1)S(1)}, bf16[4,4,15,8,128]{4,3,2,1,0:T(8,128)(2,1)}, u32[]{:S(2)}) copy-start(bf16[4,4,15,8,128]{4,3,2,1,0:T(8,128)(2,1)} %get-tuple-element.9) | copy-start | bytes 1474564
  49.5 12.5 %collective-permute-start.9 = (bf16[4,2,15,16,128]{4,3,2,1,0:T(8,128)(2,1)S(1)}, bf16[4,2,15,16,128]{4,3,2,1,0:T(8,128)(2,1)S(1)}, u32[]{:S(2)}, u32[]{:S(2)}) collective-permute-start(bf16[4,2,15,16,128]{4,3,2,1,0:T(8,128)(2,1)S(1)} %get-tuple-element.8), channel_id=1, source_target_pairs={{0,192},{16,208},{32,224},{48,240},{64,0},{80,16},{96,32},{112,48}... | collective-permute-start | bytes 1474568 | tf_op jit(solution)/shard_map/ppermute | solution.py:19
  49.5 12.6 %collective-permute-start.7 = (bf16[4,2,15,16,128]{4,3,2,1,0:T(8,128)(2,1)S(1)}, bf16[4,2,15,16,128]{4,3,2,1,0:T(8,128)(2,1)S(1)}, u32[]{:S(2)}, u32[]{:S(2)}) collective-permute-start(bf16[4,2,15,16,128]{4,3,2,1,0:T(8,128)(2,1)S(1)} %get-tuple-element.8), channel_id=1, source_target_pairs={{0,64},{16,80},{32,96},{48,112},{64,128},{80,144},{96,160},{112,17... | collective-permute-start | bytes 1474568 | tf_op jit(solution)/shard_map/ppermute | solution.py:18
  52.8 21.9 %collective-permute-start.11 = (bf16[4,4,15,8,128]{4,3,2,1,0:T(8,128)(2,1)S(1)}, bf16[4,4,15,8,128]{4,3,2,1,0:T(8,128)(2,1)S(1)}, u32[]{:S(2)}, u32[]{:S(2)}) collective-permute-start(bf16[4,4,15,8,128]{4,3,2,1,0:T(8,128)(2,1)S(1)} %copy-done.10), channel_id=1, source_target_pairs={{0,32},{16,48},{32,0},{48,16},{64,96},{80,112},{96,64},{112,80},{1... | collective-permute-start | bytes 1474568 | tf_op jit(solution)/shard_map/ppermute | solution.py:47
  62.0 13.9 %collective-permute-start.10 = (bf16[2,2,15,16,128]{4,3,2,1,0:T(8,128)(2,1)S(1)}, bf16[2,2,15,16,128]{4,3,2,1,0:T(8,128)(2,1)S(1)}, u32[]{:S(2)}, u32[]{:S(2)}) collective-permute-start(bf16[2,2,15,16,128]{4,3,2,1,0:T(8,128)(2,1)S(1)} %slice.139), channel_id=1, source_target_pairs={{0,192},{16,208},{32,224},{48,240},{64,0},{80,16},{96,32},{112,48}... | collective-permute-start | bytes 737288 | tf_op jit(solution)/shard_map/ppermute | solution.py:22
  62.2 13.7 %collective-permute-start.8 = (bf16[2,2,15,16,128]{4,3,2,1,0:T(8,128)(2,1)S(1)}, bf16[2,2,15,16,128]{4,3,2,1,0:T(8,128)(2,1)S(1)}, u32[]{:S(2)}, u32[]{:S(2)}) collective-permute-start(bf16[2,2,15,16,128]{4,3,2,1,0:T(8,128)(2,1)S(1)} %slice.138), channel_id=1, source_target_pairs={{0,64},{16,80},{32,96},{48,112},{64,128},{80,144},{96,160},{112,17... | collective-permute-start | bytes 737288 | tf_op jit(solution)/shard_map/ppermute | solution.py:21
  74.7 3.0 %collective-permute-start.12 = (bf16[4,2,15,8,128]{4,3,2,1,0:T(8,128)(2,1)S(1)}, bf16[4,2,15,8,128]{4,3,2,1,0:T(8,128)(2,1)S(1)}, u32[]{:S(2)}, u32[]{:S(2)}) collective-permute-start(bf16[4,2,15,8,128]{4,3,2,1,0:T(8,128)(2,1)S(1)} %get-tuple-element.13), channel_id=1, source_target_pairs={{0,16},{16,0},{32,48},{48,32},{64,80},{80,64},{96,112},{112,96},{1... | collective-permute-start | bytes 737288 | tf_op jit(solution)/shard_map/ppermute | solution.py:30
  78.8 25.7 %copy-start.12 = (s32[60]{0:T(128)S(1)}, s32[60]{0:T(128)}, u32[]{:S(2)}) copy-start(s32[60]{0:T(128)} %param.7) | copy-start | bytes 724
  78.8 25.7 %copy-start.11 = (s32[8]{0:T(128)S(1)}, s32[8]{0:T(128)}, u32[]{:S(2)}) copy-start(s32[8]{0:T(128)} %param.6) | copy-start | bytes 100
  78.8 13.6 %collective-permute-start.13 = (bf16[4,2,15,16,128]{4,3,2,1,0:T(8,128)(2,1)S(1)}, bf16[4,2,15,16,128]{4,3,2,1,0:T(8,128)(2,1)S(1)}, u32[]{:S(2)}, u32[]{:S(2)}) collective-permute-start(bf16[4,2,15,16,128]{4,3,2,1,0:T(8,128)(2,1)S(1)} %get-tuple-element.6), channel_id=1, source_target_pairs={{0,64},{16,80},{32,96},{48,112},{64,128},{80,144},{96,160},{112,17... | collective-permute-start | bytes 1474568 | tf_op jit(solution)/shard_map/ppermute | solution.py:18
  79.1 14.9 %collective-permute-start.15 = (bf16[4,2,15,16,128]{4,3,2,1,0:T(8,128)(2,1)S(1)}, bf16[4,2,15,16,128]{4,3,2,1,0:T(8,128)(2,1)S(1)}, u32[]{:S(2)}, u32[]{:S(2)}) collective-permute-start(bf16[4,2,15,16,128]{4,3,2,1,0:T(8,128)(2,1)S(1)} %get-tuple-element.6), channel_id=1, source_target_pairs={{0,192},{16,208},{32,224},{48,240},{64,0},{80,16},{96,32},{112,48}... | collective-permute-start | bytes 1474568 | tf_op jit(solution)/shard_map/ppermute | solution.py:19
  92.4 7.6 %collective-permute-start.14 = (bf16[2,2,15,16,128]{4,3,2,1,0:T(8,128)(2,1)S(1)}, bf16[2,2,15,16,128]{4,3,2,1,0:T(8,128)(2,1)S(1)}, u32[]{:S(2)}, u32[]{:S(2)}) collective-permute-start(bf16[2,2,15,16,128]{4,3,2,1,0:T(8,128)(2,1)S(1)} %slice.142), channel_id=1, source_target_pairs={{0,64},{16,80},{32,96},{48,112},{64,128},{80,144},{96,160},{112,17... | collective-permute-start | bytes 737288 | tf_op jit(solution)/shard_map/ppermute | solution.py:21
  94.1 8.5 %collective-permute-start.16 = (bf16[2,2,15,16,128]{4,3,2,1,0:T(8,128)(2,1)S(1)}, bf16[2,2,15,16,128]{4,3,2,1,0:T(8,128)(2,1)S(1)}, u32[]{:S(2)}, u32[]{:S(2)}) collective-permute-start(bf16[2,2,15,16,128]{4,3,2,1,0:T(8,128)(2,1)S(1)} %slice.143), channel_id=1, source_target_pairs={{0,192},{16,208},{32,224},{48,240},{64,0},{80,16},{96,32},{112,48}... | collective-permute-start | bytes 737288 | tf_op jit(solution)/shard_map/ppermute | solution.py:22
  104.4 103.5 %collective-permute-start.24 = (bf16[8,2,15,128,128]{4,3,2,1,0:T(8,128)(2,1)}, bf16[8,2,15,128,128]{4,3,2,1,0:T(8,128)(2,1)}, u32[]{:S(2)}, u32[]{:S(2)}) collective-permute-start(bf16[8,2,15,128,128]{4,3,2,1,0:T(8,128)(2,1)} %constant_dynamic-update-slice_fusion), channel_id=1, source_target_pairs={{0,16},{16,0},{32,48},{48,32},{64,80},{80,64},{96,112},{112,96},{1... | collective-permute-start | bytes 23592968 | tf_op jit(solution)/shard_map/ppermute | solution.py:62
  107.3 46.5 %collective-permute-start.18 = (bf16[8,2,15,32,128]{4,3,2,1,0:T(8,128)(2,1)S(1)}, bf16[8,2,15,32,128]{4,3,2,1,0:T(8,128)(2,1)S(1)}, u32[]{:S(2)}, u32[]{:S(2)}) collective-permute-start(bf16[8,2,15,32,128]{4,3,2,1,0:T(8,128)(2,1)S(1)} %broadcast_select_fusion), channel_id=1, source_target_pairs={{0,4},{4,8},{8,12},{12,0},{1,5},{5,9},{9,13},{13,1},{2,6},{6,10},{... | collective-permute-start | bytes 5898248 | tf_op jit(solution)/shard_map/ppermute | solution.py:71
  109.1 46.4 %collective-permute-start.17 = (bf16[8,2,15,32,128]{4,3,2,1,0:T(8,128)(2,1)S(1)}, bf16[8,2,15,32,128]{4,3,2,1,0:T(8,128)(2,1)S(1)}, u32[]{:S(2)}, u32[]{:S(2)}) collective-permute-start(bf16[8,2,15,32,128]{4,3,2,1,0:T(8,128)(2,1)S(1)} %broadcast_select_fusion), channel_id=1, source_target_pairs={{0,12},{4,0},{8,4},{12,8},{1,13},{5,1},{9,5},{13,9},{2,14},{6,2},{... | collective-permute-start | bytes 5898248 | tf_op jit(solution)/shard_map/ppermute | solution.py:72
  153.8 1.6 copy-start
  155.0 24.7 %collective-permute-start.19 = (bf16[4,2,15,32,128]{4,3,2,1,0:T(8,128)(2,1)}, bf16[4,2,15,32,128]{4,3,2,1,0:T(8,128)(2,1)S(1)}, u32[]{:S(2)}, u32[]{:S(2)}) collective-permute-start(bf16[4,2,15,32,128]{4,3,2,1,0:T(8,128)(2,1)} %slice.144), channel_id=1, source_target_pairs={{0,4},{4,8},{8,12},{12,0},{1,5},{5,9},{9,13},{13,1},{2,6},{6,10},{... | collective-permute-start | bytes 2949128 | tf_op jit(solution)/shard_map/ppermute | solution.py:74
  155.5 1.6 copy-start.2
  157.1 23.6 %collective-permute-start.20 = (bf16[4,2,15,32,128]{4,3,2,1,0:T(8,128)(2,1)}, bf16[4,2,15,32,128]{4,3,2,1,0:T(8,128)(2,1)}, u32[]{:S(2)}, u32[]{:S(2)}) collective-permute-start(bf16[4,2,15,32,128]{4,3,2,1,0:T(8,128)(2,1)} %slice.145), channel_id=1, source_target_pairs={{0,12},{4,0},{8,4},{12,8},{1,13},{5,1},{9,5},{13,9},{2,14},{6,2},{... | collective-permute-start | bytes 2949128 | tf_op jit(solution)/shard_map/ppermute | solution.py:75
  179.8 3.9 %copy-start.1 = (bf16[8,2,15,32,128]{4,3,2,1,0:T(8,128)(2,1)S(1)}, bf16[8,2,15,32,128]{4,3,2,1,0:T(8,128)(2,1)}, u32[]{:S(2)}) copy-start(bf16[8,2,15,32,128]{4,3,2,1,0:T(8,128)(2,1)} %copy-done) | copy-start | bytes 5898244
  179.8 5.3 %copy-start.3 = (bf16[8,2,15,32,128]{4,3,2,1,0:T(8,128)(2,1)S(1)}, bf16[8,2,15,32,128]{4,3,2,1,0:T(8,128)(2,1)}, u32[]{:S(2)}) copy-start(bf16[8,2,15,32,128]{4,3,2,1,0:T(8,128)(2,1)} %copy-done.2) | copy-start | bytes 5898244
  187.9 15.5 %collective-permute-start.21 = (f32[2,2,128,2,128]{4,2,3,1,0:T(8,128)S(1)}, f32[2,2,128,2,128]{4,2,3,1,0:T(8,128)S(1)}, u32[]{:S(2)}, u32[]{:S(2)}) collective-permute-start(f32[2,2,128,2,128]{4,2,3,1,0:T(8,128)S(1)} %fusion.22), channel_id=1, source_target_pairs={{0,1},{1,2},{2,3},{3,0},{4,5},{5,6},{6,7},{7,4},{8,9},{9,10},{10,1... | collective-permute-start | bytes 1572872 | tf_op jit(solution)/shard_map/ppermute | solution.py:91
  202.9 7.8 %copy-start.4 = (f32[8,2,128,2,128]{4,2,3,1,0:T(8,128)}, f32[8,2,128,2,128]{4,2,3,1,0:T(8,128)S(1)}, u32[]{:S(2)}) copy-start(f32[8,2,128,2,128]{4,2,3,1,0:T(8,128)S(1)} %bitcast_add_fusion.3) | copy-start | bytes 6291460
  203.6 28.6 %collective-permute-start.22 = (f32[2,2,128,2,128]{4,2,3,1,0:T(8,128)S(1)}, f32[2,2,128,2,128]{4,2,3,1,0:T(8,128)S(1)}, u32[]{:S(2)}, u32[]{:S(2)}) collective-permute-start(f32[2,2,128,2,128]{4,2,3,1,0:T(8,128)S(1)} %dynamic-slice_add_fusion.5), channel_id=1, source_target_pairs={{0,1},{1,2},{2,3},{3,0},{4,5},{5,6},{6,7},{7,4},{8,9},{9,10},{10,1... | collective-permute-start | bytes 1572872 | tf_op jit(solution)/shard_map/ppermute | solution.py:91
  213.6 15.9 %collective-permute-start.25 = (f32[2,2,128,2,128]{4,2,3,1,0:T(8,128)S(1)}, f32[2,2,128,2,128]{4,2,3,1,0:T(8,128)S(1)}, u32[]{:S(2)}, u32[]{:S(2)}) collective-permute-start(f32[2,2,128,2,128]{4,2,3,1,0:T(8,128)S(1)} %fusion.25), channel_id=1, source_target_pairs={{0,3},{1,0},{2,1},{3,2},{4,7},{5,4},{6,5},{7,6},{8,11},{9,8},{10,9... | collective-permute-start | bytes 1572872 | tf_op jit(solution)/shard_map/ppermute | solution.py:91
  220.9 11.2 %copy-start.5 = (f32[8,2,128,2,128]{4,2,3,1,0:T(8,128)S(1)}, f32[8,2,128,2,128]{4,2,3,1,0:T(8,128)}, u32[]{:S(2)}) copy-start(f32[8,2,128,2,128]{4,2,3,1,0:T(8,128)} %copy-done.4) | copy-start | bytes 6291460
  223.7 5.8 %copy-start.6 = (f32[8,2,128,2,128]{4,2,3,1,0:T(8,128)}, f32[8,2,128,2,128]{4,2,3,1,0:T(8,128)S(1)}, u32[]{:S(2)}) copy-start(f32[8,2,128,2,128]{4,2,3,1,0:T(8,128)S(1)} %bitcast_add_fusion) | copy-start | bytes 6291460
  230.3 17.0 %collective-permute-start.26 = (f32[2,2,128,2,128]{4,2,3,1,0:T(8,128)}, f32[2,2,128,2,128]{4,2,3,1,0:T(8,128)}, u32[]{:S(2)}, u32[]{:S(2)}) collective-permute-start(f32[2,2,128,2,128]{4,2,3,1,0:T(8,128)} %dynamic-slice_add_fusion.2), channel_id=1, source_target_pairs={{0,3},{1,0},{2,1},{3,2},{4,7},{5,4},{6,5},{7,6},{8,11},{9,8},{10,9... | collective-permute-start | bytes 1572872 | tf_op jit(solution)/shard_map/ppermute | solution.py:91
  233.0 25.8 %collective-permute-start.23 = (f32[2,2,128,2,128]{4,2,3,1,0:T(8,128)}, f32[2,2,128,2,128]{4,2,3,1,0:T(8,128)S(1)}, u32[]{:S(2)}, u32[]{:S(2)}) collective-permute-start(f32[2,2,128,2,128]{4,2,3,1,0:T(8,128)} %dynamic-slice_add_fusion.4), channel_id=1, source_target_pairs={{0,1},{1,2},{2,3},{3,0},{4,5},{5,6},{6,7},{7,4},{8,9},{9,10},{10,1... | collective-permute-start | bytes 1572872 | tf_op jit(solution)/shard_map/ppermute | solution.py:91
  249.3 21.6 %collective-permute-start.27 = (f32[2,2,128,2,128]{4,2,3,1,0:T(8,128)}, f32[2,2,128,2,128]{4,2,3,1,0:T(8,128)S(1)}, u32[]{:S(2)}, u32[]{:S(2)}) collective-permute-start(f32[2,2,128,2,128]{4,2,3,1,0:T(8,128)} %dynamic-slice_add_fusion.1), channel_id=1, source_target_pairs={{0,3},{1,0},{2,1},{3,2},{4,7},{5,4},{6,5},{7,6},{8,11},{9,8},{10,9... | collective-permute-start | bytes 1572872 | tf_op jit(solution)/shard_map/ppermute | solution.py:91

commit v10 on v8

--- a/solution.py
+++ b/solution.py
@@ -53,13 +53,15 @@
         mine = lax.dynamic_update_slice_in_dim(
             mine, piece, ((pos - step) % 4) * 4 * ncc + zh * 2 * ncc, axis=3
         )
+    halves = []
     for goff, zpart in ((0, zh_lo), (hg, zh_hi)):
         far = ring4_pieces(core_quad(zpart, core, nrow, hj), "row", nrow, 4)
         for step, piece in enumerate(far):
             mine = lax.dynamic_update_slice(
                 mine, piece, (goff, 0, 0, ((pos - step) % 4) * 4 * ncc + (1 - zh) * 2 * ncc, 0)
             )
-    other = lax.ppermute(mine, "row", [(i, i ^ 1) for i in range(nrow)])
+        halves.append(lax.ppermute(mine[goff:goff + hg], "row", [(i, i ^ 1) for i in range(nrow)]))
+    other = jnp.concatenate(halves, axis=0)
     return mine, other
 
 
@@ -77,18 +79,18 @@
     return [w, from_right, opp, from_left]
 
 
-def ring_reduce_scatter(part):
+def ring_reduce_scatter(part, dirn):
     n = lax.axis_size("rep")
     d = lax.axis_index("rep")
     width = part.shape[0] // n
-    fwd = [(i, (i + 1) % n) for i in range(n)]
+    perm = [(i, (i + dirn) % n) for i in range(n)]
 
     def chunk(t):
         return lax.dynamic_slice_in_dim(part, (t % n) * width, width, axis=0)
 
-    acc = chunk(d + n - 1)
+    acc = chunk(d + n - dirn)
     for step in range(1, n):
-        acc = lax.ppermute(acc, "rep", fwd) + chunk(d + 2 * n - step - 1)
+        acc = lax.ppermute(acc, "rep", perm) + chunk(d + 2 * n - (step + 1) * dirn)
     return acc
 
 
@@ -127,9 +129,9 @@
             )
             part = term if part is None else part + term
         if name == "em":
-            sums.append(ring_reduce_scatter(part))
+            sums.append(ring_reduce_scatter(part, 1))
         else:
-            sums.append(lax.psum_scatter(part, "rep", scatter_dimension=0, tiled=True))
+            sums.append(ring_reduce_scatter(part, -1))
     summed = jnp.where(
         core == 0, jnp.concatenate(sums, axis=3), jnp.concatenate(sums[::-1], axis=3)
     )

time: 287 us -> 250 us (0.87)
  the two profiles are of different devices: /device:TPU:1 before, /device:TPU:24 now
where the time goes in v10:
time: 250 us; the launch traced here: 249 us
  waiting for transfers between devices  112 us (45%)
  starting transfers between devices  62.8 us (25%)
  local copies, waits for them, and re-layouts  39.6 us (16%)
  matrix products  17.9 us (7%)
  other arithmetic  16.2 us (6%)
    ppermute x6, waiting for transfers between devices, ring_reduce_scatter(): acc = lax.ppermute(acc, 'rep', perm) + chunk(d + 2 * n - (step + 1) * dirn)  39.2 us
    ppermute x6, starting transfers between devices, ring_reduce_scatter(): acc = lax.ppermute(acc, 'rep', perm) + chunk(d + 2 * n - (step + 1) * dirn)  29 us
    ppermute x3, waiting for transfers between devices, ring4_pieces(): from_left = lax.ppermute(block, axis, fwd)  20.7 us
    dot_general x8, matrix products, body(): jnp.einsum('gikca,gjkcb->giajb', w_blk, t_half[:, :, :, s * width:(s + 1)...  17.9 us
    ppermute x1, waiting for transfers between devices, gather_integrals(): opp_hi = lax.ppermute(from_right[half:], 'col', bwd)  12.8 us
    ppermute x1, waiting for transfers between devices, gather_integrals(): from_right = lax.ppermute(w, 'col', bwd)  12.5 us
    ppermute x3, starting transfers between devices, ring4_pieces(): opp_hi = lax.ppermute(from_right[half:], axis, bwd)  10.4 us
    slice x2, local copies, waits for them, and re-layouts, gather_amplitudes(): mine[goff:goff + hg]  9.04 us
  transfers between devices with their start and end apart: 29, of which 19 were waited for; matrix products, arithmetic and copies ran while one was open for 27% of the time, Pallas kernels for 0%

profile of v10, /device:TPU:24, one launch (start us, length us, event | category | flops | bytes accessed | tf_op | source)
XLA Modules:
  0.0 249.2 jit_solution(4113225826096001075)
XLA Ops:
  0.0 1.3 broadcast_select_fusion.2
  1.5 1.9 collective-permute-done
  3.7 1.6 collective-permute-start.1
  5.3 1.7 collective-permute-start.3
  7.0 1.0 fusion.22
  8.0 7.2 %collective-permute-start.5 = (bf16[4,4,15,8,128]{4,3,2,1,0:T(8,128)(2,1)}, bf16[4,4,15,8,128]{4,3,2,1,0:T(8,128)(2,1)S(1)}, u32[]{:S(2)}, u32[]{:S(2)}) collective-permute-start(bf16[4,4,15,8,128]{4,3,2,1,0:T(8,128)(2,1)} %get-tuple-element.10), channel_id=1, source_target_pairs={{0,32},{16,48},{32,0},{48,16},{64,96},{80,112},{96,64},{112,80},{1... | collective-permute-start | bytes 1474568 | tf_op jit(solution)/shard_map/ppermute | solution.py:46
  15.5 13.4 %collective-permute-done.1 = bf16[8,2,15,16,128]{4,3,2,1,0:T(8,128)(2,1)} collective-permute-done((bf16[8,2,15,16,128]{4,3,2,1,0:T(8,128)(2,1)S(1)}, bf16[8,2,15,16,128]{4,3,2,1,0:T(8,128)(2,1)}, u32[]{:S(2)}, u32[]{:S(2)}) %collective-permute-start.1) | collective-permute-done | bytes 983072 | tf_op jit(solution)/shard_map/ppermute | solution.py:18
  28.9 1.9 slice.110
  31.9 3.0 %collective-permute-start.4 = (bf16[4,2,15,16,128]{4,3,2,1,0:T(8,128)(2,1)}, bf16[4,2,15,16,128]{4,3,2,1,0:T(8,128)(2,1)}, u32[]{:S(2)}, u32[]{:S(2)}) collective-permute-start(bf16[4,2,15,16,128]{4,3,2,1,0:T(8,128)(2,1)} %slice.111), channel_id=1, source_target_pairs={{0,192},{16,208},{32,224},{48,240},{64,0},{80,16},{96,32},{112,48}... | collective-permute-start | bytes 1474568 | tf_op jit(solution)/shard_map/ppermute | solution.py:22
  35.0 5.1 %broadcast_in_dim.56 = bf16[8,2,15,128,128]{4,3,2,1,0:T(8,128)(2,1)} broadcast(bf16[]{:T(256)} %constant.161.clone.1), dimensions={} | broadcast | bytes 7864322 | tf_op jit(solution)/shard_map/broadcast_in_dim | solution.py:50
  40.1 2.4 constant_dynamic-update-slice_fusion.10
  42.5 2.1 collective-permute-done.2
  44.8 2.2 maximum_dynamic-update-slice_fusion
  47.0 1.2 constant_dynamic-update-slice_fusion.9
  48.2 1.2 constant_dynamic-update-slice_fusion.8
  49.4 1.2 constant_dynamic-update-slice_fusion.7
  50.6 1.0 collective-permute-start.7
  51.6 2.7 %collective-permute-start.9 = (bf16[4,2,15,16,128]{4,3,2,1,0:T(8,128)(2,1)}, bf16[4,2,15,16,128]{4,3,2,1,0:T(8,128)(2,1)S(1)}, u32[]{:S(2)}, u32[]{:S(2)}) collective-permute-start(bf16[4,2,15,16,128]{4,3,2,1,0:T(8,128)(2,1)} %get-tuple-element.8), channel_id=1, source_target_pairs={{0,192},{16,208},{32,224},{48,240},{64,0},{80,16},{96,32},{112,48}... | collective-permute-start | bytes 1474568 | tf_op jit(solution)/shard_map/ppermute | solution.py:19
  55.2 2.0 collective-permute-start.18
  57.3 6.1 %collective-permute-done.9 = bf16[4,2,15,16,128]{4,3,2,1,0:T(8,128)(2,1)S(1)} collective-permute-done((bf16[4,2,15,16,128]{4,3,2,1,0:T(8,128)(2,1)}, bf16[4,2,15,16,128]{4,3,2,1,0:T(8,128)(2,1)S(1)}, u32[]{:S(2)}, u32[]{:S(2)}) %collective-permute-start.9) | collective-permute-done | bytes 491552 | tf_op jit(solution)/shard_map/ppermute | solution.py:19
  63.4 3.7 %collective-permute-start.10 = (bf16[2,2,15,16,128]{4,3,2,1,0:T(8,128)(2,1)S(1)}, bf16[2,2,15,16,128]{4,3,2,1,0:T(8,128)(2,1)S(1)}, u32[]{:S(2)}, u32[]{:S(2)}) collective-permute-start(bf16[2,2,15,16,128]{4,3,2,1,0:T(8,128)(2,1)S(1)} %slice.115), channel_id=1, source_target_pairs={{0,192},{16,208},{32,224},{48,240},{64,0},{80,16},{96,32},{112,48}... | collective-permute-start | bytes 737288 | tf_op jit(solution)/shard_map/ppermute | solution.py:22
  67.5 0.9 constant_dynamic-update-slice_fusion.6
  68.5 2.3 collective-permute-done.10
  70.8 4.0 %collective-permute-done.8 = bf16[2,2,15,16,128]{4,3,2,1,0:T(8,128)(2,1)S(1)} collective-permute-done((bf16[2,2,15,16,128]{4,3,2,1,0:T(8,128)(2,1)S(1)}, bf16[2,2,15,16,128]{4,3,2,1,0:T(8,128)(2,1)S(1)}, u32[]{:S(2)}, u32[]{:S(2)}) %collective-permute-start.8) | collective-permute-done | bytes 245792 | tf_op jit(solution)/shard_map/ppermute | solution.py:21
  74.8 0.9 maximum_dynamic-update-slice_fusion.1
  76.6 4.5 %slice.126 = bf16[4,2,15,128,128]{4,3,2,1,0:T(8,128)(2,1)} slice(bf16[8,2,15,128,128]{4,3,2,1,0:T(8,128)(2,1)} %constant_dynamic-update-slice_fusion.5), slice={[0:4], [0:2], [0:15], [0:128], [0:128]} | slice | bytes 7864320 | tf_op jit(solution)/shard_map/slice | solution.py:63
  81.1 1.0 constant_dynamic-update-slice_fusion.4
  82.9 3.2 %collective-permute-start.15 = (bf16[4,2,15,16,128]{4,3,2,1,0:T(8,128)(2,1)S(1)}, bf16[4,2,15,16,128]{4,3,2,1,0:T(8,128)(2,1)S(1)}, u32[]{:S(2)}, u32[]{:S(2)}) collective-permute-start(bf16[4,2,15,16,128]{4,3,2,1,0:T(8,128)(2,1)S(1)} %get-tuple-element.6), channel_id=1, source_target_pairs={{0,192},{16,208},{32,224},{48,240},{64,0},{80,16},{96,32},{112,48}... | collective-permute-start | bytes 1474568 | tf_op jit(solution)/shard_map/ppermute | solution.py:19
  86.1 7.3 %collective-permute-done.13 = bf16[4,2,15,16,128]{4,3,2,1,0:T(8,128)(2,1)S(1)} collective-permute-done((bf16[4,2,15,16,128]{4,3,2,1,0:T(8,128)(2,1)S(1)}, bf16[4,2,15,16,128]{4,3,2,1,0:T(8,128)(2,1)S(1)}, u32[]{:S(2)}, u32[]{:S(2)}) %collective-permute-start.13) | collective-permute-done | bytes 491552 | tf_op jit(solution)/shard_map/ppermute | solution.py:18
  94.2 3.8 %collective-permute-start.16 = (bf16[2,2,15,16,128]{4,3,2,1,0:T(8,128)(2,1)S(1)}, bf16[2,2,15,16,128]{4,3,2,1,0:T(8,128)(2,1)S(1)}, u32[]{:S(2)}, u32[]{:S(2)}) collective-permute-start(bf16[2,2,15,16,128]{4,3,2,1,0:T(8,128)(2,1)S(1)} %slice.119), channel_id=1, source_target_pairs={{0,192},{16,208},{32,224},{48,240},{64,0},{80,16},{96,32},{112,48}... | collective-permute-start | bytes 737288 | tf_op jit(solution)/shard_map/ppermute | solution.py:22
  97.9 0.9 constant_dynamic-update-slice_fusion.3
  98.8 2.1 collective-permute-done.14
  101.6 0.9 maximum_dynamic-update-slice_fusion.2
  102.6 0.9 constant_dynamic-update-slice_fusion.2
  103.5 4.5 %slice.127 = bf16[4,2,15,128,128]{4,3,2,1,0:T(8,128)(2,1)} slice(bf16[8,2,15,128,128]{4,3,2,1,0:T(8,128)(2,1)} %constant_dynamic-update-slice_fusion.2), slice={[4:8], [0:2], [0:15], [0:128], [0:128]} | slice | bytes 7864320 | tf_op jit(solution)/shard_map/slice | solution.py:63
  108.0 1.3 slice.122
  109.3 2.2 collective-permute-start.19
  111.5 12.5 %collective-permute-done.17 = bf16[8,2,15,32,128]{4,3,2,1,0:T(8,128)(2,1)S(1)} collective-permute-done((bf16[8,2,15,32,128]{4,3,2,1,0:T(8,128)(2,1)S(1)}, bf16[8,2,15,32,128]{4,3,2,1,0:T(8,128)(2,1)S(1)}, u32[]{:S(2)}, u32[]{:S(2)}) %collective-permute-start.17) | collective-permute-done | bytes 1966112 | tf_op jit(solution)/shard_map/ppermute | solution.py:74
  124.0 1.3 copy-done
  125.2 1.0 slice.123
  126.3 7.4 %collective-permute-done.19 = bf16[4,2,15,32,128]{4,3,2,1,0:T(8,128)(2,1)} collective-permute-done((bf16[4,2,15,32,128]{4,3,2,1,0:T(8,128)(2,1)S(1)}, bf16[4,2,15,32,128]{4,3,2,1,0:T(8,128)(2,1)}, u32[]{:S(2)}, u32[]{:S(2)}) %collective-permute-start.19) | collective-permute-done | bytes 983072 | tf_op jit(solution)/shard_map/ppermute | solution.py:76
  133.7 12.8 %collective-permute-done.20 = bf16[4,2,15,32,128]{4,3,2,1,0:T(8,128)(2,1)} collective-permute-done((bf16[4,2,15,32,128]{4,3,2,1,0:T(8,128)(2,1)}, bf16[4,2,15,32,128]{4,3,2,1,0:T(8,128)(2,1)}, u32[]{:S(2)}, u32[]{:S(2)}) %collective-permute-start.20) | collective-permute-done | bytes 983072 | tf_op jit(solution)/shard_map/ppermute | solution.py:77
  146.4 3.0 %fusion.5 = f32[8,2,128,2,128,1]{4,2,5,3,1,0:T(8,128)S(1)} fusion(bf16[8,2,15,128,128]{4,3,2,1,0:T(8,128)(2,1)} %constant_dynamic-update-slice_fusion.2, bf16[4,2,15,32,128]{4,3,2,1,0:T(8,128)(2,1)} %collective-permute-done.20, bf16[4,2,15,32,128]{4,3,2,1,0:T(8,128)(2,1)} %collective-permute-done.19), kind=kOutput, calls=%fused_computation.17 | convolution fusion | flops 507248640 | bytes 6029312 | tf_op jit(solution)/shard_map/gikca,gjkcb->giajb/dot_general | solution.py:124
  149.4 2.5 %fusion.7 = f32[8,2,128,2,128,1]{4,2,5,3,1,0:T(8,128)S(1)} fusion(bf16[8,2,15,128,128]{4,3,2,1,0:T(8,128)(2,1)} %constant_dynamic-update-slice_fusion.2, bf16[8,2,15,32,128]{4,3,2,1,0:T(8,128)(2,1)S(1)} %broadcast_select_fusion), kind=kOutput, calls=%fused_computation.21 | convolution fusion | flops 503316480 | bytes 6029312 | tf_op jit(solution)/shard_map/gikca,gjkcb->giajb/dot_general | solution.py:124
  152.0 2.4 fusion.6
  154.4 3.2 %bitcast_add_fusion.3 = f32[8,2,128,2,128]{4,2,3,1,0:T(8,128)S(1)} fusion(f32[8,2,128,2,128,1]{4,2,5,3,1,0:T(8,128)S(1)} %fusion.5, f32[8,2,128,2,128,1]{4,2,5,3,1,0:T(8,128)S(1)} %fusion.6, f32[8,2,128,2,128,1]{4,2,5,3,1,0:T(8,128)S(1)} %fusion.7, bf16[8,2,15,128,128]{4,3,2,1,0:T(8,128)(2,1)} %constant_dynamic-update-slice_fusion.2, ...), kind=kOutput, calls=%fused_computation.3 | convolution fusion | flops 504889344 | bytes 12320768 | tf_op jit(solution)/shard_map/gikca,gjkcb->giajb/dot_general | solution.py:124
  157.6 0.9 constant_dynamic-slice_fusion.1
  158.5 14.0 %collective-permute-start.21 = (f32[2,2,128,2,128]{4,2,3,1,0:T(8,128)}, f32[2,2,128,2,128]{4,2,3,1,0:T(8,128)S(1)}, u32[]{:S(2)}, u32[]{:S(2)}) collective-permute-start(f32[2,2,128,2,128]{4,2,3,1,0:T(8,128)} %constant_dynamic-slice_fusion.1), channel_id=1, source_target_pairs={{0,1},{1,2},{2,3},{3,0},{4,5},{5,6},{6,7},{7,4},{8,9},{9,10},{10,1... | collective-permute-start | bytes 1572872 | tf_op jit(solution)/shard_map/ppermute | solution.py:93
  172.5 2.4 constant_dynamic-update-slice_fusion.1
  175.0 2.9 %constant_dynamic-update-slice_fusion = bf16[8,2,15,128,128]{4,3,2,1,0:T(8,128)(2,1)S(1)} fusion(bf16[8,2,15,128,128]{4,3,2,1,0:T(8,128)(2,1)S(1)} %constant_dynamic-update-slice_fusion.1, bf16[4,2,15,128,128]{4,3,2,1,0:T(8,128)(2,1)} %collective-permute-done.25), kind=kLoop, calls=%fused_computation.55 | loop fusion | bytes 7864320 | tf_op jit(solution)/shard_map/concatenate | solution.py:64
  178.7 2.3 fusion.1
  181.9 2.8 %bitcast_add_fusion = f32[8,2,128,2,128]{4,2,3,1,0:T(8,128)S(1)} fusion(f32[8,2,128,2,128,1]{4,2,5,3,1,0:T(8,128)S(1)} %fusion.1, f32[8,2,128,2,128,1]{4,2,5,3,1,0:T(8,128)S(1)} %fusion.2, f32[8,2,128,2,128,1]{4,2,5,3,1,0:T(8,128)S(1)} %fusion.3, bf16[8,2,15,128,128]{4,3,2,1,0:T(8,128)(2,1)S(1)} %constant_dynamic-update-slice_fusion, ...), kind=kOutput, calls=%fused_computation | convolution fusion | flops 504889344 | bytes 12320768 | tf_op jit(solution)/shard_map/gikca,gjkcb->giajb/dot_general | solution.py:124
  184.6 1.3 copy-done.4
  187.6 12.4 %collective-permute-start.22 = (f32[2,2,128,2,128]{4,2,3,1,0:T(8,128)}, f32[2,2,128,2,128]{4,2,3,1,0:T(8,128)S(1)}, u32[]{:S(2)}, u32[]{:S(2)}) collective-permute-start(f32[2,2,128,2,128]{4,2,3,1,0:T(8,128)} %dynamic-slice_add_fusion.5), channel_id=1, source_target_pairs={{0,1},{1,2},{2,3},{3,0},{4,5},{5,6},{6,7},{7,4},{8,9},{9,10},{10,1... | collective-permute-start | bytes 1572872 | tf_op jit(solution)/shard_map/ppermute | solution.py:93
  200.0 7.3 %collective-permute-done.26 = f32[2,2,128,2,128]{4,2,3,1,0:T(8,128)S(1)} collective-permute-done((f32[2,2,128,2,128]{4,2,3,1,0:T(8,128)}, f32[2,2,128,2,128]{4,2,3,1,0:T(8,128)S(1)}, u32[]{:S(2)}, u32[]{:S(2)}) %collective-permute-start.26) | collective-permute-done | bytes 524320 | tf_op jit(solution)/shard_map/ppermute | solution.py:93
  207.3 1.9 dynamic-slice_add_fusion.2
  209.3 9.7 %collective-permute-done.22 = f32[2,2,128,2,128]{4,2,3,1,0:T(8,128)S(1)} collective-permute-done((f32[2,2,128,2,128]{4,2,3,1,0:T(8,128)}, f32[2,2,128,2,128]{4,2,3,1,0:T(8,128)S(1)}, u32[]{:S(2)}, u32[]{:S(2)}) %collective-permute-start.22) | collective-permute-done | bytes 524320 | tf_op jit(solution)/shard_map/ppermute | solution.py:93
  219.9 2.6 %collective-permute-start.23 = (f32[2,2,128,2,128]{4,2,3,1,0:T(8,128)}, f32[2,2,128,2,128]{4,2,3,1,0:T(8,128)S(1)}, u32[]{:S(2)}, u32[]{:S(2)}) collective-permute-start(f32[2,2,128,2,128]{4,2,3,1,0:T(8,128)} %dynamic-slice_add_fusion.4), channel_id=1, source_target_pairs={{0,1},{1,2},{2,3},{3,0},{4,5},{5,6},{6,7},{7,4},{8,9},{9,10},{10,1... | collective-permute-start | bytes 1572872 | tf_op jit(solution)/shard_map/ppermute | solution.py:93
  222.5 7.7 %collective-permute-done.27 = f32[2,2,128,2,128]{4,2,3,1,0:T(8,128)S(1)} collective-permute-done((f32[2,2,128,2,128]{4,2,3,1,0:T(8,128)}, f32[2,2,128,2,128]{4,2,3,1,0:T(8,128)S(1)}, u32[]{:S(2)}, u32[]{:S(2)}) %collective-permute-start.27) | collective-permute-done | bytes 524320 | tf_op jit(solution)/shard_map/ppermute | solution.py:93
  230.1 1.9 dynamic-slice_add_fusion.1
  232.2 9.4 %collective-permute-done.23 = f32[2,2,128,2,128]{4,2,3,1,0:T(8,128)S(1)} collective-permute-done((f32[2,2,128,2,128]{4,2,3,1,0:T(8,128)}, f32[2,2,128,2,128]{4,2,3,1,0:T(8,128)S(1)}, u32[]{:S(2)}, u32[]{:S(2)}) %collective-permute-start.23) | collective-permute-done | bytes 524320 | tf_op jit(solution)/shard_map/ppermute | solution.py:93
  241.6 5.1 %collective-permute-done.28 = f32[2,2,128,2,128]{4,2,3,1,0:T(8,128)S(1)} collective-permute-done((f32[2,2,128,2,128]{4,2,3,1,0:T(8,128)}, f32[2,2,128,2,128]{4,2,3,1,0:T(8,128)S(1)}, u32[]{:S(2)}, u32[]{:S(2)}) %collective-permute-start.28) | collective-permute-done | bytes 524320 | tf_op jit(solution)/shard_map/ppermute | solution.py:93
  246.7 1.1 dynamic-slice_add_fusion
  248.0 1.2 copy.6
  (70 shorter events, 11.3 us)
Async XLA Ops:
  0.0 7.0 %copy-start.5 = (bf16[8,4,15,8,128]{4,3,2,1,0:T(8,128)(2,1)S(1)}, bf16[8,4,15,8,128]{4,3,2,1,0:T(8,128)(2,1)}, u32[]{:S(2)}) copy-start(bf16[8,4,15,8,128]{4,3,2,1,0:T(8,128)(2,1)} %param.5) | copy-start | bytes 2949124
  1.3 13.9 %copy-start.8 = (s32[60]{0:T(128)S(1)}, s32[60]{0:T(128)}, u32[]{:S(2)}) copy-start(s32[60]{0:T(128)} %param.7) | copy-start | bytes 724
  1.3 14.0 %copy-start.7 = (s32[8]{0:T(128)S(1)}, s32[8]{0:T(128)}, u32[]{:S(2)}) copy-start(s32[8]{0:T(128)} %param.6) | copy-start | bytes 100
  1.4 2.0 collective-permute-start
  3.7 25.2 %collective-permute-start.1 = (bf16[8,2,15,16,128]{4,3,2,1,0:T(8,128)(2,1)S(1)}, bf16[8,2,15,16,128]{4,3,2,1,0:T(8,128)(2,1)}, u32[]{:S(2)}, u32[]{:S(2)}) collective-permute-start(bf16[8,2,15,16,128]{4,3,2,1,0:T(8,128)(2,1)S(1)} %maximum_select_fusion.1), channel_id=1, source_target_pairs={{0,64},{16,80},{32,96},{48,112},{64,128},{80,144},{96,160},{112,17... | collective-permute-start | bytes 2949128 | tf_op jit(solution)/shard_map/ppermute | solution.py:18
  5.3 25.8 %collective-permute-start.3 = (bf16[8,2,15,16,128]{4,3,2,1,0:T(8,128)(2,1)S(1)}, bf16[8,2,15,16,128]{4,3,2,1,0:T(8,128)(2,1)S(1)}, u32[]{:S(2)}, u32[]{:S(2)}) collective-permute-start(bf16[8,2,15,16,128]{4,3,2,1,0:T(8,128)(2,1)S(1)} %maximum_select_fusion.1), channel_id=1, source_target_pairs={{0,192},{16,208},{32,224},{48,240},{64,0},{80,16},{96,32},{112,48}... | collective-permute-start | bytes 2949128 | tf_op jit(solution)/shard_map/ppermute | solution.py:19
  8.0 26.9 %collective-permute-start.5 = (bf16[4,4,15,8,128]{4,3,2,1,0:T(8,128)(2,1)}, bf16[4,4,15,8,128]{4,3,2,1,0:T(8,128)(2,1)S(1)}, u32[]{:S(2)}, u32[]{:S(2)}) collective-permute-start(bf16[4,4,15,8,128]{4,3,2,1,0:T(8,128)(2,1)} %get-tuple-element.10), channel_id=1, source_target_pairs={{0,32},{16,48},{32,0},{48,16},{64,96},{80,112},{96,64},{112,80},{1... | collective-permute-start | bytes 1474568 | tf_op jit(solution)/shard_map/ppermute | solution.py:46
  15.2 52.1 %collective-permute-start.11 = (bf16[4,4,15,8,128]{4,3,2,1,0:T(8,128)(2,1)}, bf16[4,4,15,8,128]{4,3,2,1,0:T(8,128)(2,1)S(1)}, u32[]{:S(2)}, u32[]{:S(2)}) collective-permute-start(bf16[4,4,15,8,128]{4,3,2,1,0:T(8,128)(2,1)} %get-tuple-element.9), channel_id=1, source_target_pairs={{0,32},{16,48},{32,0},{48,16},{64,96},{80,112},{96,64},{112,80},{1... | collective-permute-start | bytes 1474568 | tf_op jit(solution)/shard_map/ppermute | solution.py:47
  30.8 13.8 %collective-permute-start.2 = (bf16[4,2,15,16,128]{4,3,2,1,0:T(8,128)(2,1)}, bf16[4,2,15,16,128]{4,3,2,1,0:T(8,128)(2,1)S(1)}, u32[]{:S(2)}, u32[]{:S(2)}) collective-permute-start(bf16[4,2,15,16,128]{4,3,2,1,0:T(8,128)(2,1)} %slice.110), channel_id=1, source_target_pairs={{0,64},{16,80},{32,96},{48,112},{64,128},{80,144},{96,160},{112,17... | collective-permute-start | bytes 1474568 | tf_op jit(solution)/shard_map/ppermute | solution.py:21
  31.9 12.9 %collective-permute-start.4 = (bf16[4,2,15,16,128]{4,3,2,1,0:T(8,128)(2,1)}, bf16[4,2,15,16,128]{4,3,2,1,0:T(8,128)(2,1)}, u32[]{:S(2)}, u32[]{:S(2)}) collective-permute-start(bf16[4,2,15,16,128]{4,3,2,1,0:T(8,128)(2,1)} %slice.111), channel_id=1, source_target_pairs={{0,192},{16,208},{32,224},{48,240},{64,0},{80,16},{96,32},{112,48}... | collective-permute-start | bytes 1474568 | tf_op jit(solution)/shard_map/ppermute | solution.py:22
  34.9 14.4 %collective-permute-start.6 = (bf16[4,2,15,8,128]{4,3,2,1,0:T(8,128)(2,1)S(1)}, bf16[4,2,15,8,128]{4,3,2,1,0:T(8,128)(2,1)S(1)}, u32[]{:S(2)}, u32[]{:S(2)}) collective-permute-start(bf16[4,2,15,8,128]{4,3,2,1,0:T(8,128)(2,1)S(1)} %get-tuple-element.15), channel_id=1, source_target_pairs={{0,16},{16,0},{32,48},{48,32},{64,80},{80,64},{96,112},{112,96},{1... | collective-permute-start | bytes 737288 | tf_op jit(solution)/shard_map/ppermute | solution.py:30
  48.2 6.9 %copy-start.6 = (bf16[8,2,15,32,128]{4,3,2,1,0:T(8,128)(2,1)S(1)}, bf16[8,2,15,32,128]{4,3,2,1,0:T(8,128)(2,1)}, u32[]{:S(2)}) copy-start(bf16[8,2,15,32,128]{4,3,2,1,0:T(8,128)(2,1)} %param.4) | copy-start | bytes 5898244
  50.6 16.5 %collective-permute-start.7 = (bf16[4,2,15,16,128]{4,3,2,1,0:T(8,128)(2,1)}, bf16[4,2,15,16,128]{4,3,2,1,0:T(8,128)(2,1)S(1)}, u32[]{:S(2)}, u32[]{:S(2)}) collective-permute-start(bf16[4,2,15,16,128]{4,3,2,1,0:T(8,128)(2,1)} %get-tuple-element.8), channel_id=1, source_target_pairs={{0,64},{16,80},{32,96},{48,112},{64,128},{80,144},{96,160},{112,17... | collective-permute-start | bytes 1474568 | tf_op jit(solution)/shard_map/ppermute | solution.py:18
  51.6 11.8 %collective-permute-start.9 = (bf16[4,2,15,16,128]{4,3,2,1,0:T(8,128)(2,1)}, bf16[4,2,15,16,128]{4,3,2,1,0:T(8,128)(2,1)S(1)}, u32[]{:S(2)}, u32[]{:S(2)}) collective-permute-start(bf16[4,2,15,16,128]{4,3,2,1,0:T(8,128)(2,1)} %get-tuple-element.8), channel_id=1, source_target_pairs={{0,192},{16,208},{32,224},{48,240},{64,0},{80,16},{96,32},{112,48}... | collective-permute-start | bytes 1474568 | tf_op jit(solution)/shard_map/ppermute | solution.py:19
  55.2 52.8 %collective-permute-start.18 = (bf16[8,2,15,32,128]{4,3,2,1,0:T(8,128)(2,1)S(1)}, bf16[8,2,15,32,128]{4,3,2,1,0:T(8,128)(2,1)}, u32[]{:S(2)}, u32[]{:S(2)}) collective-permute-start(bf16[8,2,15,32,128]{4,3,2,1,0:T(8,128)(2,1)S(1)} %broadcast_select_fusion), channel_id=1, source_target_pairs={{0,4},{4,8},{8,12},{12,0},{1,5},{5,9},{9,13},{13,1},{2,6},{6,10},{... | collective-permute-start | bytes 5898248 | tf_op jit(solution)/shard_map/ppermute | solution.py:73
  63.4 7.4 %collective-permute-start.10 = (bf16[2,2,15,16,128]{4,3,2,1,0:T(8,128)(2,1)S(1)}, bf16[2,2,15,16,128]{4,3,2,1,0:T(8,128)(2,1)S(1)}, u32[]{:S(2)}, u32[]{:S(2)}) collective-permute-start(bf16[2,2,15,16,128]{4,3,2,1,0:T(8,128)(2,1)S(1)} %slice.115), channel_id=1, source_target_pairs={{0,192},{16,208},{32,224},{48,240},{64,0},{80,16},{96,32},{112,48}... | collective-permute-start | bytes 737288 | tf_op jit(solution)/shard_map/ppermute | solution.py:22
  67.1 7.7 %collective-permute-start.8 = (bf16[2,2,15,16,128]{4,3,2,1,0:T(8,128)(2,1)S(1)}, bf16[2,2,15,16,128]{4,3,2,1,0:T(8,128)(2,1)S(1)}, u32[]{:S(2)}, u32[]{:S(2)}) collective-permute-start(bf16[2,2,15,16,128]{4,3,2,1,0:T(8,128)(2,1)S(1)} %slice.114), channel_id=1, source_target_pairs={{0,64},{16,80},{32,96},{48,112},{64,128},{80,144},{96,160},{112,17... | collective-permute-start | bytes 737288 | tf_op jit(solution)/shard_map/ppermute | solution.py:21
  67.4 13.7 %collective-permute-start.12 = (bf16[4,2,15,8,128]{4,3,2,1,0:T(8,128)(2,1)S(1)}, bf16[4,2,15,8,128]{4,3,2,1,0:T(8,128)(2,1)S(1)}, u32[]{:S(2)}, u32[]{:S(2)}) collective-permute-start(bf16[4,2,15,8,128]{4,3,2,1,0:T(8,128)(2,1)S(1)} %get-tuple-element.13), channel_id=1, source_target_pairs={{0,16},{16,0},{32,48},{48,32},{64,80},{80,64},{96,112},{112,96},{1... | collective-permute-start | bytes 737288 | tf_op jit(solution)/shard_map/ppermute | solution.py:30
  82.2 11.3 %collective-permute-start.13 = (bf16[4,2,15,16,128]{4,3,2,1,0:T(8,128)(2,1)S(1)}, bf16[4,2,15,16,128]{4,3,2,1,0:T(8,128)(2,1)S(1)}, u32[]{:S(2)}, u32[]{:S(2)}) collective-permute-start(bf16[4,2,15,16,128]{4,3,2,1,0:T(8,128)(2,1)S(1)} %get-tuple-element.6), channel_id=1, source_target_pairs={{0,64},{16,80},{32,96},{48,112},{64,128},{80,144},{96,160},{112,17... | collective-permute-start | bytes 1474568 | tf_op jit(solution)/shard_map/ppermute | solution.py:18
  82.2 41.8 %collective-permute-start.17 = (bf16[8,2,15,32,128]{4,3,2,1,0:T(8,128)(2,1)S(1)}, bf16[8,2,15,32,128]{4,3,2,1,0:T(8,128)(2,1)S(1)}, u32[]{:S(2)}, u32[]{:S(2)}) collective-permute-start(bf16[8,2,15,32,128]{4,3,2,1,0:T(8,128)(2,1)S(1)} %broadcast_select_fusion), channel_id=1, source_target_pairs={{0,12},{4,0},{8,4},{12,8},{1,13},{5,1},{9,5},{13,9},{2,14},{6,2},{... | collective-permute-start | bytes 5898248 | tf_op jit(solution)/shard_map/ppermute | solution.py:74
  82.9 11.2 %collective-permute-start.15 = (bf16[4,2,15,16,128]{4,3,2,1,0:T(8,128)(2,1)S(1)}, bf16[4,2,15,16,128]{4,3,2,1,0:T(8,128)(2,1)S(1)}, u32[]{:S(2)}, u32[]{:S(2)}) collective-permute-start(bf16[4,2,15,16,128]{4,3,2,1,0:T(8,128)(2,1)S(1)} %get-tuple-element.6), channel_id=1, source_target_pairs={{0,192},{16,208},{32,224},{48,240},{64,0},{80,16},{96,32},{112,48}... | collective-permute-start | bytes 1474568 | tf_op jit(solution)/shard_map/ppermute | solution.py:19
  93.5 7.5 %collective-permute-start.14 = (bf16[2,2,15,16,128]{4,3,2,1,0:T(8,128)(2,1)S(1)}, bf16[2,2,15,16,128]{4,3,2,1,0:T(8,128)(2,1)S(1)}, u32[]{:S(2)}, u32[]{:S(2)}) collective-permute-start(bf16[2,2,15,16,128]{4,3,2,1,0:T(8,128)(2,1)S(1)} %slice.118), channel_id=1, source_target_pairs={{0,64},{16,80},{32,96},{48,112},{64,128},{80,144},{96,160},{112,17... | collective-permute-start | bytes 737288 | tf_op jit(solution)/shard_map/ppermute | solution.py:21
  94.2 7.5 %collective-permute-start.16 = (bf16[2,2,15,16,128]{4,3,2,1,0:T(8,128)(2,1)S(1)}, bf16[2,2,15,16,128]{4,3,2,1,0:T(8,128)(2,1)S(1)}, u32[]{:S(2)}, u32[]{:S(2)}) collective-permute-start(bf16[2,2,15,16,128]{4,3,2,1,0:T(8,128)(2,1)S(1)} %slice.119), channel_id=1, source_target_pairs={{0,192},{16,208},{32,224},{48,240},{64,0},{80,16},{96,32},{112,48}... | collective-permute-start | bytes 737288 | tf_op jit(solution)/shard_map/ppermute | solution.py:22
  97.9 74.6 %collective-permute-start.24 = (bf16[4,2,15,128,128]{4,3,2,1,0:T(8,128)(2,1)}, bf16[4,2,15,128,128]{4,3,2,1,0:T(8,128)(2,1)}, u32[]{:S(2)}, u32[]{:S(2)}) collective-permute-start(bf16[4,2,15,128,128]{4,3,2,1,0:T(8,128)(2,1)} %slice.126), channel_id=1, source_target_pairs={{0,16},{16,0},{32,48},{48,32},{64,80},{80,64},{96,112},{112,96},{1... | collective-permute-start | bytes 11796488 | tf_op jit(solution)/shard_map/ppermute | solution.py:63
  108.0 66.9 %collective-permute-start.25 = (bf16[4,2,15,128,128]{4,3,2,1,0:T(8,128)(2,1)}, bf16[4,2,15,128,128]{4,3,2,1,0:T(8,128)(2,1)}, u32[]{:S(2)}, u32[]{:S(2)}) collective-permute-start(bf16[4,2,15,128,128]{4,3,2,1,0:T(8,128)(2,1)} %slice.127), channel_id=1, source_target_pairs={{0,16},{16,0},{32,48},{48,32},{64,80},{80,64},{96,112},{112,96},{1... | collective-permute-start | bytes 11796488 | tf_op jit(solution)/shard_map/ppermute | solution.py:63
  109.3 24.3 %collective-permute-start.19 = (bf16[4,2,15,32,128]{4,3,2,1,0:T(8,128)(2,1)S(1)}, bf16[4,2,15,32,128]{4,3,2,1,0:T(8,128)(2,1)}, u32[]{:S(2)}, u32[]{:S(2)}) collective-permute-start(bf16[4,2,15,32,128]{4,3,2,1,0:T(8,128)(2,1)S(1)} %slice.122), channel_id=1, source_target_pairs={{0,4},{4,8},{8,12},{12,0},{1,5},{5,9},{9,13},{13,1},{2,6},{6,10},{... | collective-permute-start | bytes 2949128 | tf_op jit(solution)/shard_map/ppermute | solution.py:76
  124.0 1.3 copy-start
  126.3 20.2 %collective-permute-start.20 = (bf16[4,2,15,32,128]{4,3,2,1,0:T(8,128)(2,1)}, bf16[4,2,15,32,128]{4,3,2,1,0:T(8,128)(2,1)}, u32[]{:S(2)}, u32[]{:S(2)}) collective-permute-start(bf16[4,2,15,32,128]{4,3,2,1,0:T(8,128)(2,1)} %slice.123), channel_id=1, source_target_pairs={{0,12},{4,0},{8,4},{12,8},{1,13},{5,1},{9,5},{13,9},{2,14},{6,2},{... | collective-permute-start | bytes 2949128 | tf_op jit(solution)/shard_map/ppermute | solution.py:77
  149.4 2.5 %copy-start.1 = (bf16[8,2,15,32,128]{4,3,2,1,0:T(8,128)(2,1)S(1)}, bf16[8,2,15,32,128]{4,3,2,1,0:T(8,128)(2,1)}, u32[]{:S(2)}) copy-start(bf16[8,2,15,32,128]{4,3,2,1,0:T(8,128)(2,1)} %copy-done) | copy-start | bytes 5898244
  157.6 14.9 %copy-start.2 = (f32[8,2,128,2,128]{4,2,3,1,0:T(8,128)}, f32[8,2,128,2,128]{4,2,3,1,0:T(8,128)S(1)}, u32[]{:S(2)}) copy-start(f32[8,2,128,2,128]{4,2,3,1,0:T(8,128)S(1)} %bitcast_add_fusion.3) | copy-start | bytes 6291460
  158.5 28.3 %collective-permute-start.21 = (f32[2,2,128,2,128]{4,2,3,1,0:T(8,128)}, f32[2,2,128,2,128]{4,2,3,1,0:T(8,128)S(1)}, u32[]{:S(2)}, u32[]{:S(2)}) collective-permute-start(f32[2,2,128,2,128]{4,2,3,1,0:T(8,128)} %constant_dynamic-slice_fusion.1), channel_id=1, source_target_pairs={{0,1},{1,2},{2,3},{3,0},{4,5},{5,6},{6,7},{7,4},{8,9},{9,10},{10,1... | collective-permute-start | bytes 1572872 | tf_op jit(solution)/shard_map/ppermute | solution.py:93
  181.8 5.0 %copy-start.3 = (f32[8,2,128,2,128]{4,2,3,1,0:T(8,128)S(1)}, f32[8,2,128,2,128]{4,2,3,1,0:T(8,128)}, u32[]{:S(2)}) copy-start(f32[8,2,128,2,128]{4,2,3,1,0:T(8,128)} %copy-done.2) | copy-start | bytes 6291460
  184.6 1.3 copy-start.4
  186.8 20.5 %collective-permute-start.26 = (f32[2,2,128,2,128]{4,2,3,1,0:T(8,128)}, f32[2,2,128,2,128]{4,2,3,1,0:T(8,128)S(1)}, u32[]{:S(2)}, u32[]{:S(2)}) collective-permute-start(f32[2,2,128,2,128]{4,2,3,1,0:T(8,128)} %constant_dynamic-slice_fusion), channel_id=1, source_target_pairs={{0,3},{1,0},{2,1},{3,2},{4,7},{5,4},{6,5},{7,6},{8,11},{9,8},{10,9... | collective-permute-start | bytes 1572872 | tf_op jit(solution)/shard_map/ppermute | solution.py:93
  187.6 31.4 %collective-permute-start.22 = (f32[2,2,128,2,128]{4,2,3,1,0:T(8,128)}, f32[2,2,128,2,128]{4,2,3,1,0:T(8,128)S(1)}, u32[]{:S(2)}, u32[]{:S(2)}) collective-permute-start(f32[2,2,128,2,128]{4,2,3,1,0:T(8,128)} %dynamic-slice_add_fusion.5), channel_id=1, source_target_pairs={{0,1},{1,2},{2,3},{3,0},{4,5},{5,6},{6,7},{7,4},{8,9},{9,10},{10,1... | collective-permute-start | bytes 1572872 | tf_op jit(solution)/shard_map/ppermute | solution.py:93
  209.2 20.9 %collective-permute-start.27 = (f32[2,2,128,2,128]{4,2,3,1,0:T(8,128)}, f32[2,2,128,2,128]{4,2,3,1,0:T(8,128)S(1)}, u32[]{:S(2)}, u32[]{:S(2)}) collective-permute-start(f32[2,2,128,2,128]{4,2,3,1,0:T(8,128)} %dynamic-slice_add_fusion.2), channel_id=1, source_target_pairs={{0,3},{1,0},{2,1},{3,2},{4,7},{5,4},{6,5},{7,6},{8,11},{9,8},{10,9... | collective-permute-start | bytes 1572872 | tf_op jit(solution)/shard_map/ppermute | solution.py:93
  219.9 21.7 %collective-permute-start.23 = (f32[2,2,128,2,128]{4,2,3,1,0:T(8,128)}, f32[2,2,128,2,128]{4,2,3,1,0:T(8,128)S(1)}, u32[]{:S(2)}, u32[]{:S(2)}) collective-permute-start(f32[2,2,128,2,128]{4,2,3,1,0:T(8,128)} %dynamic-slice_add_fusion.4), channel_id=1, source_target_pairs={{0,1},{1,2},{2,3},{3,0},{4,5},{5,6},{6,7},{7,4},{8,9},{9,10},{10,1... | collective-permute-start | bytes 1572872 | tf_op jit(solution)/shard_map/ppermute | solution.py:93
  232.0 14.7 %collective-permute-start.28 = (f32[2,2,128,2,128]{4,2,3,1,0:T(8,128)}, f32[2,2,128,2,128]{4,2,3,1,0:T(8,128)S(1)}, u32[]{:S(2)}, u32[]{:S(2)}) collective-permute-start(f32[2,2,128,2,128]{4,2,3,1,0:T(8,128)} %dynamic-slice_add_fusion.1), channel_id=1, source_target_pairs={{0,3},{1,0},{2,1},{3,2},{4,7},{5,4},{6,5},{7,6},{8,11},{9,8},{10,9... | collective-permute-start | bytes 1572872 | tf_op jit(solution)/shard_map/ppermute | solution.py:93

commit v11 on v8

--- a/solution.py
+++ b/solution.py
@@ -81,14 +81,16 @@
     n = lax.axis_size("rep")
     d = lax.axis_index("rep")
     width = part.shape[0] // n
-    fwd = [(i, (i + 1) % n) for i in range(n)]
 
     def chunk(t):
         return lax.dynamic_slice_in_dim(part, (t % n) * width, width, axis=0)
 
-    acc = chunk(d + n - 1)
+    got = []
     for step in range(1, n):
-        acc = lax.ppermute(acc, "rep", fwd) + chunk(d + 2 * n - step - 1)
+        got.append(lax.ppermute(chunk(d + step), "rep", [(i, (i + step) % n) for i in range(n)]))
+    acc = chunk(d)
+    for piece in got:
+        acc = acc + piece
     return acc
 
 
@@ -115,7 +117,7 @@
     w_blocks = gather_integrals(masked)
     t_mine, t_other = gather_amplitudes(amplitudes, col_index)
     sums = []
-    for t_half, name in ((t_mine, "em"), (t_other, "eo")):
+    for t_half in (t_mine, t_other):
         width = c_local
         part = None
         for s, w_blk in enumerate(w_blocks):
@@ -126,10 +128,7 @@
                 preferred_element_type=jnp.float32,
             )
             part = term if part is None else part + term
-        if name == "em":
-            sums.append(ring_reduce_scatter(part))
-        else:
-            sums.append(lax.psum_scatter(part, "rep", scatter_dimension=0, tiled=True))
+        sums.append(ring_reduce_scatter(part))
     summed = jnp.where(
         core == 0, jnp.concatenate(sums, axis=3), jnp.concatenate(sums[::-1], axis=3)
     )

time: 287 us -> 292 us (1.017)
  the two profiles are of different devices: /device:TPU:1 before, /device:TPU:167 now
where the time goes in v11:
time: 292 us; the launch traced here: 291 us
  waiting for transfers between devices  206 us (71%)
  starting transfers between devices  29.7 us (10%)
  matrix products  21.1 us (7%)
  local copies, waits for them, and re-layouts  20.8 us (7%)
  other arithmetic  13.9 us (5%)
    ppermute x6, waiting for transfers between devices, ring_reduce_scatter(): lax.ppermute(chunk(d + step), 'rep', [(i, (i + step) % n) for i in range(...  74.3 us
    ppermute x1, waiting for transfers between devices, gather_integrals(): from_left = lax.ppermute(w, 'col', fwd)  42.9 us
    ppermute x3, waiting for transfers between devices, ring4_pieces(): from_left = lax.ppermute(block, axis, fwd)  31.7 us
    dot_general x8, matrix products, body(): jnp.einsum('gikca,gjkcb->giajb', w_blk, t_half[:, :, :, s * width:(s + 1)...  21.1 us
    ppermute x1, waiting for transfers between devices, gather_integrals(): opp_lo = lax.ppermute(from_left[:half], 'col', fwd)  19.5 us
    ppermute x1, waiting for transfers between devices, gather_amplitudes(): zh_hi = lax.ppermute(t_part[hg:], 'row', swap)  13.9 us
    ppermute x3, waiting for transfers between devices, ring4_pieces(): from_right = lax.ppermute(block, axis, bwd)  8.95 us
    ppermute x6, starting transfers between devices, ring_reduce_scatter(): lax.ppermute(chunk(d + step), 'rep', [(i, (i + step) % n) for i in range(...  6.27 us
  transfers between devices with their start and end apart: 28, of which 17 were waited for; matrix products, arithmetic and copies ran while one was open for 16% of the time, Pallas kernels for 0%

profile of v11, /device:TPU:167, one launch (start us, length us, event | category | flops | bytes accessed | tf_op | source)
XLA Modules:
  0.0 291.2 jit_solution(292527161100398832)
XLA Ops:
  0.0 1.3 broadcast_select_fusion.2
  2.1 1.5 collective-permute-done
  4.3 1.3 collective-permute-start.3
  5.5 1.0 fusion.22
  6.6 20.4 %collective-permute-done.1 = bf16[8,2,15,16,128]{4,3,2,1,0:T(8,128)(2,1)S(1)} collective-permute-done((bf16[8,2,15,16,128]{4,3,2,1,0:T(8,128)(2,1)S(1)}, bf16[8,2,15,16,128]{4,3,2,1,0:T(8,128)(2,1)S(1)}, u32[]{:S(2)}, u32[]{:S(2)}) %collective-permute-start.1) | collective-permute-done | bytes 983072 | tf_op jit(solution)/shard_map/ppermute | solution.py:18
  27.0 1.5 collective-permute-start.2
  28.5 0.8 slice.103
  29.4 3.7 %collective-permute-done.5 = bf16[4,4,15,8,128]{4,3,2,1,0:T(8,128)(2,1)S(1)} collective-permute-done((bf16[4,4,15,8,128]{4,3,2,1,0:T(8,128)(2,1)}, bf16[4,4,15,8,128]{4,3,2,1,0:T(8,128)(2,1)S(1)}, u32[]{:S(2)}, u32[]{:S(2)}) %collective-permute-start.5) | collective-permute-done | bytes 491552 | tf_op jit(solution)/shard_map/ppermute | solution.py:46
  33.2 1.8 collective-permute-start.6
  35.0 5.1 %broadcast_in_dim.56 = bf16[8,2,15,128,128]{4,3,2,1,0:T(8,128)(2,1)} broadcast(bf16[]{:T(256)} %constant.133.clone.1), dimensions={} | broadcast | bytes 7864322 | tf_op jit(solution)/shard_map/broadcast_in_dim | solution.py:50
  40.1 1.2 constant_dynamic-update-slice_fusion.8
  41.2 0.9 collective-permute-done.4
  42.1 2.2 maximum_dynamic-update-slice_fusion
  44.4 1.2 constant_dynamic-update-slice_fusion.7
  45.6 1.2 constant_dynamic-update-slice_fusion.6
  46.8 1.1 constant_dynamic-update-slice_fusion.5
  47.8 2.7 collective-permute-start.7
  50.5 8.9 %collective-permute-done.9 = bf16[4,2,15,16,128]{4,3,2,1,0:T(8,128)(2,1)S(1)} collective-permute-done((bf16[4,2,15,16,128]{4,3,2,1,0:T(8,128)(2,1)S(1)}, bf16[4,2,15,16,128]{4,3,2,1,0:T(8,128)(2,1)S(1)}, u32[]{:S(2)}, u32[]{:S(2)}) %collective-permute-start.9) | collective-permute-done | bytes 491552 | tf_op jit(solution)/shard_map/ppermute | solution.py:19
  59.6 2.7 collective-permute-start.8
  62.3 13.9 %collective-permute-done.11 = bf16[4,4,15,8,128]{4,3,2,1,0:T(8,128)(2,1)S(1)} collective-permute-done((bf16[4,4,15,8,128]{4,3,2,1,0:T(8,128)(2,1)S(1)}, bf16[4,4,15,8,128]{4,3,2,1,0:T(8,128)(2,1)S(1)}, u32[]{:S(2)}, u32[]{:S(2)}) %collective-permute-start.11) | collective-permute-done | bytes 491552 | tf_op jit(solution)/shard_map/ppermute | solution.py:47
  76.2 2.7 collective-permute-start.12
  78.9 0.9 constant_dynamic-update-slice_fusion.4
  79.8 0.9 maximum_dynamic-update-slice_fusion.1
  80.7 0.9 constant_dynamic-update-slice_fusion.3
  81.6 1.1 constant_dynamic-update-slice_fusion.2
  82.7 1.4 collective-permute-start.15
  84.2 11.3 %collective-permute-done.13 = bf16[4,2,15,16,128]{4,3,2,1,0:T(8,128)(2,1)S(1)} collective-permute-done((bf16[4,2,15,16,128]{4,3,2,1,0:T(8,128)(2,1)S(1)}, bf16[4,2,15,16,128]{4,3,2,1,0:T(8,128)(2,1)S(1)}, u32[]{:S(2)}, u32[]{:S(2)}) %collective-permute-start.13) | collective-permute-done | bytes 491552 | tf_op jit(solution)/shard_map/ppermute | solution.py:18
  95.5 1.3 collective-permute-start.14
  97.1 0.9 constant_dynamic-update-slice_fusion.1
  98.0 4.1 %collective-permute-done.14 = bf16[2,2,15,16,128]{4,3,2,1,0:T(8,128)(2,1)S(1)} collective-permute-done((bf16[2,2,15,16,128]{4,3,2,1,0:T(8,128)(2,1)S(1)}, bf16[2,2,15,16,128]{4,3,2,1,0:T(8,128)(2,1)S(1)}, u32[]{:S(2)}, u32[]{:S(2)}) %collective-permute-start.14) | collective-permute-done | bytes 245792 | tf_op jit(solution)/shard_map/ppermute | solution.py:21
  102.2 2.3 collective-permute-done.16
  104.5 0.9 maximum_dynamic-update-slice_fusion.2
  105.4 1.0 constant_dynamic-update-slice_fusion
  106.3 2.0 collective-permute-start.24
  109.5 1.7 broadcast_select_fusion
  111.2 1.3 collective-permute-start.18
  112.6 1.5 collective-permute-start.17
  114.1 42.9 %collective-permute-done.18 = bf16[8,2,15,32,128]{4,3,2,1,0:T(8,128)(2,1)S(1)} collective-permute-done((bf16[8,2,15,32,128]{4,3,2,1,0:T(8,128)(2,1)S(1)}, bf16[8,2,15,32,128]{4,3,2,1,0:T(8,128)(2,1)S(1)}, u32[]{:S(2)}, u32[]{:S(2)}) %collective-permute-start.18) | collective-permute-done | bytes 1966112 | tf_op jit(solution)/shard_map/ppermute | solution.py:71
  157.1 1.1 copy-done
  158.3 1.1 slice.115
  159.9 1.5 collective-permute-start.20
  161.4 19.5 %collective-permute-done.19 = bf16[4,2,15,32,128]{4,3,2,1,0:T(8,128)(2,1)} collective-permute-done((bf16[4,2,15,32,128]{4,3,2,1,0:T(8,128)(2,1)S(1)}, bf16[4,2,15,32,128]{4,3,2,1,0:T(8,128)(2,1)}, u32[]{:S(2)}, u32[]{:S(2)}) %collective-permute-start.19) | collective-permute-done | bytes 983072 | tf_op jit(solution)/shard_map/ppermute | solution.py:74
  180.9 1.8 collective-permute-done.20
  182.7 3.0 %fusion.5 = f32[8,2,128,2,128,1]{4,2,5,3,1,0:T(8,128)S(1)} fusion(bf16[8,2,15,128,128]{4,3,2,1,0:T(8,128)(2,1)} %constant_dynamic-update-slice_fusion, bf16[4,2,15,32,128]{4,3,2,1,0:T(8,128)(2,1)} %collective-permute-done.20, bf16[4,2,15,32,128]{4,3,2,1,0:T(8,128)(2,1)} %collective-permute-done.19), kind=kOutput, calls=%fused_computation.17 | convolution fusion | flops 507248640 | bytes 6029312 | tf_op jit(solution)/shard_map/gikca,gjkcb->giajb/dot_general | solution.py:124
  185.7 2.5 fusion.7
  188.2 2.6 fusion.6
  190.8 2.6 bitcast_add_fusion.3
  193.4 1.1 constant_dynamic-slice_fusion.4
  195.2 2.0 collective-permute-start.22
  197.2 3.0 %fusion.1 = f32[8,2,128,2,128,1]{4,2,5,3,1,0:T(8,128)S(1)} fusion(bf16[8,2,15,128,128]{4,3,2,1,0:T(8,128)(2,1)} %collective-permute-done.24, bf16[4,2,15,32,128]{4,3,2,1,0:T(8,128)(2,1)} %collective-permute-done.20, bf16[4,2,15,32,128]{4,3,2,1,0:T(8,128)(2,1)} %collective-permute-done.19), kind=kOutput, calls=%fused_computation.9 | convolution fusion | flops 507248640 | bytes 6029312 | tf_op jit(solution)/shard_map/gikca,gjkcb->giajb/dot_general | solution.py:124
  200.2 2.4 fusion.2
  202.6 2.4 fusion.3
  205.0 2.6 bitcast_add_fusion
  207.6 1.2 constant_dynamic-slice_fusion.1
  208.8 1.5 collective-permute-start.25
  210.3 2.1 collective-permute-start.26
  212.6 26.0 %collective-permute-done.22 = f32[2,2,128,2,128]{4,2,3,1,0:T(8,128)} collective-permute-done((f32[2,2,128,2,128]{4,2,3,1,0:T(8,128)}, f32[2,2,128,2,128]{4,2,3,1,0:T(8,128)}, u32[]{:S(2)}, u32[]{:S(2)}) %collective-permute-start.22) | collective-permute-done | bytes 524320 | tf_op jit(solution)/shard_map/ppermute | solution.py:90
  238.6 27.3 %collective-permute-done.23 = f32[2,2,128,2,128]{4,2,3,1,0:T(8,128)} collective-permute-done((f32[2,2,128,2,128]{4,2,3,1,0:T(8,128)S(1)}, f32[2,2,128,2,128]{4,2,3,1,0:T(8,128)}, u32[]{:S(2)}, u32[]{:S(2)}) %collective-permute-start.23) | collective-permute-done | bytes 524320 | tf_op jit(solution)/shard_map/ppermute | solution.py:90
  265.9 1.5 add_add_fusion.1
  267.4 4.9 %collective-permute-done.25 = f32[2,2,128,2,128]{4,2,3,1,0:T(8,128)} collective-permute-done((f32[2,2,128,2,128]{4,2,3,1,0:T(8,128)}, f32[2,2,128,2,128]{4,2,3,1,0:T(8,128)}, u32[]{:S(2)}, u32[]{:S(2)}) %collective-permute-start.25) | collective-permute-done | bytes 524320 | tf_op jit(solution)/shard_map/ppermute | solution.py:90
  272.3 11.2 %collective-permute-done.26 = f32[2,2,128,2,128]{4,2,3,1,0:T(8,128)} collective-permute-done((f32[2,2,128,2,128]{4,2,3,1,0:T(8,128)}, f32[2,2,128,2,128]{4,2,3,1,0:T(8,128)}, u32[]{:S(2)}, u32[]{:S(2)}) %collective-permute-start.26) | collective-permute-done | bytes 524320 | tf_op jit(solution)/shard_map/ppermute | solution.py:90
  283.5 4.9 %collective-permute-done.27 = f32[2,2,128,2,128]{4,2,3,1,0:T(8,128)} collective-permute-done((f32[2,2,128,2,128]{4,2,3,1,0:T(8,128)}, f32[2,2,128,2,128]{4,2,3,1,0:T(8,128)}, u32[]{:S(2)}, u32[]{:S(2)}) %collective-permute-start.27) | collective-permute-done | bytes 524320 | tf_op jit(solution)/shard_map/ppermute | solution.py:90
  288.4 1.5 add_add_fusion
  290.0 1.2 copy.6
  (64 shorter events, 4.8 us)
Async XLA Ops:
  0.0 5.5 %copy-start.5 = (bf16[8,4,15,8,128]{4,3,2,1,0:T(8,128)(2,1)S(1)}, bf16[8,4,15,8,128]{4,3,2,1,0:T(8,128)(2,1)}, u32[]{:S(2)}) copy-start(bf16[8,4,15,8,128]{4,3,2,1,0:T(8,128)(2,1)} %param.5) | copy-start | bytes 2949124
  1.3 2.3 collective-permute-start
  4.0 23.0 %collective-permute-start.1 = (bf16[8,2,15,16,128]{4,3,2,1,0:T(8,128)(2,1)S(1)}, bf16[8,2,15,16,128]{4,3,2,1,0:T(8,128)(2,1)S(1)}, u32[]{:S(2)}, u32[]{:S(2)}) collective-permute-start(bf16[8,2,15,16,128]{4,3,2,1,0:T(8,128)(2,1)S(1)} %maximum_select_fusion.1), channel_id=1, source_target_pairs={{0,64},{16,80},{32,96},{48,112},{64,128},{80,144},{96,160},{112,17... | collective-permute-start | bytes 2949128 | tf_op jit(solution)/shard_map/ppermute | solution.py:18
  4.3 24.3 %collective-permute-start.3 = (bf16[8,2,15,16,128]{4,3,2,1,0:T(8,128)(2,1)S(1)}, bf16[8,2,15,16,128]{4,3,2,1,0:T(8,128)(2,1)S(1)}, u32[]{:S(2)}, u32[]{:S(2)}) collective-permute-start(bf16[8,2,15,16,128]{4,3,2,1,0:T(8,128)(2,1)S(1)} %maximum_select_fusion.1), channel_id=1, source_target_pairs={{0,192},{16,208},{32,224},{48,240},{64,0},{80,16},{96,32},{112,48}... | collective-permute-start | bytes 2949128 | tf_op jit(solution)/shard_map/ppermute | solution.py:19
  6.6 26.5 %collective-permute-start.5 = (bf16[4,4,15,8,128]{4,3,2,1,0:T(8,128)(2,1)}, bf16[4,4,15,8,128]{4,3,2,1,0:T(8,128)(2,1)S(1)}, u32[]{:S(2)}, u32[]{:S(2)}) collective-permute-start(bf16[4,4,15,8,128]{4,3,2,1,0:T(8,128)(2,1)} %get-tuple-element.16), channel_id=1, source_target_pairs={{0,32},{16,48},{32,0},{48,16},{64,96},{80,112},{96,64},{112,80},{1... | collective-permute-start | bytes 1474568 | tf_op jit(solution)/shard_map/ppermute | solution.py:46
  27.0 1.5 copy-start.6
  27.0 14.2 %collective-permute-start.2 = (bf16[4,2,15,16,128]{4,3,2,1,0:T(8,128)(2,1)S(1)}, bf16[4,2,15,16,128]{4,3,2,1,0:T(8,128)(2,1)S(1)}, u32[]{:S(2)}, u32[]{:S(2)}) collective-permute-start(bf16[4,2,15,16,128]{4,3,2,1,0:T(8,128)(2,1)S(1)} %slice.102), channel_id=1, source_target_pairs={{0,64},{16,80},{32,96},{48,112},{64,128},{80,144},{96,160},{112,17... | collective-permute-start | bytes 1474568 | tf_op jit(solution)/shard_map/ppermute | solution.py:21
  29.3 12.8 %collective-permute-start.4 = (bf16[4,2,15,16,128]{4,3,2,1,0:T(8,128)(2,1)}, bf16[4,2,15,16,128]{4,3,2,1,0:T(8,128)(2,1)}, u32[]{:S(2)}, u32[]{:S(2)}) collective-permute-start(bf16[4,2,15,16,128]{4,3,2,1,0:T(8,128)(2,1)} %slice.103), channel_id=1, source_target_pairs={{0,192},{16,208},{32,224},{48,240},{64,0},{80,16},{96,32},{112,48}... | collective-permute-start | bytes 1474568 | tf_op jit(solution)/shard_map/ppermute | solution.py:22
  33.1 6.9 %copy-start.7 = (bf16[8,2,15,16,128]{4,3,2,1,0:T(8,128)(2,1)S(1)}, bf16[8,2,15,16,128]{4,3,2,1,0:T(8,128)(2,1)}, u32[]{:S(2)}) copy-start(bf16[8,2,15,16,128]{4,3,2,1,0:T(8,128)(2,1)} %copy-done.6) | copy-start | bytes 2949124
  33.2 13.6 %collective-permute-start.6 = (bf16[4,2,15,8,128]{4,3,2,1,0:T(8,128)(2,1)S(1)}, bf16[4,2,15,8,128]{4,3,2,1,0:T(8,128)(2,1)S(1)}, u32[]{:S(2)}, u32[]{:S(2)}) collective-permute-start(bf16[4,2,15,8,128]{4,3,2,1,0:T(8,128)(2,1)S(1)} %get-tuple-element.21), channel_id=1, source_target_pairs={{0,16},{16,0},{32,48},{48,32},{64,80},{80,64},{96,112},{112,96},{1... | collective-permute-start | bytes 737288 | tf_op jit(solution)/shard_map/ppermute | solution.py:30
  45.6 4.9 %copy-start.8 = (bf16[4,4,15,8,128]{4,3,2,1,0:T(8,128)(2,1)S(1)}, bf16[4,4,15,8,128]{4,3,2,1,0:T(8,128)(2,1)}, u32[]{:S(2)}) copy-start(bf16[4,4,15,8,128]{4,3,2,1,0:T(8,128)(2,1)} %get-tuple-element.15) | copy-start | bytes 1474564
  47.8 11.6 %collective-permute-start.9 = (bf16[4,2,15,16,128]{4,3,2,1,0:T(8,128)(2,1)S(1)}, bf16[4,2,15,16,128]{4,3,2,1,0:T(8,128)(2,1)S(1)}, u32[]{:S(2)}, u32[]{:S(2)}) collective-permute-start(bf16[4,2,15,16,128]{4,3,2,1,0:T(8,128)(2,1)S(1)} %get-tuple-element.8), channel_id=1, source_target_pairs={{0,192},{16,208},{32,224},{48,240},{64,0},{80,16},{96,32},{112,48}... | collective-permute-start | bytes 1474568 | tf_op jit(solution)/shard_map/ppermute | solution.py:19
  47.8 11.7 %collective-permute-start.7 = (bf16[4,2,15,16,128]{4,3,2,1,0:T(8,128)(2,1)S(1)}, bf16[4,2,15,16,128]{4,3,2,1,0:T(8,128)(2,1)S(1)}, u32[]{:S(2)}, u32[]{:S(2)}) collective-permute-start(bf16[4,2,15,16,128]{4,3,2,1,0:T(8,128)(2,1)S(1)} %get-tuple-element.8), channel_id=1, source_target_pairs={{0,64},{16,80},{32,96},{48,112},{64,128},{80,144},{96,160},{112,17... | collective-permute-start | bytes 1474568 | tf_op jit(solution)/shard_map/ppermute | solution.py:18
  50.5 25.7 %collective-permute-start.11 = (bf16[4,4,15,8,128]{4,3,2,1,0:T(8,128)(2,1)S(1)}, bf16[4,4,15,8,128]{4,3,2,1,0:T(8,128)(2,1)S(1)}, u32[]{:S(2)}, u32[]{:S(2)}) collective-permute-start(bf16[4,4,15,8,128]{4,3,2,1,0:T(8,128)(2,1)S(1)} %copy-done.8), channel_id=1, source_target_pairs={{0,32},{16,48},{32,0},{48,16},{64,96},{80,112},{96,64},{112,80},{1... | collective-permute-start | bytes 1474568 | tf_op jit(solution)/shard_map/ppermute | solution.py:47
  59.5 20.3 %collective-permute-start.10 = (bf16[2,2,15,16,128]{4,3,2,1,0:T(8,128)(2,1)S(1)}, bf16[2,2,15,16,128]{4,3,2,1,0:T(8,128)(2,1)S(1)}, u32[]{:S(2)}, u32[]{:S(2)}) collective-permute-start(bf16[2,2,15,16,128]{4,3,2,1,0:T(8,128)(2,1)S(1)} %slice.107), channel_id=1, source_target_pairs={{0,192},{16,208},{32,224},{48,240},{64,0},{80,16},{96,32},{112,48}... | collective-permute-start | bytes 737288 | tf_op jit(solution)/shard_map/ppermute | solution.py:22
  59.6 20.2 %collective-permute-start.8 = (bf16[2,2,15,16,128]{4,3,2,1,0:T(8,128)(2,1)S(1)}, bf16[2,2,15,16,128]{4,3,2,1,0:T(8,128)(2,1)S(1)}, u32[]{:S(2)}, u32[]{:S(2)}) collective-permute-start(bf16[2,2,15,16,128]{4,3,2,1,0:T(8,128)(2,1)S(1)} %slice.106), channel_id=1, source_target_pairs={{0,64},{16,80},{32,96},{48,112},{64,128},{80,144},{96,160},{112,17... | collective-permute-start | bytes 737288 | tf_op jit(solution)/shard_map/ppermute | solution.py:21
  76.2 5.4 %collective-permute-start.12 = (bf16[4,2,15,8,128]{4,3,2,1,0:T(8,128)(2,1)S(1)}, bf16[4,2,15,8,128]{4,3,2,1,0:T(8,128)(2,1)S(1)}, u32[]{:S(2)}, u32[]{:S(2)}) collective-permute-start(bf16[4,2,15,8,128]{4,3,2,1,0:T(8,128)(2,1)S(1)} %get-tuple-element.19), channel_id=1, source_target_pairs={{0,16},{16,0},{32,48},{48,32},{64,80},{80,64},{96,112},{112,96},{1... | collective-permute-start | bytes 737288 | tf_op jit(solution)/shard_map/ppermute | solution.py:30
  82.7 25.7 %copy-start.10 = (s32[60]{0:T(128)S(1)}, s32[60]{0:T(128)}, u32[]{:S(2)}) copy-start(s32[60]{0:T(128)} %param.7) | copy-start | bytes 724
  82.7 25.8 %copy-start.9 = (s32[8]{0:T(128)S(1)}, s32[8]{0:T(128)}, u32[]{:S(2)}) copy-start(s32[8]{0:T(128)} %param.6) | copy-start | bytes 100
  82.7 12.8 %collective-permute-start.13 = (bf16[4,2,15,16,128]{4,3,2,1,0:T(8,128)(2,1)S(1)}, bf16[4,2,15,16,128]{4,3,2,1,0:T(8,128)(2,1)S(1)}, u32[]{:S(2)}, u32[]{:S(2)}) collective-permute-start(bf16[4,2,15,16,128]{4,3,2,1,0:T(8,128)(2,1)S(1)} %get-tuple-element.6), channel_id=1, source_target_pairs={{0,64},{16,80},{32,96},{48,112},{64,128},{80,144},{96,160},{112,17... | collective-permute-start | bytes 1474568 | tf_op jit(solution)/shard_map/ppermute | solution.py:18
  82.7 14.1 %collective-permute-start.15 = (bf16[4,2,15,16,128]{4,3,2,1,0:T(8,128)(2,1)S(1)}, bf16[4,2,15,16,128]{4,3,2,1,0:T(8,128)(2,1)S(1)}, u32[]{:S(2)}, u32[]{:S(2)}) collective-permute-start(bf16[4,2,15,16,128]{4,3,2,1,0:T(8,128)(2,1)S(1)} %get-tuple-element.6), channel_id=1, source_target_pairs={{0,192},{16,208},{32,224},{48,240},{64,0},{80,16},{96,32},{112,48}... | collective-permute-start | bytes 1474568 | tf_op jit(solution)/shard_map/ppermute | solution.py:19
  95.5 6.7 %collective-permute-start.14 = (bf16[2,2,15,16,128]{4,3,2,1,0:T(8,128)(2,1)S(1)}, bf16[2,2,15,16,128]{4,3,2,1,0:T(8,128)(2,1)S(1)}, u32[]{:S(2)}, u32[]{:S(2)}) collective-permute-start(bf16[2,2,15,16,128]{4,3,2,1,0:T(8,128)(2,1)S(1)} %slice.110), channel_id=1, source_target_pairs={{0,64},{16,80},{32,96},{48,112},{64,128},{80,144},{96,160},{112,17... | collective-permute-start | bytes 737288 | tf_op jit(solution)/shard_map/ppermute | solution.py:21
  96.8 7.6 %collective-permute-start.16 = (bf16[2,2,15,16,128]{4,3,2,1,0:T(8,128)(2,1)S(1)}, bf16[2,2,15,16,128]{4,3,2,1,0:T(8,128)(2,1)S(1)}, u32[]{:S(2)}, u32[]{:S(2)}) collective-permute-start(bf16[2,2,15,16,128]{4,3,2,1,0:T(8,128)(2,1)S(1)} %slice.111), channel_id=1, source_target_pairs={{0,192},{16,208},{32,224},{48,240},{64,0},{80,16},{96,32},{112,48}... | collective-permute-start | bytes 737288 | tf_op jit(solution)/shard_map/ppermute | solution.py:22
  106.3 90.9 %collective-permute-start.24 = (bf16[8,2,15,128,128]{4,3,2,1,0:T(8,128)(2,1)}, bf16[8,2,15,128,128]{4,3,2,1,0:T(8,128)(2,1)}, u32[]{:S(2)}, u32[]{:S(2)}) collective-permute-start(bf16[8,2,15,128,128]{4,3,2,1,0:T(8,128)(2,1)} %constant_dynamic-update-slice_fusion), channel_id=1, source_target_pairs={{0,16},{16,0},{32,48},{48,32},{64,80},{80,64},{96,112},{112,96},{1... | collective-permute-start | bytes 23592968 | tf_op jit(solution)/shard_map/ppermute | solution.py:62
  111.2 45.7 %collective-permute-start.18 = (bf16[8,2,15,32,128]{4,3,2,1,0:T(8,128)(2,1)S(1)}, bf16[8,2,15,32,128]{4,3,2,1,0:T(8,128)(2,1)S(1)}, u32[]{:S(2)}, u32[]{:S(2)}) collective-permute-start(bf16[8,2,15,32,128]{4,3,2,1,0:T(8,128)(2,1)S(1)} %broadcast_select_fusion), channel_id=1, source_target_pairs={{0,4},{4,8},{8,12},{12,0},{1,5},{5,9},{9,13},{13,1},{2,6},{6,10},{... | collective-permute-start | bytes 5898248 | tf_op jit(solution)/shard_map/ppermute | solution.py:71
  112.6 44.6 %collective-permute-start.17 = (bf16[8,2,15,32,128]{4,3,2,1,0:T(8,128)(2,1)S(1)}, bf16[8,2,15,32,128]{4,3,2,1,0:T(8,128)(2,1)S(1)}, u32[]{:S(2)}, u32[]{:S(2)}) collective-permute-start(bf16[8,2,15,32,128]{4,3,2,1,0:T(8,128)(2,1)S(1)} %broadcast_select_fusion), channel_id=1, source_target_pairs={{0,12},{4,0},{8,4},{12,8},{1,13},{5,1},{9,5},{13,9},{2,14},{6,2},{... | collective-permute-start | bytes 5898248 | tf_op jit(solution)/shard_map/ppermute | solution.py:72
  157.0 1.3 copy-start
  157.0 23.9 %collective-permute-start.19 = (bf16[4,2,15,32,128]{4,3,2,1,0:T(8,128)(2,1)S(1)}, bf16[4,2,15,32,128]{4,3,2,1,0:T(8,128)(2,1)}, u32[]{:S(2)}, u32[]{:S(2)}) collective-permute-start(bf16[4,2,15,32,128]{4,3,2,1,0:T(8,128)(2,1)S(1)} %slice.114), channel_id=1, source_target_pairs={{0,4},{4,8},{8,12},{12,0},{1,5},{5,9},{9,13},{13,1},{2,6},{6,10},{... | collective-permute-start | bytes 2949128 | tf_op jit(solution)/shard_map/ppermute | solution.py:74
  158.3 1.6 copy-start.2
  159.9 22.8 %collective-permute-start.20 = (bf16[4,2,15,32,128]{4,3,2,1,0:T(8,128)(2,1)}, bf16[4,2,15,32,128]{4,3,2,1,0:T(8,128)(2,1)}, u32[]{:S(2)}, u32[]{:S(2)}) collective-permute-start(bf16[4,2,15,32,128]{4,3,2,1,0:T(8,128)(2,1)} %slice.115), channel_id=1, source_target_pairs={{0,12},{4,0},{8,4},{12,8},{1,13},{5,1},{9,5},{13,9},{2,14},{6,2},{... | collective-permute-start | bytes 2949128 | tf_op jit(solution)/shard_map/ppermute | solution.py:75
  185.7 2.5 copy-start.3
  188.2 2.6 copy-start.1
  193.4 6.8 %copy-start.4 = (f32[8,2,128,2,128]{4,2,3,1,0:T(8,128)}, f32[8,2,128,2,128]{4,2,3,1,0:T(8,128)S(1)}, u32[]{:S(2)}) copy-start(f32[8,2,128,2,128]{4,2,3,1,0:T(8,128)S(1)} %bitcast_add_fusion.3) | copy-start | bytes 6291460
  194.5 17.9 %collective-permute-start.21 = (f32[2,2,128,2,128]{4,2,3,1,0:T(8,128)S(1)}, f32[2,2,128,2,128]{4,2,3,1,0:T(8,128)S(1)}, u32[]{:S(2)}, u32[]{:S(2)}) collective-permute-start(f32[2,2,128,2,128]{4,2,3,1,0:T(8,128)S(1)} %get-tuple-element.9), channel_id=1, source_target_pairs={{0,1},{1,2},{2,3},{3,0},{4,5},{5,6},{6,7},{7,4},{8,9},{9,10},{10,1... | collective-permute-start | bytes 1572872 | tf_op jit(solution)/shard_map/ppermute | solution.py:90
  195.2 43.4 %collective-permute-start.22 = (f32[2,2,128,2,128]{4,2,3,1,0:T(8,128)}, f32[2,2,128,2,128]{4,2,3,1,0:T(8,128)}, u32[]{:S(2)}, u32[]{:S(2)}) collective-permute-start(f32[2,2,128,2,128]{4,2,3,1,0:T(8,128)} %get-tuple-element.11), channel_id=1, source_target_pairs={{0,2},{1,3},{2,0},{3,1},{4,6},{5,7},{6,4},{7,5},{8,10},{9,11},{10,... | collective-permute-start | bytes 1572872 | tf_op jit(solution)/shard_map/ppermute | solution.py:90
  197.2 68.7 %collective-permute-start.23 = (f32[2,2,128,2,128]{4,2,3,1,0:T(8,128)S(1)}, f32[2,2,128,2,128]{4,2,3,1,0:T(8,128)}, u32[]{:S(2)}, u32[]{:S(2)}) collective-permute-start(f32[2,2,128,2,128]{4,2,3,1,0:T(8,128)S(1)} %get-tuple-element.10), channel_id=1, source_target_pairs={{0,3},{1,0},{2,1},{3,2},{4,7},{5,4},{6,5},{7,6},{8,11},{9,8},{10,9... | collective-permute-start | bytes 1572872 | tf_op jit(solution)/shard_map/ppermute | solution.py:90
  208.8 63.5 %collective-permute-start.25 = (f32[2,2,128,2,128]{4,2,3,1,0:T(8,128)}, f32[2,2,128,2,128]{4,2,3,1,0:T(8,128)}, u32[]{:S(2)}, u32[]{:S(2)}) collective-permute-start(f32[2,2,128,2,128]{4,2,3,1,0:T(8,128)} %get-tuple-element.12), channel_id=1, source_target_pairs={{0,1},{1,2},{2,3},{3,0},{4,5},{5,6},{6,7},{7,4},{8,9},{9,10},{10,1... | collective-permute-start | bytes 1572872 | tf_op jit(solution)/shard_map/ppermute | solution.py:90
  210.3 73.2 %collective-permute-start.26 = (f32[2,2,128,2,128]{4,2,3,1,0:T(8,128)}, f32[2,2,128,2,128]{4,2,3,1,0:T(8,128)}, u32[]{:S(2)}, u32[]{:S(2)}) collective-permute-start(f32[2,2,128,2,128]{4,2,3,1,0:T(8,128)} %get-tuple-element.14), channel_id=1, source_target_pairs={{0,2},{1,3},{2,0},{3,1},{4,6},{5,7},{6,4},{7,5},{8,10},{9,11},{10,... | collective-permute-start | bytes 1572872 | tf_op jit(solution)/shard_map/ppermute | solution.py:90
  212.5 76.0 %collective-permute-start.27 = (f32[2,2,128,2,128]{4,2,3,1,0:T(8,128)}, f32[2,2,128,2,128]{4,2,3,1,0:T(8,128)}, u32[]{:S(2)}, u32[]{:S(2)}) collective-permute-start(f32[2,2,128,2,128]{4,2,3,1,0:T(8,128)} %get-tuple-element.13), channel_id=1, source_target_pairs={{0,3},{1,0},{2,1},{3,2},{4,7},{5,4},{6,5},{7,6},{8,11},{9,8},{10,9... | collective-permute-start | bytes 1572872 | tf_op jit(solution)/shard_map/ppermute | solution.py:90
